TPU v7x, 256 devices: a whole 4x4x8 slice. The times are simulated.
256 devices in a mesh: row: 16 (over x, z_lo), col: 16 (over y, z_hi, core).
Axes of the slice: x: 4, y: 4, z: 8 (z_hi: 2, z_lo: 4; z = z_hi * 4 + z_lo), core: 2. Of those that a mesh axis runs over, the one named last changes fastest.
Arguments:
- hidden: bfloat16 [2560, 8192], P('row', 'col'), may hold values from -6 to 6
- w_query: bfloat16 [8192, 8192], P('col', 'row'), may hold values from -0.0625 to 0.0625
- w_keyval: bfloat16 [8192, 2048], P('col', 'row'), may hold values from -0.15625 to 0.15625
- prefix_cache: bfloat16 [2, 16384, 2048], P(None, 'col', 'row'), may hold values from -60 to 60, as said below
- suffix_lengths: int32 [16], replicated, may hold values from 32 to 160, as said below
- group_ids: int32 [16], replicated, may hold values from 0 to 1, as said below
Outputs:
- attended: bfloat16 [2560, 8192], P('col', 'row')
Inputs may be any that keep to these rules, and one draw needn't show every extreme that they name: `suffix_lengths`: every suffix has 32 to 160 live tokens; some request has exactly 160 and some exactly 32. `group_ids`: exactly 8 requests read each prefix. `prefix_cache`: finite values.
All inputs are finite; a program needn't handle non-finite values.
Results may differ from a plain program's by a relative error of at most 0.011.
Values may be sent and summed in bfloat16 or wider, within the bound.
No kernel may reach another device: no remote copies, remote signals or barrier semaphores. Data moves between devices by JAX's collectives and lax.ppermute only.
A program may use at most 128 MiB of HBM per device.

v0:
```python
import jax
import jax.numpy as jnp
from jax import lax
from jax.sharding import PartitionSpec as P

HD = 128
PREFIX = 16384
SUF = 160


def partner(value, axis, stride):
    mask = 2**stride
    pairs = [(source, source ^ mask) for source in range(lax.axis_size(axis))]
    return lax.ppermute(value, axis, pairs)


def rotary_tables(positions):
    freqs = 500000.0 ** (-(jnp.arange(HD // 2, dtype=jnp.float32) * 2.0 / HD))
    angles = positions.astype(jnp.float32)[:, None] * freqs[None, :]
    return (jnp.cos(angles), jnp.sin(angles))


def rotate(values, cosine, sine):
    first = values[..., : HD // 2]
    second = values[..., HD // 2 :]
    cosine = cosine[:, None, :]
    sine = sine[:, None, :]
    return jnp.concatenate(
        [first * cosine - second * sine, second * cosine + first * sine], axis=-1
    )


def block_size(count):
    size = count
    for _ in range(24):
        if size > 2048 and size % 2 == 0:
            size = size // 2
    return size


def block_stats(req_query, keys, values, scale):
    scores = jnp.einsum("thd,kd->htk", req_query, keys, preferred_element_type=jnp.float32) * scale
    top = jnp.max(scores, axis=-1)
    weights = jnp.exp(scores - top[..., None])
    total = jnp.sum(weights, axis=-1)
    accum = jnp.einsum(
        "htk,kd->htd", weights.astype(jnp.bfloat16), values, preferred_element_type=jnp.float32
    )
    return (top, total, accum)


def combine(first, second):
    top = jnp.maximum(first[0], second[0])
    scale_one = jnp.exp(first[0] - top)
    scale_two = jnp.exp(second[0] - top)
    total = first[1] * scale_one + second[1] * scale_two
    accum = first[2] * scale_one[..., None] + second[2] * scale_two[..., None]
    return (top, total, accum)


def empty_state(heads_here):
    return (
        jnp.full((heads_here, SUF), -1e30, jnp.float32),
        jnp.zeros((heads_here, SUF), jnp.float32),
        jnp.zeros((heads_here, SUF, HD), jnp.float32),
    )


def attend_keys(req_query, keys, values, scale):
    count = keys.shape[0]
    size = block_size(count)
    key_blocks = keys.reshape(count // size, size, HD)
    value_blocks = values.reshape(count // size, size, HD)

    def advance(state, pieces):
        return (combine(state, block_stats(req_query, pieces[0], pieces[1], scale)), None)

    state, _ = lax.scan(advance, empty_state(req_query.shape[1]), (key_blocks, value_blocks))
    return state


def per_device(hidden, w_query, w_keyval, prefix_cache, suffix_lengths, group_ids):
    n_col = lax.axis_size("col")
    row_id = lax.axis_index("row")
    col_id = lax.axis_index("col")
    heads_here = w_query.shape[1] // HD
    segments = w_keyval.shape[1] // HD
    scale = 1.0 / HD**0.5
    gathered = lax.all_gather(hidden, "row", axis=0, tiled=True)
    weights_all = jnp.concatenate([w_query, w_keyval], axis=1)
    tok_block = gathered.shape[0] // n_col
    projected = lax.psum_scatter(
        jnp.dot(gathered, weights_all, preferred_element_type=jnp.float32),
        "col",
        scatter_dimension=0,
        tiled=True,
    )
    req_here = tok_block // SUF
    positions = PREFIX + jnp.arange(tok_block, dtype=jnp.int32) % SUF
    cosine, sine = rotary_tables(positions)
    query = projected[:, : heads_here * HD].reshape(tok_block, heads_here, HD)
    query = rotate(query, cosine, sine).astype(jnp.bfloat16)
    keyval = projected[:, heads_here * HD :].reshape(tok_block, segments, HD)
    segment_ids = row_id * segments + jnp.arange(segments, dtype=jnp.int32)
    is_key = segment_ids % 2 == 0
    keyval = jnp.where(is_key[None, :, None], rotate(keyval, cosine, sine), keyval).astype(
        jnp.bfloat16
    )
    cache = prefix_cache.reshape(prefix_cache.shape[0], prefix_cache.shape[1], segments, HD)
    other_keyval, other_cache = partner((keyval, cache), "row", 0)
    is_even = row_id % 2 == 0
    suffix_keys = jnp.where(is_even, keyval[:, 0], other_keyval[:, 0])
    suffix_values = jnp.where(is_even, other_keyval[:, 0], keyval[:, 0])
    cache_keys = jnp.where(is_even, cache[:, :, 0], other_cache[:, :, 0])
    cache_values = jnp.where(is_even, other_cache[:, :, 0], cache[:, :, 0])
    req_query = query.reshape(req_here, SUF, heads_here, HD)
    first_req = col_id * req_here
    lengths_here = lax.dynamic_slice_in_dim(suffix_lengths, first_req, req_here)
    groups_here = lax.dynamic_slice_in_dim(group_ids, first_req, req_here)
    start_state = jax.tree.map(
        lambda leaf: jnp.broadcast_to(leaf, (req_here,) + leaf.shape), empty_state(heads_here)
    )
    piece_keys = lax.all_gather(cache_keys, "col", axis=1, tiled=True)
    piece_values = lax.all_gather(cache_values, "col", axis=1, tiled=True)

    def per_request(inputs_one):
        one_query, group, top, total, accum = inputs_one
        keys = lax.dynamic_index_in_dim(piece_keys, group, 0, keepdims=False)
        values = lax.dynamic_index_in_dim(piece_values, group, 0, keepdims=False)
        return combine((top, total, accum), attend_keys(one_query, keys, values, scale))

    prefix_state = lax.map(
        per_request, (req_query, groups_here, start_state[0], start_state[1], start_state[2])
    )
    own_keys = suffix_keys.reshape(req_here, SUF, HD)
    own_values = suffix_values.reshape(req_here, SUF, HD)

    def finish(inputs_one):
        one_query, keys, values, length, top, total, accum = inputs_one
        places = jnp.arange(SUF, dtype=jnp.int32)
        mask = (places[None, :] <= places[:, None]) & (places[None, :] < length)
        scores = (
            jnp.einsum("thd,kd->htk", one_query, keys, preferred_element_type=jnp.float32) * scale
        )
        scores = jnp.where(mask[None], scores, -1e30)
        own_top = jnp.max(scores, axis=-1)
        weights = jnp.exp(scores - own_top[..., None])
        own_total = jnp.sum(weights, axis=-1)
        own_accum = jnp.einsum(
            "htk,kd->htd", weights.astype(jnp.bfloat16), values, preferred_element_type=jnp.float32
        )
        merged = combine((top, total, accum), (own_top, own_total, own_accum))
        result = merged[2] / merged[1][..., None]
        live = (places < length).astype(jnp.float32)
        result = result * live[None, :, None]
        return jnp.transpose(result, (1, 0, 2))

    output = lax.map(
        finish,
        (
            req_query,
            own_keys,
            own_values,
            lengths_here,
            prefix_state[0],
            prefix_state[1],
            prefix_state[2],
        ),
    )
    return output.reshape(tok_block, heads_here * HD).astype(jnp.bfloat16)


def solution(mesh):
    return jax.shard_map(
        per_device,
        mesh=mesh,
        in_specs=(
            P("row", "col"),
            P("col", "row"),
            P("col", "row"),
            P(None, "col", "row"),
            P(),
            P(),
        ),
        out_specs=P("col", "row"),
        check_vma=False,
    )
```

profile of v0, /device:TPU:32, one launch (start us, length us, event | category | flops | bytes accessed | tf_op | source)
XLA Modules:
  0.0 530.4 jit_solution(9526909621574564188)
XLA Ops:
  7.3 91.1 %all-gather.6.cloned.1.call-done = bf16[2560,512]{1,0:T(8,128)(2,1)} async-done(((bf16[160,512]{1,0:T(8,128)(2,1)}), bf16[2560,512]{1,0:T(8,128)(2,1)}) %all-gather.6.cloned.1.call-update) | async-done | bytes 2621456 | tf_op jit(solution)/shard_map/all_gather | solution.py:89
  98.4 6.6 %convolution_bitcast_fusion = f32[2560,640]{0,1:T(8,128)} fusion(bf16[2560,512]{1,0:T(8,128)(2,1)} %all-gather.6.cloned.1.call-done, bf16[512,128]{1,0:T(8,128)(2,1)} %param.10, bf16[512,512]{1,0:T(8,128)(2,1)} %param.9), kind=kOutput, calls=%fused_computation.24 | convolution fusion | flops 1679032320 | bytes 9830400 | tf_op jit(solution)/shard_map/dot_general | solution.py:93
  105.0 8.2 %copy.37 = f32[2560,640]{1,0:T(8,128)} copy(f32[2560,640]{0,1:T(8,128)} %convolution_bitcast_fusion) | data formatting | bytes 13107200
  115.4 8.0 %collective-permute-done = bf16[2,1024,1,128]{3,1,0,2:T(8,128)(2,1)S(1)} collective-permute-done((bf16[2,1024,1,128]{3,1,0,2:T(8,128)(2,1)S(1)}, bf16[2,1024,1,128]{3,1,0,2:T(8,128)(2,1)S(1)}, u32[]{:S(2)}, u32[]{:S(2)}) %collective-permute-start) | collective-permute-done | bytes 524320 | tf_op jit(solution)/shard_map/ppermute | solution.py:14
  130.1 103.3 %reduce-scatter.4.cloned.1.call-done = f32[160,640]{1,0:T(8,128)} async-done(((f32[2560,640]{1,0:T(8,128)}), f32[160,640]{1,0:T(8,128)}) %reduce-scatter.4.cloned.1.call-update) | async-done | bytes 409616
  234.8 2.5 collective-permute-start.1
  239.9 101.6 %all-gather.4.cloned.1.call-done = bf16[2,16384,128]{2,1,0:T(8,128)(2,1)} async-done(((bf16[2,1024,128]{2,1,0:T(8,128)(2,1)}), bf16[2,16384,128]{2,1,0:T(8,128)(2,1)}) %all-gather.4.cloned.1.call-update) | async-done | bytes 8388624 | tf_op jit(solution)/shard_map/all_gather | solution.py:123
  341.6 3.7 constant_dynamic-slice_fusion.1
  345.2 101.8 %all-gather.8.cloned.1.call-done = bf16[2,16384,128]{2,1,0:T(8,128)(2,1)} async-done(((bf16[2,1024,128]{2,1,0:T(8,128)(2,1)}), bf16[2,16384,128]{2,1,0:T(8,128)(2,1)}) %all-gather.8.cloned.1.call-update) | async-done | bytes 8388624 | tf_op jit(solution)/shard_map/all_gather | solution.py:124
  447.1 3.7 constant_dynamic-slice_fusion
  450.8 71.8 %while.20 = (s32[]{:T(128)}, f32[4,160]{1,0:T(4,128)S(1)}, f32[4,160]{1,0:T(4,128)S(1)}, f32[4,160,128]{2,1,0:T(8,128)S(1)}, bf16[8,2048,128]{2,1,0:T(8,128)(2,1...) while((s32[]{:T(128)}, f32[4,160]{1,0:T(4,128)S(1)}, ...), condition=%wide.region_4.5_spmd.clone, body=%wide.region_1.4_spmd.clone.sunk | while | flops 681905920 | bytes 38604932 | solution.py:78
  452.8 2.3 copy-done
  456.1 3.6 fusion.75
  461.7 2.3 copy-done
  465.0 3.6 fusion.75
  470.7 2.3 copy-done
  474.0 3.6 fusion.75
  479.7 2.3 copy-done
  483.0 3.6 fusion.75
  488.6 2.3 copy-done
  492.0 3.6 fusion.75
  500.9 3.6 fusion.75
  509.9 3.6 fusion.75
  518.9 3.6 fusion.75
  (79 shorter events, 43.8 us)
Async XLA Ops:
  6.5 91.9 %all-gather.6.cloned.1.call-start = ((), (), s32[]{:S(2)}) async-start(), calls=%async_computation.2 | async-start | bytes 2785280 | tf_op jit(solution)/shard_map/all_gather | solution.py:89
  7.3 226.2 %reduce-scatter.4.cloned.1.call-start = ((), (), s32[]{:S(2)}) async-start(), calls=%async_computation.4 | async-start | bytes 6963200
  113.2 1.0 copy-start.1
  113.2 11.9 %copy-start.2 = (s32[16]{0:T(128)S(1)}, s32[16]{0:T(128)}, u32[]{:S(2)}) copy-start(s32[16]{0:T(128)} %param.13) | copy-start | bytes 196
  113.2 14.0 %copy-start.3 = (s32[16]{0:T(128)S(1)}, s32[16]{0:T(128)}, u32[]{:S(2)}) copy-start(s32[16]{0:T(128)} %param.12) | copy-start | bytes 196
  113.2 228.4 %all-gather.4.cloned.1.call-start = ((), (), s32[]{:S(2)}) async-start(), calls=%async_computation.1 | async-start | bytes 8912896 | tf_op jit(solution)/shard_map/all_gather | solution.py:123
  114.2 9.2 %collective-permute-start = (bf16[2,1024,1,128]{3,1,0,2:T(8,128)(2,1)S(1)}, bf16[2,1024,1,128]{3,1,0,2:T(8,128)(2,1)S(1)}, u32[]{:S(2)}, u32[]{:S(2)}) collective-permute-start(bf16[2,1024,1,128]{3,1,0,2:T(8,128)(2,1)S(1)} %bitcast.92), channel_id=1, source_target_pairs={{0,16},{16,0},{32,48},{48,32},{64,80},{80,64},{96,112},{112,96},{1... | collective-permute-start | bytes 1572872 | tf_op jit(solution)/shard_map/ppermute | solution.py:14
  124.5 322.6 %all-gather.8.cloned.1.call-start = ((), (), s32[]{:S(2)}) async-start(), calls=%async_computation.3 | async-start | bytes 8912896 | tf_op jit(solution)/shard_map/all_gather | solution.py:124
  234.8 4.7 collective-permute-start.1
  452.7 2.3 copy-start
  461.7 2.3 copy-start
  470.7 2.3 copy-start
  479.7 2.3 copy-start
  488.6 2.3 copy-start
  497.6 2.3 copy-start
  506.6 2.3 copy-start
  515.6 2.3 copy-start
Sparse Core Ops, SparseCore 0:
  9.1 89.2 all-gather.5
  113.3 120.0 reduce-scatter.3
  236.2 105.3 all-gather.3
  344.2 102.8 all-gather.7
where the time goes:
time: 534 us; the launch traced here: 530 us
  waiting for transfers between devices  408 us (76%)
  matrix products  52.5 us (10%)
  local copies, waits for them, and re-layouts  39.4 us (7%)
  between operations  15.4 us (3%)
  other arithmetic  11.5 us (2%)
    unnamed x5, waiting for transfers between devices  105 us
    all_gather x1, waiting for transfers between devices, per_device(): piece_values = lax.all_gather(cache_values, 'col', axis=1, tiled=True)  102 us
    all_gather x1, waiting for transfers between devices, per_device(): piece_keys = lax.all_gather(cache_keys, 'col', axis=1, tiled=True)  102 us
    all_gather x1, waiting for transfers between devices, per_device(): gathered = lax.all_gather(hidden, 'row', axis=0, tiled=True)  91.1 us
    dot_general x8, matrix products, block_stats(): jnp.einsum('htk,kd->htd', weights.astype(jnp.bfloat16), values, preferred...  29 us
    while x16, local copies, waits for them, and re-layouts  18.4 us
    dot_general x8, matrix products, block_stats(): jnp.einsum('thd,kd->htk', req_query, keys, preferred_element_type=jnp.flo...  15.9 us
  transfers between devices with their start and end apart: 6, of which 6 were waited for; matrix products, arithmetic and copies ran while one was open for 2% of the time, Pallas kernels for 0%

commit v1 on v0

--- a/solution.py
+++ b/solution.py
@@ -79,7 +79,31 @@
     return state
 
 
+def flat_perm(n_row, n_col, target):
+    pairs = []
+    for r in range(n_row):
+        for c in range(n_col):
+            dest = target(r, c)
+            if dest is not None:
+                pairs.append((r * n_col + c, dest[0] * n_col + dest[1]))
+    return pairs
+
+
+def combine_all(states):
+    top = states[0][0]
+    for state in states[1:]:
+        top = jnp.maximum(top, state[0])
+    total = 0.0
+    accum = 0.0
+    for state in states:
+        factor = jnp.exp(state[0] - top)
+        total = total + state[1] * factor
+        accum = accum + state[2] * factor[..., None]
+    return (top, total, accum)
+
+
 def per_device(hidden, w_query, w_keyval, prefix_cache, suffix_lengths, group_ids):
+    n_row = lax.axis_size("row")
     n_col = lax.axis_size("col")
     row_id = lax.axis_index("row")
     col_id = lax.axis_index("col")
@@ -95,7 +119,6 @@
         scatter_dimension=0,
         tiled=True,
     )
-    req_here = tok_block // SUF
     positions = PREFIX + jnp.arange(tok_block, dtype=jnp.int32) % SUF
     cosine, sine = rotary_tables(positions)
     query = projected[:, : heads_here * HD].reshape(tok_block, heads_here, HD)
@@ -106,68 +129,71 @@
     keyval = jnp.where(is_key[None, :, None], rotate(keyval, cosine, sine), keyval).astype(
         jnp.bfloat16
     )
-    cache = prefix_cache.reshape(prefix_cache.shape[0], prefix_cache.shape[1], segments, HD)
-    other_keyval, other_cache = partner((keyval, cache), "row", 0)
-    is_even = row_id % 2 == 0
+    odd = row_id % 2
+    is_even = odd == 0
+    other_keyval, other_cache = partner((keyval, prefix_cache), "row", 0)
     suffix_keys = jnp.where(is_even, keyval[:, 0], other_keyval[:, 0])
     suffix_values = jnp.where(is_even, other_keyval[:, 0], keyval[:, 0])
-    cache_keys = jnp.where(is_even, cache[:, :, 0], other_cache[:, :, 0])
-    cache_values = jnp.where(is_even, other_cache[:, :, 0], cache[:, :, 0])
-    req_query = query.reshape(req_here, SUF, heads_here, HD)
-    first_req = col_id * req_here
-    lengths_here = lax.dynamic_slice_in_dim(suffix_lengths, first_req, req_here)
-    groups_here = lax.dynamic_slice_in_dim(group_ids, first_req, req_here)
-    start_state = jax.tree.map(
-        lambda leaf: jnp.broadcast_to(leaf, (req_here,) + leaf.shape), empty_state(heads_here)
-    )
-    piece_keys = lax.all_gather(cache_keys, "col", axis=1, tiled=True)
-    piece_values = lax.all_gather(cache_values, "col", axis=1, tiled=True)
-
-    def per_request(inputs_one):
-        one_query, group, top, total, accum = inputs_one
-        keys = lax.dynamic_index_in_dim(piece_keys, group, 0, keepdims=False)
-        values = lax.dynamic_index_in_dim(piece_values, group, 0, keepdims=False)
-        return combine((top, total, accum), attend_keys(one_query, keys, values, scale))
-
-    prefix_state = lax.map(
-        per_request, (req_query, groups_here, start_state[0], start_state[1], start_state[2])
-    )
-    own_keys = suffix_keys.reshape(req_here, SUF, HD)
-    own_values = suffix_values.reshape(req_here, SUF, HD)
-
-    def finish(inputs_one):
-        one_query, keys, values, length, top, total, accum = inputs_one
-        places = jnp.arange(SUF, dtype=jnp.int32)
-        mask = (places[None, :] <= places[:, None]) & (places[None, :] < length)
-        scores = (
-            jnp.einsum("thd,kd->htk", one_query, keys, preferred_element_type=jnp.float32) * scale
-        )
-        scores = jnp.where(mask[None], scores, -1e30)
-        own_top = jnp.max(scores, axis=-1)
-        weights = jnp.exp(scores - own_top[..., None])
-        own_total = jnp.sum(weights, axis=-1)
-        own_accum = jnp.einsum(
-            "htk,kd->htd", weights.astype(jnp.bfloat16), values, preferred_element_type=jnp.float32
-        )
-        merged = combine((top, total, accum), (own_top, own_total, own_accum))
-        result = merged[2] / merged[1][..., None]
-        live = (places < length).astype(jnp.float32)
-        result = result * live[None, :, None]
-        return jnp.transpose(result, (1, 0, 2))
-
-    output = lax.map(
-        finish,
-        (
-            req_query,
-            own_keys,
-            own_values,
-            lengths_here,
-            prefix_state[0],
-            prefix_state[1],
-            prefix_state[2],
-        ),
-    )
-    return output.reshape(tok_block, heads_here * HD).astype(jnp.bfloat16)
+    cache_keys = jnp.where(is_even, prefix_cache, other_cache)
+    cache_values = jnp.where(is_even, other_cache, prefix_cache)
+    kv_block = jnp.concatenate([cache_keys, cache_values], axis=-1)
+
+    half_bit = 2
+    handled = col_id ^ (half_bit * odd)
+    masks = [m for m in range(1, n_col) if m & half_bit == 0]
+    blocks = [lax.dynamic_index_in_dim(kv_block, group_ids[handled], 0, keepdims=False)]
+    for mask in masks:
+        peer_group = group_ids[(col_id ^ mask) ^ (half_bit * odd)]
+        piece = lax.dynamic_index_in_dim(kv_block, peer_group, 0, keepdims=False)
+        pairs = [(c, c ^ mask) for c in range(n_col)]
+        blocks.append(lax.ppermute(piece, "col", pairs))
+    half_kv = jnp.concatenate(blocks, axis=0)
+    half_keys = half_kv[:, :HD]
+    half_values = half_kv[:, HD:]
+
+    axes = ("row", "col")
+    cross = flat_perm(n_row, n_col, lambda r, c: (r ^ 1, c ^ half_bit) if r % 2 == 0 else (r ^ 1, c))
+    back = flat_perm(n_row, n_col, lambda r, c: (r ^ 1, c) if r % 2 == 0 else (r ^ 1, c ^ half_bit))
+    same = flat_perm(n_row, n_col, lambda r, c: (r, c ^ half_bit) if r % 2 == 1 else None)
+    q_cross = lax.ppermute(query, axes, cross)
+    q_same = lax.ppermute(query, axes, same)
+    q_first = jnp.where(is_even, query, q_cross)
+    q_second = jnp.where(is_even, q_cross, q_same)
+    q_all = jnp.concatenate([q_first, q_second], axis=1)
+
+    half_state = attend_keys(q_all, half_keys, half_values, scale)
+    mine = jax.tree.map(
+        lambda a, b: jnp.where(is_even, a, b),
+        jax.tree.map(lambda x: x[:heads_here], half_state),
+        jax.tree.map(lambda x: x[heads_here:], half_state),
+    )
+    theirs = jax.tree.map(
+        lambda a, b: jnp.where(is_even, a, b),
+        jax.tree.map(lambda x: x[heads_here:], half_state),
+        jax.tree.map(lambda x: x[:heads_here], half_state),
+    )
+    from_cross = lax.ppermute(theirs, axes, back)
+    from_same = lax.ppermute(mine, axes, same)
+    first_state = jax.tree.map(lambda a, b: jnp.where(is_even, a, b), mine, from_same)
+
+    length = suffix_lengths[col_id]
+    places = jnp.arange(SUF, dtype=jnp.int32)
+    mask = (places[None, :] <= places[:, None]) & (places[None, :] < length)
+    scores = (
+        jnp.einsum("thd,kd->htk", query, suffix_keys, preferred_element_type=jnp.float32) * scale
+    )
+    scores = jnp.where(mask[None], scores, -1e30)
+    own_top = jnp.max(scores, axis=-1)
+    weights = jnp.exp(scores - own_top[..., None])
+    own_total = jnp.sum(weights, axis=-1)
+    own_accum = jnp.einsum(
+        "htk,kd->htd", weights.astype(jnp.bfloat16), suffix_values, preferred_element_type=jnp.float32
+    )
+    merged = combine_all([first_state, from_cross, (own_top, own_total, own_accum)])
+    result = merged[2] / merged[1][..., None]
+    live = (places < length).astype(jnp.float32)
+    result = result * live[None, :, None]
+    return jnp.transpose(result, (1, 0, 2)).reshape(tok_block, heads_here * HD).astype(jnp.bfloat16)
 
 
 def solution(mesh):

time: 534 us -> 356 us (0.67)
  waiting for transfers between devices: 408 us -> 198 us
  starting transfers between devices: 3.78 us -> 29.7 us
  between operations: 15.4 us -> 29.4 us
  matrix products: 52.5 us -> 41.5 us
    all_gather x2 -> x0, waiting for transfers between devices: 203 us -> none  [the longest x1 102 us: per_device(): piece_values = lax.all_gather(cache_values, 'col', axis=1, tiled=True)]
    ppermute x0 -> x15, waiting for transfers between devices: none -> 73.4 us  [the longest x7 52.8 us: per_device(): blocks.append(lax.ppermute(piece, 'col', pairs))]
    unnamed x5 -> x3, waiting for transfers between devices: 105 us -> 32.7 us
    ppermute x0 -> x15, starting transfers between devices: none -> 26.1 us  [the longest x3 13.5 us: per_device(): from_same = lax.ppermute(mine, axes, same)]
    dot_general x8 -> x4, matrix products: 29 us -> 20.6 us  [block_stats(): jnp.einsum('htk,kd->htd', weights.astype(jnp.bfloat16), values, preferred...]
    ppermute x2, waiting for transfers between devices: 8.43 us -> 0.53 us  [partner(): return lax.ppermute(value, axis, pairs)]
    dynamic_slice x4 -> x2, local copies, waits for them, and re-layouts: 8.63 us -> 1.29 us  [the longest x1 0.68 us: per_device(): peer_group = group_ids[col_id ^ mask ^ half_bit * odd]]
    unnamed x11 -> x27, local copies, waits for them, and re-layouts: 9.79 us -> 16 us
  transfers between devices with their start and end apart: 6 -> 19, of which waited for: 6 -> 11; matrix products, arithmetic and copies ran while one was open for 2% -> 4% of each run, Pallas kernels for 0% -> 0%
where the time goes in v1:
time: 356 us; the launch traced here: 354 us
  waiting for transfers between devices  198 us (56%)
  matrix products  41.5 us (12%)
  local copies, waits for them, and re-layouts  39.7 us (11%)
  starting transfers between devices  29.7 us (8%)
  between operations  29.4 us (8%)
  other arithmetic  16.2 us (5%)
    all_gather x1, waiting for transfers between devices, per_device(): gathered = lax.all_gather(hidden, 'row', axis=0, tiled=True)  91.1 us
    ppermute x7, waiting for transfers between devices, per_device(): blocks.append(lax.ppermute(piece, 'col', pairs))  52.8 us
    unnamed x3, waiting for transfers between devices  32.7 us
    dot_general x4, matrix products, block_stats(): jnp.einsum('htk,kd->htd', weights.astype(jnp.bfloat16), values, preferred...  20.6 us
    while x8, local copies, waits for them, and re-layouts  16.1 us
    unnamed x27, local copies, waits for them, and re-layouts  16 us
    ppermute x3, starting transfers between devices, per_device(): from_same = lax.ppermute(mine, axes, same)  13.5 us
    ppermute x1, waiting for transfers between devices, per_device(): q_cross = lax.ppermute(query, axes, cross)  12.5 us
  transfers between devices with their start and end apart: 19, of which 11 were waited for; matrix products, arithmetic and copies ran while one was open for 4% of the time, Pallas kernels for 0%

profile of v1, /device:TPU:32, one launch (start us, length us, event | category | flops | bytes accessed | tf_op | source)
XLA Modules:
  0.0 354.4 jit_solution(18435070876985730292)
XLA Ops:
  7.3 91.1 %all-gather.2.cloned.1.call-done = bf16[2560,512]{1,0:T(8,128)(2,1)} async-done(((bf16[160,512]{1,0:T(8,128)(2,1)}), bf16[2560,512]{1,0:T(8,128)(2,1)}) %all-gather.2.cloned.1.call-update) | async-done | bytes 2621456 | tf_op jit(solution)/shard_map/all_gather | solution.py:113
  98.4 6.6 %convolution_bitcast_fusion = f32[2560,640]{0,1:T(8,128)} fusion(bf16[2560,512]{1,0:T(8,128)(2,1)} %all-gather.2.cloned.1.call-done, bf16[512,128]{1,0:T(8,128)(2,1)} %param.10, bf16[512,512]{1,0:T(8,128)(2,1)} %param.9), kind=kOutput, calls=%fused_computation.22 | convolution fusion | flops 1679032320 | bytes 9830400 | tf_op jit(solution)/shard_map/dot_general | solution.py:117
  105.0 8.1 %copy.37 = f32[2560,640]{1,0:T(8,128)} copy(f32[2560,640]{0,1:T(8,128)} %convolution_bitcast_fusion) | data formatting | bytes 13107200
  139.3 3.7 %collective-permute-start.4 = (bf16[1024,256]{1,0:T(8,128)(2,1)S(1)}, bf16[1024,256]{1,0:T(8,128)(2,1)S(1)}, u32[]{:S(2)}, u32[]{:S(2)}) collective-permute-start(bf16[1024,256]{1,0:T(8,128)(2,1)S(1)} %get-tuple-element.101), channel_id=1, source_target_pairs={{0,8},{1,9},{2,10},{3,11},{4,12},{5,13},{6,14},{7,15},{8,0},{9,1},... | collective-permute-start | bytes 1572872 | tf_op jit(solution)/shard_map/ppermute | solution.py:149
  149.7 11.7 %collective-permute-done.3 = bf16[1024,256]{1,0:T(8,128)(2,1)} collective-permute-done((bf16[1024,256]{1,0:T(8,128)(2,1)}, bf16[1024,256]{1,0:T(8,128)(2,1)}, u32[]{:S(2)}, u32[]{:S(2)}) %collective-permute-start.3) | collective-permute-done | bytes 524320 | tf_op jit(solution)/shard_map/ppermute | solution.py:149
  162.5 14.7 %collective-permute-done.4 = bf16[1024,256]{1,0:T(8,128)(2,1)S(1)} collective-permute-done((bf16[1024,256]{1,0:T(8,128)(2,1)S(1)}, bf16[1024,256]{1,0:T(8,128)(2,1)S(1)}, u32[]{:S(2)}, u32[]{:S(2)}) %collective-permute-start.4) | collective-permute-done | bytes 524320 | tf_op jit(solution)/shard_map/ppermute | solution.py:149
  177.2 11.4 %collective-permute-done.5 = bf16[1024,256]{1,0:T(8,128)(2,1)S(1)} collective-permute-done((bf16[1024,256]{1,0:T(8,128)(2,1)S(1)}, bf16[1024,256]{1,0:T(8,128)(2,1)S(1)}, u32[]{:S(2)}, u32[]{:S(2)}) %collective-permute-start.5) | collective-permute-done | bytes 524320 | tf_op jit(solution)/shard_map/ppermute | solution.py:149
  188.7 14.9 %collective-permute-done.7 = bf16[1024,256]{1,0:T(8,128)(2,1)S(1)} collective-permute-done((bf16[1024,256]{1,0:T(8,128)(2,1)S(1)}, bf16[1024,256]{1,0:T(8,128)(2,1)S(1)}, u32[]{:S(2)}, u32[]{:S(2)}) %collective-permute-start.7) | collective-permute-done | bytes 524320 | tf_op jit(solution)/shard_map/ppermute | solution.py:149
  205.2 32.0 %reduce-scatter.4.cloned.1.call-done = f32[160,640]{1,0:T(8,128)} async-done(((f32[2560,640]{1,0:T(8,128)}), f32[160,640]{1,0:T(8,128)}) %reduce-scatter.4.cloned.1.call-update) | async-done | bytes 409616
  254.4 12.5 %collective-permute-done.8 = bf16[160,4,128]{2,0,1:T(8,128)(2,1)S(1)} collective-permute-done((bf16[160,4,128]{2,0,1:T(8,128)(2,1)S(1)}, bf16[160,4,128]{2,0,1:T(8,128)(2,1)S(1)}, u32[]{:S(2)}, u32[]{:S(2)}) %collective-permute-start.8) | collective-permute-done | bytes 163872 | tf_op jit(solution)/shard_map/ppermute | solution.py:158
  267.0 55.0 %while.15 = (s32[]{:T(128)}, f32[8,160]{1,0:T(8,128)S(1)}, f32[8,160]{1,0:T(8,128)S(1)}, f32[8,160,128]{2,1,0:T(8,128)S(1)}, bf16[4,2048,128]{2,1,0:T(8,128)(2,1...) while((s32[]{:T(128)}, f32[8,160]{1,0:T(8,128)S(1)}, ...), condition=%wide.region_4.5_spmd.clone, body=%wide.region_1.4_spmd.clone.sunk | while | flops 1363811840 | bytes 76168840 | solution.py:78
  267.0 2.7 bitcast_reduce_fusion.2
  269.7 4.0 %copy-done = f32[2048,160,8]{0,1,2:T(8,128)} copy-done((f32[2048,160,8]{0,1,2:T(8,128)}, f32[2048,160,8]{0,1,2:T(8,128)S(1)}, u32[]{:S(2)}) %copy-start) | copy-done | bytes 10485784 | tf_op jit(solution)/shard_map/while
  275.6 5.1 %fusion.85 = f32[8,160,128]{2,1,0:T(8,128)S(1)} fusion(f32[2048,160,8]{0,1,2:T(8,128)} %copy-done, f32[8,160]{1,0:T(8,128)S(1)} %get-tuple-element.181, f32[8,160,128]{2,1,0:T(8,128)S(1)} %get-tuple-element.198, bf16[4,2048,128]{2,1,0:T(8,128)(2,1)S(1)} %get-tuple-element.210, s32[]{:T(128)} %get-tuple-element.195, ...), kind=kOutput, calls=%fused_computation.7.clone.1 | convolution fusion | flops 679608320 | bytes 12345349 | tf_op jit(solution)/shard_map/while/body/eval_jaxpr/htk,kd->htd/dot_general | solution.py:46
  283.5 4.0 %copy-done = f32[2048,160,8]{0,1,2:T(8,128)} copy-done((f32[2048,160,8]{0,1,2:T(8,128)}, f32[2048,160,8]{0,1,2:T(8,128)S(1)}, u32[]{:S(2)}) %copy-start) | copy-done | bytes 10485784 | tf_op jit(solution)/shard_map/while
  289.4 5.1 %fusion.85 = f32[8,160,128]{2,1,0:T(8,128)S(1)} fusion(f32[2048,160,8]{0,1,2:T(8,128)} %copy-done, f32[8,160]{1,0:T(8,128)S(1)} %get-tuple-element.181, f32[8,160,128]{2,1,0:T(8,128)S(1)} %get-tuple-element.198, bf16[4,2048,128]{2,1,0:T(8,128)(2,1)S(1)} %get-tuple-element.210, s32[]{:T(128)} %get-tuple-element.195, ...), kind=kOutput, calls=%fused_computation.7.clone.1 | convolution fusion | flops 679608320 | bytes 12345349 | tf_op jit(solution)/shard_map/while/body/eval_jaxpr/htk,kd->htd/dot_general | solution.py:46
  297.2 4.0 %copy-done = f32[2048,160,8]{0,1,2:T(8,128)} copy-done((f32[2048,160,8]{0,1,2:T(8,128)}, f32[2048,160,8]{0,1,2:T(8,128)S(1)}, u32[]{:S(2)}) %copy-start) | copy-done | bytes 10485784 | tf_op jit(solution)/shard_map/while
  303.2 5.1 %fusion.85 = f32[8,160,128]{2,1,0:T(8,128)S(1)} fusion(f32[2048,160,8]{0,1,2:T(8,128)} %copy-done, f32[8,160]{1,0:T(8,128)S(1)} %get-tuple-element.181, f32[8,160,128]{2,1,0:T(8,128)S(1)} %get-tuple-element.198, bf16[4,2048,128]{2,1,0:T(8,128)(2,1)S(1)} %get-tuple-element.210, s32[]{:T(128)} %get-tuple-element.195, ...), kind=kOutput, calls=%fused_computation.7.clone.1 | convolution fusion | flops 679608320 | bytes 12345349 | tf_op jit(solution)/shard_map/while/body/eval_jaxpr/htk,kd->htd/dot_general | solution.py:46
  311.0 4.0 %copy-done = f32[2048,160,8]{0,1,2:T(8,128)} copy-done((f32[2048,160,8]{0,1,2:T(8,128)}, f32[2048,160,8]{0,1,2:T(8,128)S(1)}, u32[]{:S(2)}) %copy-start) | copy-done | bytes 10485784 | tf_op jit(solution)/shard_map/while
  316.9 5.1 %fusion.85 = f32[8,160,128]{2,1,0:T(8,128)S(1)} fusion(f32[2048,160,8]{0,1,2:T(8,128)} %copy-done, f32[8,160]{1,0:T(8,128)S(1)} %get-tuple-element.181, f32[8,160,128]{2,1,0:T(8,128)S(1)} %get-tuple-element.198, bf16[4,2048,128]{2,1,0:T(8,128)(2,1)S(1)} %get-tuple-element.210, s32[]{:T(128)} %get-tuple-element.195, ...), kind=kOutput, calls=%fused_computation.7.clone.1 | convolution fusion | flops 679608320 | bytes 12345349 | tf_op jit(solution)/shard_map/while/body/eval_jaxpr/htk,kd->htd/dot_general | solution.py:46
  322.1 3.8 %collective-permute-start.10 = (f32[4,160,128]{2,1,0:T(8,128)S(1)}, f32[4,160,128]{2,1,0:T(8,128)S(1)}, u32[]{:S(2)}, u32[]{:S(2)}) collective-permute-start(f32[4,160,128]{2,1,0:T(8,128)S(1)} %get-tuple-element.107), channel_id=1, source_target_pairs={{16,18},{17,19},{18,16},{19,17},{20,22},{21,23},{22,20},{23,21},{2... | collective-permute-start | bytes 983048 | tf_op jit(solution)/shard_map/ppermute | solution.py:176
  326.0 6.0 %collective-permute-start.11 = (f32[4,160]{1,0:T(4,128)S(1)}, f32[4,160]{1,0:T(4,128)S(1)}, u32[]{:S(2)}, u32[]{:S(2)}) collective-permute-start(f32[4,160]{1,0:T(4,128)S(1)} %get-tuple-element.115), channel_id=1, source_target_pairs={{16,18},{17,19},{18,16},{19,17},{20,22},{21,23},{22,20},{23,21},{2... | collective-permute-start | bytes 7688 | tf_op jit(solution)/shard_map/ppermute | solution.py:176
  332.1 3.8 %collective-permute-start.15 = (f32[4,160]{1,0:T(4,128)S(1)}, f32[4,160]{1,0:T(4,128)S(1)}, u32[]{:S(2)}, u32[]{:S(2)}) collective-permute-start(f32[4,160]{1,0:T(4,128)S(1)} %get-tuple-element.117), channel_id=1, source_target_pairs={{16,18},{17,19},{18,16},{19,17},{20,22},{21,23},{22,20},{23,21},{2... | collective-permute-start | bytes 7688 | tf_op jit(solution)/shard_map/ppermute | solution.py:176
  335.9 5.6 %collective-permute-done.11 = f32[4,160]{1,0:T(4,128)S(1)} collective-permute-done((f32[4,160]{1,0:T(4,128)S(1)}, f32[4,160]{1,0:T(4,128)S(1)}, u32[]{:S(2)}, u32[]{:S(2)}) %collective-permute-start.11) | collective-permute-done | bytes 2592 | tf_op jit(solution)/shard_map/ppermute | solution.py:176
  (103 shorter events, 59.7 us)
Async XLA Ops:
  6.5 91.9 %all-gather.2.cloned.1.call-start = ((), (), s32[]{:S(2)}) async-start(), calls=%async_computation.1 | async-start | bytes 2785280 | tf_op jit(solution)/shard_map/all_gather | solution.py:113
  7.3 230.0 %reduce-scatter.4.cloned.1.call-start = ((), (), s32[]{:S(2)}) async-start(), calls=%async_computation.2 | async-start | bytes 6963200
  113.2 14.9 %copy-start.7 = (s32[16]{0:T(128)S(1)}, s32[16]{0:T(128)}, u32[]{:S(2)}) copy-start(s32[16]{0:T(128)} %param.12) | copy-start | bytes 196
  114.2 16.2 %collective-permute-start = (bf16[2,1024,128]{2,1,0:T(8,128)(2,1)S(1)}, bf16[2,1024,128]{2,1,0:T(8,128)(2,1)S(1)}, u32[]{:S(2)}, u32[]{:S(2)}) collective-permute-start(bf16[2,1024,128]{2,1,0:T(8,128)(2,1)S(1)} %copy-done.1), channel_id=1, source_target_pairs={{0,16},{16,0},{32,48},{48,32},{64,80},{80,64},{96,112},{112,96},{1... | collective-permute-start | bytes 1572872 | tf_op jit(solution)/shard_map/ppermute | solution.py:14
  128.7 8.8 %copy-start.6 = (f32[64]{0:T(128)}, f32[64]{0:T(128)S(1)}, u32[]{:S(2)}) copy-start(f32[64]{0:T(128)S(1)} %negate_power_fusion) | copy-start | bytes 772
  131.9 11.4 %collective-permute-start.1 = (bf16[1024,256]{1,0:T(8,128)(2,1)}, bf16[1024,256]{1,0:T(8,128)(2,1)}, u32[]{:S(2)}, u32[]{:S(2)}) collective-permute-start(bf16[1024,256]{1,0:T(8,128)(2,1)} %get-tuple-element.98), channel_id=1, source_target_pairs={{0,1},{1,0},{2,3},{3,2},{4,5},{5,4},{6,7},{7,6},{8,9},{9,8},{10,11... | collective-permute-start | bytes 1572872 | tf_op jit(solution)/shard_map/ppermute | solution.py:149
  131.9 15.1 %collective-permute-start.2 = (bf16[1024,256]{1,0:T(8,128)(2,1)}, bf16[1024,256]{1,0:T(8,128)(2,1)}, u32[]{:S(2)}, u32[]{:S(2)}) collective-permute-start(bf16[1024,256]{1,0:T(8,128)(2,1)} %get-tuple-element.99), channel_id=1, source_target_pairs={{0,4},{1,5},{2,6},{3,7},{4,0},{5,1},{6,2},{7,3},{8,12},{9,13},{10,... | collective-permute-start | bytes 1572872 | tf_op jit(solution)/shard_map/ppermute | solution.py:149
  134.2 27.2 %collective-permute-start.3 = (bf16[1024,256]{1,0:T(8,128)(2,1)}, bf16[1024,256]{1,0:T(8,128)(2,1)}, u32[]{:S(2)}, u32[]{:S(2)}) collective-permute-start(bf16[1024,256]{1,0:T(8,128)(2,1)} %get-tuple-element.100), channel_id=1, source_target_pairs={{0,5},{1,4},{2,7},{3,6},{4,1},{5,0},{6,3},{7,2},{8,13},{9,12},{10,... | collective-permute-start | bytes 1572872 | tf_op jit(solution)/shard_map/ppermute | solution.py:149
  139.3 37.9 %collective-permute-start.4 = (bf16[1024,256]{1,0:T(8,128)(2,1)S(1)}, bf16[1024,256]{1,0:T(8,128)(2,1)S(1)}, u32[]{:S(2)}, u32[]{:S(2)}) collective-permute-start(bf16[1024,256]{1,0:T(8,128)(2,1)S(1)} %get-tuple-element.101), channel_id=1, source_target_pairs={{0,8},{1,9},{2,10},{3,11},{4,12},{5,13},{6,14},{7,15},{8,0},{9,1},... | collective-permute-start | bytes 1572872 | tf_op jit(solution)/shard_map/ppermute | solution.py:149
  143.1 45.5 %collective-permute-start.5 = (bf16[1024,256]{1,0:T(8,128)(2,1)S(1)}, bf16[1024,256]{1,0:T(8,128)(2,1)S(1)}, u32[]{:S(2)}, u32[]{:S(2)}) collective-permute-start(bf16[1024,256]{1,0:T(8,128)(2,1)S(1)} %get-tuple-element.102), channel_id=1, source_target_pairs={{0,9},{1,8},{2,11},{3,10},{4,13},{5,12},{6,15},{7,14},{8,1},{9,0},... | collective-permute-start | bytes 1572872 | tf_op jit(solution)/shard_map/ppermute | solution.py:149
  143.2 45.4 %collective-permute-start.6 = (bf16[1024,256]{1,0:T(8,128)(2,1)S(1)}, bf16[1024,256]{1,0:T(8,128)(2,1)S(1)}, u32[]{:S(2)}, u32[]{:S(2)}) collective-permute-start(bf16[1024,256]{1,0:T(8,128)(2,1)S(1)} %fusion.43), channel_id=1, source_target_pairs={{0,12},{1,13},{2,14},{3,15},{4,8},{5,9},{6,10},{7,11},{8,4},{9,5},... | collective-permute-start | bytes 1572872 | tf_op jit(solution)/shard_map/ppermute | solution.py:149
  147.0 56.6 %collective-permute-start.7 = (bf16[1024,256]{1,0:T(8,128)(2,1)S(1)}, bf16[1024,256]{1,0:T(8,128)(2,1)S(1)}, u32[]{:S(2)}, u32[]{:S(2)}) collective-permute-start(bf16[1024,256]{1,0:T(8,128)(2,1)S(1)} %get-tuple-element.97), channel_id=1, source_target_pairs={{0,13},{1,12},{2,15},{3,14},{4,9},{5,8},{6,11},{7,10},{8,5},{9,4},... | collective-permute-start | bytes 1572872 | tf_op jit(solution)/shard_map/ppermute | solution.py:149
  245.7 21.3 %copy-start.2 = (bf16[160,128]{0,1:T(8,128)(2,1)}, bf16[160,128]{0,1:T(8,128)(2,1)S(1)}, u32[]{:S(2)}) copy-start(bf16[160,128]{0,1:T(8,128)(2,1)S(1)} %fusion.52) | copy-start | bytes 122884
  245.7 6.7 %collective-permute-start.13 = (bf16[160,1,128]{0,2,1:T(8,128)(2,1)S(1)}, bf16[160,1,128]{0,2,1:T(8,128)(2,1)S(1)}, u32[]{:S(2)}, u32[]{:S(2)}) collective-permute-start(bf16[160,1,128]{0,2,1:T(8,128)(2,1)S(1)} %bitcast.113), channel_id=1, source_target_pairs={{0,16},{16,0},{32,48},{48,32},{64,80},{80,64},{96,112},{112,96},{1... | collective-permute-start | bytes 122888 | tf_op jit(solution)/shard_map/ppermute | solution.py:14
  249.3 17.6 %collective-permute-start.8 = (bf16[160,4,128]{2,0,1:T(8,128)(2,1)S(1)}, bf16[160,4,128]{2,0,1:T(8,128)(2,1)S(1)}, u32[]{:S(2)}, u32[]{:S(2)}) collective-permute-start(bf16[160,4,128]{2,0,1:T(8,128)(2,1)S(1)} %pad_maximum_fusion.1), channel_id=1, source_target_pairs={{0,18},{1,19},{2,16},{3,17},{4,22},{5,23},{6,20},{7,21},{8,26},{9,... | collective-permute-start | bytes 491528 | tf_op jit(solution)/shard_map/ppermute | solution.py:158
  249.4 17.5 %collective-permute-start.9 = (bf16[160,4,128]{2,0,1:T(8,128)(2,1)S(1)}, bf16[160,4,128]{2,0,1:T(8,128)(2,1)S(1)}, u32[]{:S(2)}, u32[]{:S(2)}) collective-permute-start(bf16[160,4,128]{2,0,1:T(8,128)(2,1)S(1)} %pad_maximum_fusion.1), channel_id=1, source_target_pairs={{16,18},{17,19},{18,16},{19,17},{20,22},{21,23},{22,20},{23,21},{2... | collective-permute-start | bytes 491528 | tf_op jit(solution)/shard_map/ppermute | solution.py:159
  267.0 78.2 %copy-start.3 = (bf16[160,128]{0,1:T(8,128)(2,1)S(1)}, bf16[160,128]{0,1:T(8,128)(2,1)}, u32[]{:S(2)}) copy-start(bf16[160,128]{0,1:T(8,128)(2,1)} %copy-done.2) | copy-start | bytes 122884
  267.0 78.2 %copy-start.8 = (f32[160]{0:T(256)S(1)}, f32[160]{0:T(256)}, u32[]{:S(2)}) copy-start(f32[160]{0:T(256)} %fusion.66) | copy-start | bytes 1924
  322.1 23.0 %collective-permute-start.10 = (f32[4,160,128]{2,1,0:T(8,128)S(1)}, f32[4,160,128]{2,1,0:T(8,128)S(1)}, u32[]{:S(2)}, u32[]{:S(2)}) collective-permute-start(f32[4,160,128]{2,1,0:T(8,128)S(1)} %get-tuple-element.107), channel_id=1, source_target_pairs={{16,18},{17,19},{18,16},{19,17},{20,22},{21,23},{22,20},{23,21},{2... | collective-permute-start | bytes 983048 | tf_op jit(solution)/shard_map/ppermute | solution.py:176
  325.9 19.2 %collective-permute-start.14 = (f32[4,160,128]{2,1,0:T(8,128)S(1)}, f32[4,160,128]{2,1,0:T(8,128)S(1)}, u32[]{:S(2)}, u32[]{:S(2)}) collective-permute-start(f32[4,160,128]{2,1,0:T(8,128)S(1)} %get-tuple-element.108), channel_id=1, source_target_pairs={{0,16},{1,17},{2,18},{3,19},{4,20},{5,21},{6,22},{7,23},{8,24},{9,... | collective-permute-start | bytes 983048 | tf_op jit(solution)/shard_map/ppermute | solution.py:175
  326.0 15.5 %collective-permute-start.11 = (f32[4,160]{1,0:T(4,128)S(1)}, f32[4,160]{1,0:T(4,128)S(1)}, u32[]{:S(2)}, u32[]{:S(2)}) collective-permute-start(f32[4,160]{1,0:T(4,128)S(1)} %get-tuple-element.115), channel_id=1, source_target_pairs={{16,18},{17,19},{18,16},{19,17},{20,22},{21,23},{22,20},{23,21},{2... | collective-permute-start | bytes 7688 | tf_op jit(solution)/shard_map/ppermute | solution.py:176
  332.0 10.7 %collective-permute-start.12 = (f32[4,160]{1,0:T(4,128)S(1)}, f32[4,160]{1,0:T(4,128)S(1)}, u32[]{:S(2)}, u32[]{:S(2)}) collective-permute-start(f32[4,160]{1,0:T(4,128)S(1)} %get-tuple-element.116), channel_id=1, source_target_pairs={{0,16},{1,17},{2,18},{3,19},{4,20},{5,21},{6,22},{7,23},{8,24},{9,... | collective-permute-start | bytes 7688 | tf_op jit(solution)/shard_map/ppermute | solution.py:175
  332.1 10.6 %collective-permute-start.15 = (f32[4,160]{1,0:T(4,128)S(1)}, f32[4,160]{1,0:T(4,128)S(1)}, u32[]{:S(2)}, u32[]{:S(2)}) collective-permute-start(f32[4,160]{1,0:T(4,128)S(1)} %get-tuple-element.117), channel_id=1, source_target_pairs={{16,18},{17,19},{18,16},{19,17},{20,22},{21,23},{22,20},{23,21},{2... | collective-permute-start | bytes 7688 | tf_op jit(solution)/shard_map/ppermute | solution.py:176
  341.5 3.6 %collective-permute-start.16 = (f32[4,160]{1,0:T(4,128)S(1)}, f32[4,160]{1,0:T(4,128)S(1)}, u32[]{:S(2)}, u32[]{:S(2)}) collective-permute-start(f32[4,160]{1,0:T(4,128)S(1)} %get-tuple-element.118), channel_id=1, source_target_pairs={{0,16},{1,17},{2,18},{3,19},{4,20},{5,21},{6,22},{7,23},{8,24},{9,... | collective-permute-start | bytes 7688 | tf_op jit(solution)/shard_map/ppermute | solution.py:175
  (7 other events, 27.4 us)
Sparse Core Ops, SparseCore 0:
  9.1 89.2 all-gather.1
  113.3 123.8 reduce-scatter.3

commit v2 on v1

--- a/solution.py
+++ b/solution.py
@@ -110,15 +110,37 @@
     heads_here = w_query.shape[1] // HD
     segments = w_keyval.shape[1] // HD
     scale = 1.0 / HD**0.5
-    gathered = lax.all_gather(hidden, "row", axis=0, tiled=True)
+    half_bit = 2
+    stacked = [hidden]
+    for mask in range(1, n_row):
+        stacked.append(lax.ppermute(hidden, "row", [(i, i ^ mask) for i in range(n_row)]))
+    stacked = jnp.stack(stacked)
+    order = row_id ^ jnp.arange(n_row, dtype=jnp.int32)
+    gathered = jnp.take(stacked, order, axis=0).reshape(-1, hidden.shape[1])
     weights_all = jnp.concatenate([w_query, w_keyval], axis=1)
     tok_block = gathered.shape[0] // n_col
-    projected = lax.psum_scatter(
-        jnp.dot(gathered, weights_all, preferred_element_type=jnp.float32),
-        "col",
-        scatter_dimension=0,
-        tiled=True,
-    )
+    partial = jnp.dot(gathered, weights_all, preferred_element_type=jnp.float32)
+    partial = partial.reshape(n_col, tok_block, partial.shape[1])
+    own_pair = jnp.stack(
+        [
+            lax.dynamic_index_in_dim(partial, col_id, 0, keepdims=False),
+            lax.dynamic_index_in_dim(partial, col_id ^ half_bit, 0, keepdims=False),
+        ]
+    )
+    half_sum = own_pair
+    low = partial.astype(jnp.bfloat16)
+    for mask in [m for m in range(1, n_col) if m & half_bit == 0]:
+        peer = col_id ^ mask
+        piece = jnp.stack(
+            [
+                lax.dynamic_index_in_dim(low, peer, 0, keepdims=False),
+                lax.dynamic_index_in_dim(low, peer ^ half_bit, 0, keepdims=False),
+            ]
+        )
+        got = lax.ppermute(piece, "col", [(c, c ^ mask) for c in range(n_col)])
+        half_sum = half_sum + got.astype(jnp.float32)
+    across = lax.ppermute(half_sum[1], "col", [(c, c ^ half_bit) for c in range(n_col)])
+    projected = half_sum[0] + across
     positions = PREFIX + jnp.arange(tok_block, dtype=jnp.int32) % SUF
     cosine, sine = rotary_tables(positions)
     query = projected[:, : heads_here * HD].reshape(tok_block, heads_here, HD)
@@ -138,7 +160,6 @@
     cache_values = jnp.where(is_even, other_cache, prefix_cache)
     kv_block = jnp.concatenate([cache_keys, cache_values], axis=-1)
 
-    half_bit = 2
     handled = col_id ^ (half_bit * odd)
     masks = [m for m in range(1, n_col) if m & half_bit == 0]
     blocks = [lax.dynamic_index_in_dim(kv_block, group_ids[handled], 0, keepdims=False)]

time: 356 us -> 296 us (0.83)
  waiting for transfers between devices: 198 us -> 111 us
  starting transfers between devices: 29.7 us -> 69.5 us
  between operations: 29.4 us -> 15.9 us
    all_gather x1 -> x0, waiting for transfers between devices: 91.1 us -> none  [per_device(): gathered = lax.all_gather(hidden, 'row', axis=0, tiled=True)]
    ppermute x0 -> x23, waiting for transfers between devices: none -> 60.7 us  [the longest x7 32.8 us: per_device(): got = lax.ppermute(piece, 'col', [(c, c ^ mask) for c in range(n_col)])]
    ppermute x0 -> x23, starting transfers between devices: none -> 43.9 us  [the longest x15 28.8 us: per_device(): lax.ppermute(hidden, 'row', [(i, i ^ mask) for i in range(n_row)])]
    unnamed x3 -> x0, waiting for transfers between devices: 32.7 us -> none
    ppermute x7, waiting for transfers between devices: 52.8 us -> 34.7 us  [per_device(): blocks.append(lax.ppermute(piece, 'col', pairs))]
    ppermute x1, waiting for transfers between devices: 12.5 us -> 0.01 us  [per_device(): q_cross = lax.ppermute(query, axes, cross)]
    ppermute x3, waiting for transfers between devices: 5.63 us -> 9.62 us  [per_device(): from_same = lax.ppermute(mine, axes, same)]
    unnamed x27 -> x41, local copies, waits for them, and re-layouts: 16 us -> 15.5 us
  transfers between devices with their start and end apart: 19 -> 40, of which waited for: 11 -> 17; matrix products, arithmetic and copies ran while one was open for 4% -> 14% of each run, Pallas kernels for 0% -> 0%
where the time goes in v2:
time: 296 us; the launch traced here: 295 us
  waiting for transfers between devices  111 us (38%)
  starting transfers between devices  69.5 us (23%)
  local copies, waits for them, and re-layouts  40.9 us (14%)
  matrix products  38.7 us (13%)
  other arithmetic  18.5 us (6%)
  between operations  15.9 us (5%)
    ppermute x7, waiting for transfers between devices, per_device(): blocks.append(lax.ppermute(piece, 'col', pairs))  34.7 us
    ppermute x7, waiting for transfers between devices, per_device(): got = lax.ppermute(piece, 'col', [(c, c ^ mask) for c in range(n_col)])  32.8 us
    ppermute x15, starting transfers between devices, per_device(): lax.ppermute(hidden, 'row', [(i, i ^ mask) for i in range(n_row)])  28.8 us
    dot_general x4, matrix products, block_stats(): jnp.einsum('htk,kd->htd', weights.astype(jnp.bfloat16), values, preferred...  20.5 us
    ppermute x15, waiting for transfers between devices, per_device(): lax.ppermute(hidden, 'row', [(i, i ^ mask) for i in range(n_row)])  16.6 us
    while x8, local copies, waits for them, and re-layouts  16.1 us
    unnamed x41, local copies, waits for them, and re-layouts  15.5 us
    ppermute x3, starting transfers between devices, per_device(): from_same = lax.ppermute(mine, axes, same)  12.7 us
  transfers between devices with their start and end apart: 40, of which 17 were waited for; matrix products, arithmetic and copies ran while one was open for 14% of the time, Pallas kernels for 0%

profile of v2, /device:TPU:32, one launch (start us, length us, event | category | flops | bytes accessed | tf_op | source)
XLA Modules:
  0.0 294.9 jit_solution(10253651892051398861)
XLA Ops:
  47.5 8.2 %collective-permute-done.14 = bf16[160,512]{1,0:T(8,128)(2,1)S(1)} collective-permute-done((bf16[160,512]{1,0:T(8,128)(2,1)}, bf16[160,512]{1,0:T(8,128)(2,1)S(1)}, u32[]{:S(2)}, u32[]{:S(2)}) %collective-permute-start.14) | collective-permute-done | bytes 163872 | tf_op jit(solution)/shard_map/ppermute | solution.py:116
  59.7 5.0 %collective-permute-start.21 = (bf16[160,512]{1,0:T(8,128)(2,1)S(1)}, bf16[160,512]{1,0:T(8,128)(2,1)S(1)}, u32[]{:S(2)}, u32[]{:S(2)}) collective-permute-start(bf16[160,512]{1,0:T(8,128)(2,1)S(1)} %copy-done.4), channel_id=1, source_target_pairs={{0,224},{16,240},{32,192},{48,208},{64,160},{80,176},{96,128},{112... | collective-permute-start | bytes 491528 | tf_op jit(solution)/shard_map/ppermute | solution.py:116
  69.0 4.1 %collective-permute-done.19 = bf16[160,512]{1,0:T(8,128)(2,1)S(1)} collective-permute-done((bf16[160,512]{1,0:T(8,128)(2,1)S(1)}, bf16[160,512]{1,0:T(8,128)(2,1)S(1)}, u32[]{:S(2)}, u32[]{:S(2)}) %collective-permute-start.19) | collective-permute-done | bytes 163872 | tf_op jit(solution)/shard_map/ppermute | solution.py:116
  100.4 4.8 %collective-permute-done.25 = bf16[2,160,640]{2,1,0:T(8,128)(2,1)S(1)} collective-permute-done((bf16[2,160,640]{2,1,0:T(8,128)(2,1)S(1)}, bf16[2,160,640]{2,1,0:T(8,128)(2,1)S(1)}, u32[]{:S(2)}, u32[]{:S(2)}) %collective-permute-start.25) | collective-permute-done | bytes 409632 | tf_op jit(solution)/shard_map/ppermute | solution.py:140
  105.2 12.2 %collective-permute-done.26 = bf16[2,160,640]{2,1,0:T(8,128)(2,1)S(1)} collective-permute-done((bf16[2,160,640]{2,1,0:T(8,128)(2,1)S(1)}, bf16[2,160,640]{2,1,0:T(8,128)(2,1)S(1)}, u32[]{:S(2)}, u32[]{:S(2)}) %collective-permute-start.26) | collective-permute-done | bytes 409632 | tf_op jit(solution)/shard_map/ppermute | solution.py:140
  117.4 7.8 %collective-permute-done.27 = bf16[2,160,640]{2,1,0:T(8,128)(2,1)S(1)} collective-permute-done((bf16[2,160,640]{2,1,0:T(8,128)(2,1)S(1)}, bf16[2,160,640]{2,1,0:T(8,128)(2,1)S(1)}, u32[]{:S(2)}, u32[]{:S(2)}) %collective-permute-start.27) | collective-permute-done | bytes 409632 | tf_op jit(solution)/shard_map/ppermute | solution.py:140
  125.2 4.2 %collective-permute-done.29 = bf16[2,160,640]{2,1,0:T(8,128)(2,1)S(1)} collective-permute-done((bf16[2,160,640]{2,1,0:T(8,128)(2,1)S(1)}, bf16[2,160,640]{2,1,0:T(8,128)(2,1)S(1)}, u32[]{:S(2)}, u32[]{:S(2)}) %collective-permute-start.29) | collective-permute-done | bytes 409632 | tf_op jit(solution)/shard_map/ppermute | solution.py:140
  129.8 5.0 %collective-permute-start.30 = (f32[160,640]{1,0:T(8,128)S(1)}, f32[160,640]{1,0:T(8,128)S(1)}, u32[]{:S(2)}, u32[]{:S(2)}) collective-permute-start(f32[160,640]{1,0:T(8,128)S(1)} %slice_bitcast_fusion), channel_id=1, source_target_pairs={{0,2},{1,3},{2,0},{3,1},{4,6},{5,7},{6,4},{7,5},{8,10},{9,11},{10,... | collective-permute-start | bytes 1228808 | tf_op jit(solution)/shard_map/ppermute | solution.py:142
  142.5 11.4 %collective-permute-done.30 = f32[160,640]{1,0:T(8,128)S(1)} collective-permute-done((f32[160,640]{1,0:T(8,128)S(1)}, f32[160,640]{1,0:T(8,128)S(1)}, u32[]{:S(2)}, u32[]{:S(2)}) %collective-permute-start.30) | collective-permute-done | bytes 409632 | tf_op jit(solution)/shard_map/ppermute | solution.py:142
  170.5 5.8 %collective-permute-done.4 = bf16[1024,256]{1,0:T(8,128)(2,1)} collective-permute-done((bf16[1024,256]{1,0:T(8,128)(2,1)S(1)}, bf16[1024,256]{1,0:T(8,128)(2,1)}, u32[]{:S(2)}, u32[]{:S(2)}) %collective-permute-start.4) | collective-permute-done | bytes 524320 | tf_op jit(solution)/shard_map/ppermute | solution.py:170
  180.3 6.1 %collective-permute-done.5 = bf16[1024,256]{1,0:T(8,128)(2,1)S(1)} collective-permute-done((bf16[1024,256]{1,0:T(8,128)(2,1)S(1)}, bf16[1024,256]{1,0:T(8,128)(2,1)S(1)}, u32[]{:S(2)}, u32[]{:S(2)}) %collective-permute-start.5) | collective-permute-done | bytes 524320 | tf_op jit(solution)/shard_map/ppermute | solution.py:170
  186.5 11.5 %collective-permute-done.6 = bf16[1024,256]{1,0:T(8,128)(2,1)S(1)} collective-permute-done((bf16[1024,256]{1,0:T(8,128)(2,1)}, bf16[1024,256]{1,0:T(8,128)(2,1)S(1)}, u32[]{:S(2)}, u32[]{:S(2)}) %collective-permute-start.6) | collective-permute-done | bytes 524320 | tf_op jit(solution)/shard_map/ppermute | solution.py:170
  198.0 11.2 %collective-permute-done.7 = bf16[1024,256]{1,0:T(8,128)(2,1)S(1)} collective-permute-done((bf16[1024,256]{1,0:T(8,128)(2,1)S(1)}, bf16[1024,256]{1,0:T(8,128)(2,1)S(1)}, u32[]{:S(2)}, u32[]{:S(2)}) %collective-permute-start.7) | collective-permute-done | bytes 524320 | tf_op jit(solution)/shard_map/ppermute | solution.py:170
  211.1 55.1 %while.15 = (s32[]{:T(128)}, f32[8,160]{1,0:T(8,128)S(1)}, f32[8,160]{1,0:T(8,128)S(1)}, f32[8,160,128]{2,1,0:T(8,128)S(1)}, bf16[4,2048,128]{2,1,0:T(8,128)(2,1...) while((s32[]{:T(128)}, f32[8,160]{1,0:T(8,128)S(1)}, ...), condition=%wide.region_3.4_spmd.clone, body=%wide.region_0.3_spmd.clone.sunk | while | flops 1363811840 | bytes 76168840 | solution.py:78
  213.8 4.0 %copy-done = f32[2048,160,8]{0,1,2:T(8,128)} copy-done((f32[2048,160,8]{0,1,2:T(8,128)}, f32[2048,160,8]{0,1,2:T(8,128)S(1)}, u32[]{:S(2)}) %copy-start) | copy-done | bytes 10485784 | tf_op jit(solution)/shard_map/while
  219.7 5.1 %fusion.97 = f32[8,160,128]{2,1,0:T(8,128)S(1)} fusion(f32[2048,160,8]{0,1,2:T(8,128)} %copy-done, f32[8,160]{1,0:T(8,128)S(1)} %get-tuple-element.199, f32[8,160,128]{2,1,0:T(8,128)S(1)} %get-tuple-element.216, bf16[4,2048,128]{2,1,0:T(8,128)(2,1)S(1)} %get-tuple-element.228, s32[]{:T(128)} %get-tuple-element.213, ...), kind=kOutput, calls=%fused_computation.8.clone.1 | convolution fusion | flops 679608320 | bytes 12345349 | tf_op jit(solution)/shard_map/while/body/eval_jaxpr/htk,kd->htd/dot_general | solution.py:46
  227.6 4.0 %copy-done = f32[2048,160,8]{0,1,2:T(8,128)} copy-done((f32[2048,160,8]{0,1,2:T(8,128)}, f32[2048,160,8]{0,1,2:T(8,128)S(1)}, u32[]{:S(2)}) %copy-start) | copy-done | bytes 10485784 | tf_op jit(solution)/shard_map/while
  233.5 5.1 %fusion.97 = f32[8,160,128]{2,1,0:T(8,128)S(1)} fusion(f32[2048,160,8]{0,1,2:T(8,128)} %copy-done, f32[8,160]{1,0:T(8,128)S(1)} %get-tuple-element.199, f32[8,160,128]{2,1,0:T(8,128)S(1)} %get-tuple-element.216, bf16[4,2048,128]{2,1,0:T(8,128)(2,1)S(1)} %get-tuple-element.228, s32[]{:T(128)} %get-tuple-element.213, ...), kind=kOutput, calls=%fused_computation.8.clone.1 | convolution fusion | flops 679608320 | bytes 12345349 | tf_op jit(solution)/shard_map/while/body/eval_jaxpr/htk,kd->htd/dot_general | solution.py:46
  241.4 4.0 %copy-done = f32[2048,160,8]{0,1,2:T(8,128)} copy-done((f32[2048,160,8]{0,1,2:T(8,128)}, f32[2048,160,8]{0,1,2:T(8,128)S(1)}, u32[]{:S(2)}) %copy-start) | copy-done | bytes 10485784 | tf_op jit(solution)/shard_map/while
  247.3 5.1 %fusion.97 = f32[8,160,128]{2,1,0:T(8,128)S(1)} fusion(f32[2048,160,8]{0,1,2:T(8,128)} %copy-done, f32[8,160]{1,0:T(8,128)S(1)} %get-tuple-element.199, f32[8,160,128]{2,1,0:T(8,128)S(1)} %get-tuple-element.216, bf16[4,2048,128]{2,1,0:T(8,128)(2,1)S(1)} %get-tuple-element.228, s32[]{:T(128)} %get-tuple-element.213, ...), kind=kOutput, calls=%fused_computation.8.clone.1 | convolution fusion | flops 679608320 | bytes 12345349 | tf_op jit(solution)/shard_map/while/body/eval_jaxpr/htk,kd->htd/dot_general | solution.py:46
  255.1 4.0 %copy-done = f32[2048,160,8]{0,1,2:T(8,128)} copy-done((f32[2048,160,8]{0,1,2:T(8,128)}, f32[2048,160,8]{0,1,2:T(8,128)S(1)}, u32[]{:S(2)}) %copy-start) | copy-done | bytes 10485784 | tf_op jit(solution)/shard_map/while
  261.1 5.1 %fusion.97 = f32[8,160,128]{2,1,0:T(8,128)S(1)} fusion(f32[2048,160,8]{0,1,2:T(8,128)} %copy-done, f32[8,160]{1,0:T(8,128)S(1)} %get-tuple-element.199, f32[8,160,128]{2,1,0:T(8,128)S(1)} %get-tuple-element.216, bf16[4,2048,128]{2,1,0:T(8,128)(2,1)S(1)} %get-tuple-element.228, s32[]{:T(128)} %get-tuple-element.213, ...), kind=kOutput, calls=%fused_computation.8.clone.1 | convolution fusion | flops 679608320 | bytes 12345349 | tf_op jit(solution)/shard_map/while/body/eval_jaxpr/htk,kd->htd/dot_general | solution.py:46
  269.4 6.8 %collective-permute-start.34 = (f32[4,160]{1,0:T(4,128)S(1)}, f32[4,160]{1,0:T(4,128)S(1)}, u32[]{:S(2)}, u32[]{:S(2)}) collective-permute-start(f32[4,160]{1,0:T(4,128)S(1)} %get-tuple-element.131), channel_id=1, source_target_pairs={{16,18},{17,19},{18,16},{19,17},{20,22},{21,23},{22,20},{23,21},{2... | collective-permute-start | bytes 7688 | tf_op jit(solution)/shard_map/ppermute | solution.py:197
  279.2 9.6 %collective-permute-done.34 = f32[4,160]{1,0:T(4,128)S(1)} collective-permute-done((f32[4,160]{1,0:T(4,128)S(1)}, f32[4,160]{1,0:T(4,128)S(1)}, u32[]{:S(2)}, u32[]{:S(2)}) %collective-permute-start.34) | collective-permute-done | bytes 2592 | tf_op jit(solution)/shard_map/ppermute | solution.py:197
  (175 shorter events, 128.4 us)
Async XLA Ops:
  0.0 30.7 %collective-permute-start.8 = (bf16[160,512]{1,0:T(8,128)(2,1)}, bf16[160,512]{1,0:T(8,128)(2,1)S(1)}, u32[]{:S(2)}, u32[]{:S(2)}) collective-permute-start(bf16[160,512]{1,0:T(8,128)(2,1)} %param.8), channel_id=1, source_target_pairs={{0,16},{16,0},{32,48},{48,32},{64,80},{80,64},{96,112},{112,96},{1... | collective-permute-start | bytes 491528 | tf_op jit(solution)/shard_map/ppermute | solution.py:116
  1.8 31.2 %collective-permute-start.9 = (bf16[160,512]{1,0:T(8,128)(2,1)}, bf16[160,512]{1,0:T(8,128)(2,1)S(1)}, u32[]{:S(2)}, u32[]{:S(2)}) collective-permute-start(bf16[160,512]{1,0:T(8,128)(2,1)} %param.8), channel_id=1, source_target_pairs={{0,32},{16,48},{32,0},{48,16},{64,96},{80,112},{96,64},{112,80},{1... | collective-permute-start | bytes 491528 | tf_op jit(solution)/shard_map/ppermute | solution.py:116
  3.4 31.7 %collective-permute-start.10 = (bf16[160,512]{1,0:T(8,128)(2,1)}, bf16[160,512]{1,0:T(8,128)(2,1)S(1)}, u32[]{:S(2)}, u32[]{:S(2)}) collective-permute-start(bf16[160,512]{1,0:T(8,128)(2,1)} %param.8), channel_id=1, source_target_pairs={{0,48},{16,32},{32,16},{48,0},{64,112},{80,96},{96,80},{112,64},{1... | collective-permute-start | bytes 491528 | tf_op jit(solution)/shard_map/ppermute | solution.py:116
  3.8 34.6 %collective-permute-start.11 = (bf16[160,512]{1,0:T(8,128)(2,1)}, bf16[160,512]{1,0:T(8,128)(2,1)S(1)}, u32[]{:S(2)}, u32[]{:S(2)}) collective-permute-start(bf16[160,512]{1,0:T(8,128)(2,1)} %param.8), channel_id=1, source_target_pairs={{0,64},{16,80},{32,96},{48,112},{64,0},{80,16},{96,32},{112,48},{1... | collective-permute-start | bytes 491528 | tf_op jit(solution)/shard_map/ppermute | solution.py:116
  5.3 36.4 %collective-permute-start.12 = (bf16[160,512]{1,0:T(8,128)(2,1)}, bf16[160,512]{1,0:T(8,128)(2,1)S(1)}, u32[]{:S(2)}, u32[]{:S(2)}) collective-permute-start(bf16[160,512]{1,0:T(8,128)(2,1)} %param.8), channel_id=1, source_target_pairs={{0,80},{16,64},{32,112},{48,96},{64,16},{80,0},{96,48},{112,32},{1... | collective-permute-start | bytes 491528 | tf_op jit(solution)/shard_map/ppermute | solution.py:116
  35.1 24.0 %collective-permute-start.15 = (bf16[160,512]{1,0:T(8,128)(2,1)}, bf16[160,512]{1,0:T(8,128)(2,1)S(1)}, u32[]{:S(2)}, u32[]{:S(2)}) collective-permute-start(bf16[160,512]{1,0:T(8,128)(2,1)} %param.8), channel_id=1, source_target_pairs={{0,128},{16,144},{32,160},{48,176},{64,192},{80,208},{96,224},{112... | collective-permute-start | bytes 491528 | tf_op jit(solution)/shard_map/ppermute | solution.py:116
  41.7 23.7 %collective-permute-start.17 = (bf16[160,512]{1,0:T(8,128)(2,1)}, bf16[160,512]{1,0:T(8,128)(2,1)S(1)}, u32[]{:S(2)}, u32[]{:S(2)}) collective-permute-start(bf16[160,512]{1,0:T(8,128)(2,1)} %param.8), channel_id=1, source_target_pairs={{0,160},{16,176},{32,128},{48,144},{64,224},{80,240},{96,192},{112... | collective-permute-start | bytes 491528 | tf_op jit(solution)/shard_map/ppermute | solution.py:116
  45.2 23.1 %collective-permute-start.18 = (bf16[160,512]{1,0:T(8,128)(2,1)}, bf16[160,512]{1,0:T(8,128)(2,1)S(1)}, u32[]{:S(2)}, u32[]{:S(2)}) collective-permute-start(bf16[160,512]{1,0:T(8,128)(2,1)} %param.8), channel_id=1, source_target_pairs={{0,176},{16,160},{32,144},{48,128},{64,240},{80,224},{96,208},{112... | collective-permute-start | bytes 491528 | tf_op jit(solution)/shard_map/ppermute | solution.py:116
  87.0 30.4 %collective-permute-start.26 = (bf16[2,160,640]{2,1,0:T(8,128)(2,1)S(1)}, bf16[2,160,640]{2,1,0:T(8,128)(2,1)S(1)}, u32[]{:S(2)}, u32[]{:S(2)}) collective-permute-start(bf16[2,160,640]{2,1,0:T(8,128)(2,1)S(1)} %pad_maximum_fusion.3), channel_id=1, source_target_pairs={{0,8},{1,9},{2,10},{3,11},{4,12},{5,13},{6,14},{7,15},{8,0},{9,1},... | collective-permute-start | bytes 1228808 | tf_op jit(solution)/shard_map/ppermute | solution.py:140
  90.4 34.8 %collective-permute-start.27 = (bf16[2,160,640]{2,1,0:T(8,128)(2,1)S(1)}, bf16[2,160,640]{2,1,0:T(8,128)(2,1)S(1)}, u32[]{:S(2)}, u32[]{:S(2)}) collective-permute-start(bf16[2,160,640]{2,1,0:T(8,128)(2,1)S(1)} %pad_maximum_fusion.4), channel_id=1, source_target_pairs={{0,9},{1,8},{2,11},{3,10},{4,13},{5,12},{6,15},{7,14},{8,1},{9,0},... | collective-permute-start | bytes 1228808 | tf_op jit(solution)/shard_map/ppermute | solution.py:140
  90.6 34.7 %collective-permute-start.28 = (bf16[2,160,640]{2,1,0:T(8,128)(2,1)S(1)}, bf16[2,160,640]{2,1,0:T(8,128)(2,1)S(1)}, u32[]{:S(2)}, u32[]{:S(2)}) collective-permute-start(bf16[2,160,640]{2,1,0:T(8,128)(2,1)S(1)} %pad_maximum_fusion.5), channel_id=1, source_target_pairs={{0,12},{1,13},{2,14},{3,15},{4,8},{5,9},{6,10},{7,11},{8,4},{9,5},... | collective-permute-start | bytes 1228808 | tf_op jit(solution)/shard_map/ppermute | solution.py:140
  97.3 32.1 %collective-permute-start.29 = (bf16[2,160,640]{2,1,0:T(8,128)(2,1)S(1)}, bf16[2,160,640]{2,1,0:T(8,128)(2,1)S(1)}, u32[]{:S(2)}, u32[]{:S(2)}) collective-permute-start(bf16[2,160,640]{2,1,0:T(8,128)(2,1)S(1)} %pad_maximum_fusion.6), channel_id=1, source_target_pairs={{0,13},{1,12},{2,15},{3,14},{4,9},{5,8},{6,11},{7,10},{8,5},{9,4},... | collective-permute-start | bytes 1228808 | tf_op jit(solution)/shard_map/ppermute | solution.py:140
  129.8 24.1 %collective-permute-start.30 = (f32[160,640]{1,0:T(8,128)S(1)}, f32[160,640]{1,0:T(8,128)S(1)}, u32[]{:S(2)}, u32[]{:S(2)}) collective-permute-start(f32[160,640]{1,0:T(8,128)S(1)} %slice_bitcast_fusion), channel_id=1, source_target_pairs={{0,2},{1,3},{2,0},{3,1},{4,6},{5,7},{6,4},{7,5},{8,10},{9,11},{10,... | collective-permute-start | bytes 1228808 | tf_op jit(solution)/shard_map/ppermute | solution.py:142
  136.1 27.1 %collective-permute-start.1 = (bf16[1024,256]{1,0:T(8,128)(2,1)}, bf16[1024,256]{1,0:T(8,128)(2,1)}, u32[]{:S(2)}, u32[]{:S(2)}) collective-permute-start(bf16[1024,256]{1,0:T(8,128)(2,1)} %get-tuple-element.114), channel_id=1, source_target_pairs={{0,1},{1,0},{2,3},{3,2},{4,5},{5,4},{6,7},{7,6},{8,9},{9,8},{10,11... | collective-permute-start | bytes 1572872 | tf_op jit(solution)/shard_map/ppermute | solution.py:170
  136.2 30.3 %collective-permute-start.2 = (bf16[1024,256]{1,0:T(8,128)(2,1)}, bf16[1024,256]{1,0:T(8,128)(2,1)}, u32[]{:S(2)}, u32[]{:S(2)}) collective-permute-start(bf16[1024,256]{1,0:T(8,128)(2,1)} %get-tuple-element.115), channel_id=1, source_target_pairs={{0,4},{1,5},{2,6},{3,7},{4,0},{5,1},{6,2},{7,3},{8,12},{9,13},{10,... | collective-permute-start | bytes 1572872 | tf_op jit(solution)/shard_map/ppermute | solution.py:170
  136.5 32.8 %collective-permute-start.3 = (bf16[1024,256]{1,0:T(8,128)(2,1)}, bf16[1024,256]{1,0:T(8,128)(2,1)}, u32[]{:S(2)}, u32[]{:S(2)}) collective-permute-start(bf16[1024,256]{1,0:T(8,128)(2,1)} %get-tuple-element.116), channel_id=1, source_target_pairs={{0,5},{1,4},{2,7},{3,6},{4,1},{5,0},{6,3},{7,2},{8,13},{9,12},{10,... | collective-permute-start | bytes 1572872 | tf_op jit(solution)/shard_map/ppermute | solution.py:170
  137.9 38.3 %collective-permute-start.4 = (bf16[1024,256]{1,0:T(8,128)(2,1)S(1)}, bf16[1024,256]{1,0:T(8,128)(2,1)}, u32[]{:S(2)}, u32[]{:S(2)}) collective-permute-start(bf16[1024,256]{1,0:T(8,128)(2,1)S(1)} %get-tuple-element.117), channel_id=1, source_target_pairs={{0,8},{1,9},{2,10},{3,11},{4,12},{5,13},{6,14},{7,15},{8,0},{9,1},... | collective-permute-start | bytes 1572872 | tf_op jit(solution)/shard_map/ppermute | solution.py:170
  160.0 26.4 %collective-permute-start.5 = (bf16[1024,256]{1,0:T(8,128)(2,1)S(1)}, bf16[1024,256]{1,0:T(8,128)(2,1)S(1)}, u32[]{:S(2)}, u32[]{:S(2)}) collective-permute-start(bf16[1024,256]{1,0:T(8,128)(2,1)S(1)} %get-tuple-element.118), channel_id=1, source_target_pairs={{0,9},{1,8},{2,11},{3,10},{4,13},{5,12},{6,15},{7,14},{8,1},{9,0},... | collective-permute-start | bytes 1572872 | tf_op jit(solution)/shard_map/ppermute | solution.py:170
  163.2 34.8 %collective-permute-start.6 = (bf16[1024,256]{1,0:T(8,128)(2,1)}, bf16[1024,256]{1,0:T(8,128)(2,1)S(1)}, u32[]{:S(2)}, u32[]{:S(2)}) collective-permute-start(bf16[1024,256]{1,0:T(8,128)(2,1)} %fusion.52), channel_id=1, source_target_pairs={{0,12},{1,13},{2,14},{3,15},{4,8},{5,9},{6,10},{7,11},{8,4},{9,5},... | collective-permute-start | bytes 1572872 | tf_op jit(solution)/shard_map/ppermute | solution.py:170
  166.5 42.8 %collective-permute-start.7 = (bf16[1024,256]{1,0:T(8,128)(2,1)S(1)}, bf16[1024,256]{1,0:T(8,128)(2,1)S(1)}, u32[]{:S(2)}, u32[]{:S(2)}) collective-permute-start(bf16[1024,256]{1,0:T(8,128)(2,1)S(1)} %get-tuple-element.113), channel_id=1, source_target_pairs={{0,13},{1,12},{2,15},{3,14},{4,9},{5,8},{6,11},{7,10},{8,5},{9,4},... | collective-permute-start | bytes 1572872 | tf_op jit(solution)/shard_map/ppermute | solution.py:170
  169.3 41.7 %collective-permute-start.31 = (bf16[160,4,128]{2,0,1:T(8,128)(2,1)S(1)}, bf16[160,4,128]{2,0,1:T(8,128)(2,1)S(1)}, u32[]{:S(2)}, u32[]{:S(2)}) collective-permute-start(bf16[160,4,128]{2,0,1:T(8,128)(2,1)S(1)} %pad_maximum_fusion.8), channel_id=1, source_target_pairs={{0,18},{1,19},{2,16},{3,17},{4,22},{5,23},{6,20},{7,21},{8,26},{9,... | collective-permute-start | bytes 491528 | tf_op jit(solution)/shard_map/ppermute | solution.py:179
  176.3 34.7 %collective-permute-start.32 = (bf16[160,4,128]{2,0,1:T(8,128)(2,1)S(1)}, bf16[160,4,128]{2,0,1:T(8,128)(2,1)S(1)}, u32[]{:S(2)}, u32[]{:S(2)}) collective-permute-start(bf16[160,4,128]{2,0,1:T(8,128)(2,1)S(1)} %pad_maximum_fusion.8), channel_id=1, source_target_pairs={{16,18},{17,19},{18,16},{19,17},{20,22},{21,23},{22,20},{23,21},{2... | collective-permute-start | bytes 491528 | tf_op jit(solution)/shard_map/ppermute | solution.py:180
  266.3 26.2 %collective-permute-start.33 = (f32[4,160,128]{2,1,0:T(8,128)S(1)}, f32[4,160,128]{2,1,0:T(8,128)S(1)}, u32[]{:S(2)}, u32[]{:S(2)}) collective-permute-start(f32[4,160,128]{2,1,0:T(8,128)S(1)} %get-tuple-element.123), channel_id=1, source_target_pairs={{16,18},{17,19},{18,16},{19,17},{20,22},{21,23},{22,20},{23,21},{2... | collective-permute-start | bytes 983048 | tf_op jit(solution)/shard_map/ppermute | solution.py:197
  269.3 23.2 %collective-permute-start.37 = (f32[4,160,128]{2,1,0:T(8,128)S(1)}, f32[4,160,128]{2,1,0:T(8,128)S(1)}, u32[]{:S(2)}, u32[]{:S(2)}) collective-permute-start(f32[4,160,128]{2,1,0:T(8,128)S(1)} %get-tuple-element.124), channel_id=1, source_target_pairs={{0,16},{1,17},{2,18},{3,19},{4,20},{5,21},{6,22},{7,23},{8,24},{9,... | collective-permute-start | bytes 983048 | tf_op jit(solution)/shard_map/ppermute | solution.py:196
  (30 other events, 709.6 us)

commit v3 on v2

--- a/solution.py
+++ b/solution.py
@@ -102,6 +102,19 @@
     return (top, total, accum)
 
 
+def pack_state(state):
+    top, total, accum = state
+    stats = jnp.stack([top, total]).reshape(-1, HD)
+    return jnp.concatenate([accum.reshape(-1, HD), stats], axis=0)
+
+
+def unpack_state(packed, heads):
+    rows = heads * SUF
+    accum = packed[:rows].reshape(heads, SUF, HD)
+    stats = packed[rows:].reshape(2, heads, SUF)
+    return (stats[0], stats[1], accum)
+
+
 def per_device(hidden, w_query, w_keyval, prefix_cache, suffix_lengths, group_ids):
     n_row = lax.axis_size("row")
     n_col = lax.axis_size("col")
@@ -111,12 +124,24 @@
     segments = w_keyval.shape[1] // HD
     scale = 1.0 / HD**0.5
     half_bit = 2
-    stacked = [hidden]
-    for mask in range(1, n_row):
-        stacked.append(lax.ppermute(hidden, "row", [(i, i ^ mask) for i in range(n_row)]))
-    stacked = jnp.stack(stacked)
-    order = row_id ^ jnp.arange(n_row, dtype=jnp.int32)
-    gathered = jnp.take(stacked, order, axis=0).reshape(-1, hidden.shape[1])
+    gathered = lax.all_gather(hidden, "row", axis=0, tiled=True)
+    odd = row_id % 2
+    is_even = odd == 0
+    handled = col_id ^ (half_bit * odd)
+    other_cache = partner(prefix_cache, "row", 0)
+    cache_keys = jnp.where(is_even, prefix_cache, other_cache)
+    cache_values = jnp.where(is_even, other_cache, prefix_cache)
+    kv_block = jnp.concatenate([cache_keys, cache_values], axis=-1)
+
+    masks = [m for m in range(1, n_col) if m & half_bit == 0]
+    blocks = [lax.dynamic_index_in_dim(kv_block, group_ids[handled], 0, keepdims=False)]
+    for mask in masks:
+        peer_group = group_ids[(col_id ^ mask) ^ (half_bit * odd)]
+        piece = lax.dynamic_index_in_dim(kv_block, peer_group, 0, keepdims=False)
+        pairs = [(c, c ^ mask) for c in range(n_col)]
+        blocks.append(lax.ppermute(piece, "col", pairs))
+    half_kv = jnp.concatenate(blocks, axis=0)
+    gathered, half_kv = lax.optimization_barrier((gathered, half_kv))
     weights_all = jnp.concatenate([w_query, w_keyval], axis=1)
     tok_block = gathered.shape[0] // n_col
     partial = jnp.dot(gathered, weights_all, preferred_element_type=jnp.float32)
@@ -151,24 +176,9 @@
     keyval = jnp.where(is_key[None, :, None], rotate(keyval, cosine, sine), keyval).astype(
         jnp.bfloat16
     )
-    odd = row_id % 2
-    is_even = odd == 0
-    other_keyval, other_cache = partner((keyval, prefix_cache), "row", 0)
+    other_keyval = partner(keyval, "row", 0)
     suffix_keys = jnp.where(is_even, keyval[:, 0], other_keyval[:, 0])
     suffix_values = jnp.where(is_even, other_keyval[:, 0], keyval[:, 0])
-    cache_keys = jnp.where(is_even, prefix_cache, other_cache)
-    cache_values = jnp.where(is_even, other_cache, prefix_cache)
-    kv_block = jnp.concatenate([cache_keys, cache_values], axis=-1)
-
-    handled = col_id ^ (half_bit * odd)
-    masks = [m for m in range(1, n_col) if m & half_bit == 0]
-    blocks = [lax.dynamic_index_in_dim(kv_block, group_ids[handled], 0, keepdims=False)]
-    for mask in masks:
-        peer_group = group_ids[(col_id ^ mask) ^ (half_bit * odd)]
-        piece = lax.dynamic_index_in_dim(kv_block, peer_group, 0, keepdims=False)
-        pairs = [(c, c ^ mask) for c in range(n_col)]
-        blocks.append(lax.ppermute(piece, "col", pairs))
-    half_kv = jnp.concatenate(blocks, axis=0)
     half_keys = half_kv[:, :HD]
     half_values = half_kv[:, HD:]
 
@@ -193,8 +203,8 @@
         jax.tree.map(lambda x: x[heads_here:], half_state),
         jax.tree.map(lambda x: x[:heads_here], half_state),
     )
-    from_cross = lax.ppermute(theirs, axes, back)
-    from_same = lax.ppermute(mine, axes, same)
+    from_cross = unpack_state(lax.ppermute(pack_state(theirs), axes, back), heads_here)
+    from_same = unpack_state(lax.ppermute(pack_state(mine), axes, same), heads_here)
     first_state = jax.tree.map(lambda a, b: jnp.where(is_even, a, b), mine, from_same)
 
     length = suffix_lengths[col_id]

time: 296 us -> 251 us (0.85)
  starting transfers between devices: 69.5 us -> 33.6 us
  local copies, waits for them, and re-layouts: 40.9 us -> 23.1 us
  matrix products: 38.7 us -> 25.2 us
  between operations: 15.9 us -> 28.6 us
  waiting for transfers between devices: 111 us -> 116 us
  other arithmetic: 18.5 us -> 23.4 us
    ppermute x21 -> x2, starting transfers between devices: 41.6 us -> 4.17 us  [the longest x1 4.09 us: per_device(): lax.ppermute(pack_state(mine), axes, same)]
    ppermute x21 -> x2, waiting for transfers between devices: 28.6 us -> 10.1 us  [the longest x1 10.1 us: per_device(): lax.ppermute(pack_state(mine), axes, same)]
    while x8 -> x0, local copies, waits for them, and re-layouts: 16.1 us -> none
    dot_general x4, matrix products: 20.5 us -> 8.05 us  [block_stats(): jnp.einsum('htk,kd->htd', weights.astype(jnp.bfloat16), values, preferred...]
    all_gather x0 -> x1, waiting for transfers between devices: none -> 11.1 us  [per_device(): gathered = lax.all_gather(hidden, 'row', axis=0, tiled=True)]
    ppermute x1, waiting for transfers between devices: 0.01 us -> 7.16 us  [per_device(): q_same = lax.ppermute(query, axes, same)]
    ppermute x2, starting transfers between devices: 0.32 us -> 6.24 us  [partner(): return lax.ppermute(value, axis, pairs)]
    unnamed x41 -> x16, local copies, waits for them, and re-layouts: 15.5 us -> 10.7 us
  transfers between devices with their start and end apart: 40 -> 22, of which waited for: 17 -> 15; matrix products, arithmetic and copies ran while one was open for 14% -> 13% of each run, Pallas kernels for 0% -> 0%
where the time goes in v3:
time: 251 us; the launch traced here: 250 us
  waiting for transfers between devices  116 us (46%)
  starting transfers between devices  33.6 us (13%)
  between operations  28.6 us (11%)
  matrix products  25.2 us (10%)
  other arithmetic  23.4 us (9%)
  local copies, waits for them, and re-layouts  23.1 us (9%)
    ppermute x7, waiting for transfers between devices, per_device(): blocks.append(lax.ppermute(piece, 'col', pairs))  38.6 us
    ppermute x7, waiting for transfers between devices, per_device(): got = lax.ppermute(piece, 'col', [(c, c ^ mask) for c in range(n_col)])  31.9 us
    ppermute x1, waiting for transfers between devices, per_device(): lax.ppermute(half_sum[1], 'col', [(c, c ^ half_bit) for c in range(n_col)])  14 us
    all_gather x1, waiting for transfers between devices, per_device(): gathered = lax.all_gather(hidden, 'row', axis=0, tiled=True)  11.1 us
    unnamed x16, local copies, waits for them, and re-layouts  10.7 us
    dot_general x4, matrix products, block_stats(): jnp.einsum('thd,kd->htk', req_query, keys, preferred_element_type=jnp.flo...  10.7 us
    ppermute x1, waiting for transfers between devices, per_device(): lax.ppermute(pack_state(mine), axes, same)  10.1 us
    dot_general x4, matrix products, block_stats(): jnp.einsum('htk,kd->htd', weights.astype(jnp.bfloat16), values, preferred...  8.05 us
  transfers between devices with their start and end apart: 22, of which 15 were waited for; matrix products, arithmetic and copies ran while one was open for 13% of the time, Pallas kernels for 0%

profile of v3, /device:TPU:32, one launch (start us, length us, event | category | flops | bytes accessed | tf_op | source)
XLA Modules:
  0.0 249.8 jit_solution(1691048183763502390)
XLA Ops:
  44.4 7.7 %collective-permute-done.3 = bf16[1024,256]{1,0:T(8,128)(2,1)} collective-permute-done((bf16[1024,256]{1,0:T(8,128)(2,1)S(1)}, bf16[1024,256]{1,0:T(8,128)(2,1)}, u32[]{:S(2)}, u32[]{:S(2)}) %collective-permute-start.3) | collective-permute-done | bytes 524320 | tf_op jit(solution)/shard_map/ppermute | solution.py:142
  54.1 11.0 %collective-permute-done.4 = bf16[1024,256]{1,0:T(8,128)(2,1)S(1)} collective-permute-done((bf16[1024,256]{1,0:T(8,128)(2,1)S(1)}, bf16[1024,256]{1,0:T(8,128)(2,1)S(1)}, u32[]{:S(2)}, u32[]{:S(2)}) %collective-permute-start.4) | collective-permute-done | bytes 524320 | tf_op jit(solution)/shard_map/ppermute | solution.py:142
  65.9 9.5 %collective-permute-done.5 = bf16[1024,256]{1,0:T(8,128)(2,1)S(1)} collective-permute-done((bf16[1024,256]{1,0:T(8,128)(2,1)S(1)}, bf16[1024,256]{1,0:T(8,128)(2,1)S(1)}, u32[]{:S(2)}, u32[]{:S(2)}) %collective-permute-start.5) | collective-permute-done | bytes 524320 | tf_op jit(solution)/shard_map/ppermute | solution.py:142
  77.0 9.3 %collective-permute-done.7 = bf16[1024,256]{1,0:T(8,128)(2,1)S(1)} collective-permute-done((bf16[1024,256]{1,0:T(8,128)(2,1)S(1)}, bf16[1024,256]{1,0:T(8,128)(2,1)S(1)}, u32[]{:S(2)}, u32[]{:S(2)}) %collective-permute-start.7) | collective-permute-done | bytes 524320 | tf_op jit(solution)/shard_map/ppermute | solution.py:142
  87.2 11.1 %all-gather.2.cloned.1.call-done = bf16[2560,512]{1,0:T(8,128)(2,1)} async-done(((bf16[160,512]{1,0:T(8,128)(2,1)}), bf16[2560,512]{1,0:T(8,128)(2,1)}) %all-gather.2.cloned.1.call-update) | async-done | bytes 2621456 | tf_op jit(solution)/shard_map/all_gather | solution.py:127
  98.2 4.0 %fusion.28 = f32[2560,640]{1,0:T(8,128)S(1)} fusion(bf16[2560,512]{1,0:T(8,128)(2,1)} %all-gather.2.cloned.1.call-done, bf16[512,128]{1,0:T(8,128)(2,1)S(1)} %copy-done.4, bf16[512,512]{1,0:T(8,128)(2,1)} %param.9), kind=kOutput, calls=%fused_computation.49 | convolution fusion | flops 1679032320 | bytes 9830400 | tf_op jit(solution)/shard_map/dot_general | solution.py:147
  108.1 2.7 %collective-permute-start.11 = (bf16[2,160,640]{2,1,0:T(8,128)(2,1)}, bf16[2,160,640]{2,1,0:T(8,128)(2,1)S(1)}, u32[]{:S(2)}, u32[]{:S(2)}) collective-permute-start(bf16[2,160,640]{2,1,0:T(8,128)(2,1)} %pad_maximum_fusion.3), channel_id=1, source_target_pairs={{0,8},{1,9},{2,10},{3,11},{4,12},{5,13},{6,14},{7,15},{8,0},{9,1},... | collective-permute-start | bytes 1228808 | tf_op jit(solution)/shard_map/ppermute | solution.py:165
  113.1 2.8 %collective-permute-start.13 = (bf16[2,160,640]{2,1,0:T(8,128)(2,1)}, bf16[2,160,640]{2,1,0:T(8,128)(2,1)S(1)}, u32[]{:S(2)}, u32[]{:S(2)}) collective-permute-start(bf16[2,160,640]{2,1,0:T(8,128)(2,1)} %pad_maximum_fusion.5), channel_id=1, source_target_pairs={{0,12},{1,13},{2,14},{3,15},{4,8},{5,9},{6,10},{7,11},{8,4},{9,5},... | collective-permute-start | bytes 1228808 | tf_op jit(solution)/shard_map/ppermute | solution.py:165
  117.6 8.2 %collective-permute-done.10 = bf16[2,160,640]{2,1,0:T(8,128)(2,1)S(1)} collective-permute-done((bf16[2,160,640]{2,1,0:T(8,128)(2,1)S(1)}, bf16[2,160,640]{2,1,0:T(8,128)(2,1)S(1)}, u32[]{:S(2)}, u32[]{:S(2)}) %collective-permute-start.10) | collective-permute-done | bytes 409632 | tf_op jit(solution)/shard_map/ppermute | solution.py:165
  128.0 9.7 %collective-permute-done.11 = bf16[2,160,640]{2,1,0:T(8,128)(2,1)S(1)} collective-permute-done((bf16[2,160,640]{2,1,0:T(8,128)(2,1)}, bf16[2,160,640]{2,1,0:T(8,128)(2,1)S(1)}, u32[]{:S(2)}, u32[]{:S(2)}) %collective-permute-start.11) | collective-permute-done | bytes 409632 | tf_op jit(solution)/shard_map/ppermute | solution.py:165
  139.1 5.4 %collective-permute-done.13 = bf16[2,160,640]{2,1,0:T(8,128)(2,1)S(1)} collective-permute-done((bf16[2,160,640]{2,1,0:T(8,128)(2,1)}, bf16[2,160,640]{2,1,0:T(8,128)(2,1)S(1)}, u32[]{:S(2)}, u32[]{:S(2)}) %collective-permute-start.13) | collective-permute-done | bytes 409632 | tf_op jit(solution)/shard_map/ppermute | solution.py:165
  144.4 7.3 %collective-permute-done.14 = bf16[2,160,640]{2,1,0:T(8,128)(2,1)S(1)} collective-permute-done((bf16[2,160,640]{2,1,0:T(8,128)(2,1)}, bf16[2,160,640]{2,1,0:T(8,128)(2,1)S(1)}, u32[]{:S(2)}, u32[]{:S(2)}) %collective-permute-start.14) | collective-permute-done | bytes 409632 | tf_op jit(solution)/shard_map/ppermute | solution.py:165
  152.2 4.1 %collective-permute-start.15 = (f32[160,640]{1,0:T(8,128)S(1)}, f32[160,640]{1,0:T(8,128)S(1)}, u32[]{:S(2)}, u32[]{:S(2)}) collective-permute-start(f32[160,640]{1,0:T(8,128)S(1)} %slice_bitcast_fusion), channel_id=1, source_target_pairs={{0,2},{1,3},{2,0},{3,1},{4,6},{5,7},{6,4},{7,5},{8,10},{9,11},{10,... | collective-permute-start | bytes 1228808 | tf_op jit(solution)/shard_map/ppermute | solution.py:167
  156.3 3.8 %fusion.77 = (bf16[8192,128]{1,0:T(8,128)(2,1)S(1)}, bf16[8192,128]{1,0:T(8,128)(2,1)}) fusion(bf16[8192,256]{1,0:T(8,128)(2,1)} %constant_dynamic-update-slice_fusion), kind=kLoop, calls=%fused_computation.164 | loop fusion | bytes 8388608 | tf_op jit(solution)/shard_map/slice | solution.py:183
  160.1 14.0 %collective-permute-done.15 = f32[160,640]{1,0:T(8,128)S(1)} collective-permute-done((f32[160,640]{1,0:T(8,128)S(1)}, f32[160,640]{1,0:T(8,128)S(1)}, u32[]{:S(2)}, u32[]{:S(2)}) %collective-permute-start.15) | collective-permute-done | bytes 409632 | tf_op jit(solution)/shard_map/ppermute | solution.py:167
  178.0 4.3 %collective-permute-start.20 = (bf16[160,1,128]{2,0,1:T(8,128)(2,1)S(1)}, bf16[160,1,128]{2,0,1:T(8,128)(2,1)S(1)}, u32[]{:S(2)}, u32[]{:S(2)}) collective-permute-start(bf16[160,1,128]{2,0,1:T(8,128)(2,1)S(1)} %bitcast.133), channel_id=1, source_target_pairs={{0,16},{16,0},{32,48},{48,32},{64,80},{80,64},{96,112},{112,96},{1... | collective-permute-start | bytes 122888 | tf_op jit(solution)/shard_map/ppermute | solution.py:14
  183.7 3.7 %collective-permute-start.17 = (bf16[160,4,128]{2,0,1:T(8,128)(2,1)S(1)}, bf16[160,4,128]{2,0,1:T(8,128)(2,1)S(1)}, u32[]{:S(2)}, u32[]{:S(2)}) collective-permute-start(bf16[160,4,128]{2,0,1:T(8,128)(2,1)S(1)} %pad_maximum_fusion.10), channel_id=1, source_target_pairs={{16,18},{17,19},{18,16},{19,17},{20,22},{21,23},{22,20},{23,21},{2... | collective-permute-start | bytes 491528 | tf_op jit(solution)/shard_map/ppermute | solution.py:190
  189.4 7.2 %collective-permute-done.17 = bf16[160,4,128]{2,0,1:T(8,128)(2,1)S(1)} collective-permute-done((bf16[160,4,128]{2,0,1:T(8,128)(2,1)S(1)}, bf16[160,4,128]{2,0,1:T(8,128)(2,1)S(1)}, u32[]{:S(2)}, u32[]{:S(2)}) %collective-permute-start.17) | collective-permute-done | bytes 163872 | tf_op jit(solution)/shard_map/ppermute | solution.py:190
  198.9 26.4 %while.15 = (s32[]{:T(128)}, f32[8,160]{1,0:T(8,128)S(1)}, f32[8,160]{1,0:T(8,128)S(1)}, f32[8,160,128]{2,1,0:T(8,128)S(1)}, bf16[4,2048,128]{2,1,0:T(8,128)(2,1...) while((s32[]{:T(128)}, f32[8,160]{1,0:T(8,128)S(1)}, ...), condition=%wide.region_3.4_spmd.clone, body=%wide.region_0.3_spmd.clone.sunk | while | flops 1363811840 | bytes 34225268 | solution.py:78
  198.9 2.7 %bitcast_reduce_fusion.2 = (f32[8,160]{1,0:T(8,128)S(1)}, f32[2048,160,8]{0,1,2:T(8,128)S(1)}) fusion(bf16[160,8,128]{2,0,1:T(8,128)(2,1)S(1)} %get-tuple-element.235, bf16[4,2048,128]{2,1,0:T(8,128)(2,1)} %get-tuple-element.234, s32[]{:T(128)S(6)} %copy.33), kind=kOutput, calls=%fused_computation.1.clone.1 | convolution fusion | flops 676330240 | bytes 11342852 | tf_op jit(solution)/shard_map/while/body/eval_jaxpr/thd,kd->htk/dot_general | solution.py:42
  205.6 2.7 %bitcast_reduce_fusion.2 = (f32[8,160]{1,0:T(8,128)S(1)}, f32[2048,160,8]{0,1,2:T(8,128)S(1)}) fusion(bf16[160,8,128]{2,0,1:T(8,128)(2,1)S(1)} %get-tuple-element.235, bf16[4,2048,128]{2,1,0:T(8,128)(2,1)} %get-tuple-element.234, s32[]{:T(128)S(6)} %copy.33), kind=kOutput, calls=%fused_computation.1.clone.1 | convolution fusion | flops 676330240 | bytes 11342852 | tf_op jit(solution)/shard_map/while/body/eval_jaxpr/thd,kd->htk/dot_general | solution.py:42
  212.2 2.7 %bitcast_reduce_fusion.2 = (f32[8,160]{1,0:T(8,128)S(1)}, f32[2048,160,8]{0,1,2:T(8,128)S(1)}) fusion(bf16[160,8,128]{2,0,1:T(8,128)(2,1)S(1)} %get-tuple-element.235, bf16[4,2048,128]{2,1,0:T(8,128)(2,1)} %get-tuple-element.234, s32[]{:T(128)S(6)} %copy.33), kind=kOutput, calls=%fused_computation.1.clone.1 | convolution fusion | flops 676330240 | bytes 11342852 | tf_op jit(solution)/shard_map/while/body/eval_jaxpr/thd,kd->htk/dot_general | solution.py:42
  225.6 4.1 %collective-permute-start.18 = (f32[650,128]{1,0:T(8,128)S(1)}, f32[650,128]{1,0:T(8,128)S(1)}, u32[]{:S(2)}, u32[]{:S(2)}) collective-permute-start(f32[650,128]{1,0:T(8,128)S(1)} %pad_maximum_fusion.7), channel_id=1, source_target_pairs={{16,18},{17,19},{18,16},{19,17},{20,22},{21,23},{22,20},{23,21},{2... | collective-permute-start | bytes 998408 | tf_op jit(solution)/shard_map/ppermute | solution.py:207
  231.1 10.1 %collective-permute-done.18 = f32[650,128]{1,0:T(8,128)S(1)} collective-permute-done((f32[650,128]{1,0:T(8,128)S(1)}, f32[650,128]{1,0:T(8,128)S(1)}, u32[]{:S(2)}, u32[]{:S(2)}) %collective-permute-start.18) | collective-permute-done | bytes 332832 | tf_op jit(solution)/shard_map/ppermute | solution.py:207
  (116 shorter events, 73.1 us)
Async XLA Ops:
  6.5 91.7 %all-gather.2.cloned.1.call-start = ((), (), s32[]{:S(2)}) async-start(), calls=%async_computation | async-start | bytes 2785280 | tf_op jit(solution)/shard_map/all_gather | solution.py:127
  7.3 16.3 %collective-permute-start = (bf16[2,1024,128]{2,1,0:T(8,128)(2,1)}, bf16[2,1024,128]{2,1,0:T(8,128)(2,1)S(1)}, u32[]{:S(2)}, u32[]{:S(2)}) collective-permute-start(bf16[2,1024,128]{2,1,0:T(8,128)(2,1)} %param.11), channel_id=1, source_target_pairs={{0,16},{16,0},{32,48},{48,32},{64,80},{80,64},{96,112},{112,96},{1... | collective-permute-start | bytes 1572872 | tf_op jit(solution)/shard_map/ppermute | solution.py:14
  26.0 11.5 %collective-permute-start.1 = (bf16[1024,256]{1,0:T(8,128)(2,1)}, bf16[1024,256]{1,0:T(8,128)(2,1)}, u32[]{:S(2)}, u32[]{:S(2)}) collective-permute-start(bf16[1024,256]{1,0:T(8,128)(2,1)} %get-tuple-element.118), channel_id=1, source_target_pairs={{0,1},{1,0},{2,3},{3,2},{4,5},{5,4},{6,7},{7,6},{8,9},{9,8},{10,11... | collective-permute-start | bytes 1572872 | tf_op jit(solution)/shard_map/ppermute | solution.py:142
  26.7 15.1 %collective-permute-start.2 = (bf16[1024,256]{1,0:T(8,128)(2,1)}, bf16[1024,256]{1,0:T(8,128)(2,1)}, u32[]{:S(2)}, u32[]{:S(2)}) collective-permute-start(bf16[1024,256]{1,0:T(8,128)(2,1)} %get-tuple-element.119), channel_id=1, source_target_pairs={{0,4},{1,5},{2,6},{3,7},{4,0},{5,1},{6,2},{7,3},{8,12},{9,13},{10,... | collective-permute-start | bytes 1572872 | tf_op jit(solution)/shard_map/ppermute | solution.py:142
  27.4 24.8 %collective-permute-start.3 = (bf16[1024,256]{1,0:T(8,128)(2,1)S(1)}, bf16[1024,256]{1,0:T(8,128)(2,1)}, u32[]{:S(2)}, u32[]{:S(2)}) collective-permute-start(bf16[1024,256]{1,0:T(8,128)(2,1)S(1)} %get-tuple-element.120), channel_id=1, source_target_pairs={{0,5},{1,4},{2,7},{3,6},{4,1},{5,0},{6,3},{7,2},{8,13},{9,12},{10,... | collective-permute-start | bytes 1572872 | tf_op jit(solution)/shard_map/ppermute | solution.py:142
  33.3 31.8 %collective-permute-start.4 = (bf16[1024,256]{1,0:T(8,128)(2,1)S(1)}, bf16[1024,256]{1,0:T(8,128)(2,1)S(1)}, u32[]{:S(2)}, u32[]{:S(2)}) collective-permute-start(bf16[1024,256]{1,0:T(8,128)(2,1)S(1)} %get-tuple-element.121), channel_id=1, source_target_pairs={{0,8},{1,9},{2,10},{3,11},{4,12},{5,13},{6,14},{7,15},{8,0},{9,1},... | collective-permute-start | bytes 1572872 | tf_op jit(solution)/shard_map/ppermute | solution.py:142
  34.9 63.3 %copy-start.4 = (bf16[512,128]{1,0:T(8,128)(2,1)S(1)}, bf16[512,128]{1,0:T(8,128)(2,1)}, u32[]{:S(2)}) copy-start(bf16[512,128]{1,0:T(8,128)(2,1)} %param.10) | copy-start | bytes 393220
  34.9 40.4 %collective-permute-start.5 = (bf16[1024,256]{1,0:T(8,128)(2,1)S(1)}, bf16[1024,256]{1,0:T(8,128)(2,1)S(1)}, u32[]{:S(2)}, u32[]{:S(2)}) collective-permute-start(bf16[1024,256]{1,0:T(8,128)(2,1)S(1)} %get-tuple-element.122), channel_id=1, source_target_pairs={{0,9},{1,8},{2,11},{3,10},{4,13},{5,12},{6,15},{7,14},{8,1},{9,0},... | collective-permute-start | bytes 1572872 | tf_op jit(solution)/shard_map/ppermute | solution.py:142
  37.5 38.6 %collective-permute-start.6 = (bf16[1024,256]{1,0:T(8,128)(2,1)S(1)}, bf16[1024,256]{1,0:T(8,128)(2,1)S(1)}, u32[]{:S(2)}, u32[]{:S(2)}) collective-permute-start(bf16[1024,256]{1,0:T(8,128)(2,1)S(1)} %fusion.50), channel_id=1, source_target_pairs={{0,12},{1,13},{2,14},{3,15},{4,8},{5,9},{6,10},{7,11},{8,4},{9,5},... | collective-permute-start | bytes 1572872 | tf_op jit(solution)/shard_map/ppermute | solution.py:142
  41.8 44.5 %collective-permute-start.7 = (bf16[1024,256]{1,0:T(8,128)(2,1)S(1)}, bf16[1024,256]{1,0:T(8,128)(2,1)S(1)}, u32[]{:S(2)}, u32[]{:S(2)}) collective-permute-start(bf16[1024,256]{1,0:T(8,128)(2,1)S(1)} %get-tuple-element.117), channel_id=1, source_target_pairs={{0,13},{1,12},{2,15},{3,14},{4,9},{5,8},{6,11},{7,10},{8,5},{9,4},... | collective-permute-start | bytes 1572872 | tf_op jit(solution)/shard_map/ppermute | solution.py:142
  105.4 12.1 %collective-permute-start.9 = (bf16[2,160,640]{2,1,0:T(8,128)(2,1)S(1)}, bf16[2,160,640]{2,1,0:T(8,128)(2,1)S(1)}, u32[]{:S(2)}, u32[]{:S(2)}) collective-permute-start(bf16[2,160,640]{2,1,0:T(8,128)(2,1)S(1)} %pad_maximum_fusion.1), channel_id=1, source_target_pairs={{0,4},{1,5},{2,6},{3,7},{4,0},{5,1},{6,2},{7,3},{8,12},{9,13},{10,... | collective-permute-start | bytes 1228808 | tf_op jit(solution)/shard_map/ppermute | solution.py:165
  107.1 18.6 %collective-permute-start.10 = (bf16[2,160,640]{2,1,0:T(8,128)(2,1)S(1)}, bf16[2,160,640]{2,1,0:T(8,128)(2,1)S(1)}, u32[]{:S(2)}, u32[]{:S(2)}) collective-permute-start(bf16[2,160,640]{2,1,0:T(8,128)(2,1)S(1)} %pad_maximum_fusion.2), channel_id=1, source_target_pairs={{0,5},{1,4},{2,7},{3,6},{4,1},{5,0},{6,3},{7,2},{8,13},{9,12},{10,... | collective-permute-start | bytes 1228808 | tf_op jit(solution)/shard_map/ppermute | solution.py:165
  108.1 29.6 %collective-permute-start.11 = (bf16[2,160,640]{2,1,0:T(8,128)(2,1)}, bf16[2,160,640]{2,1,0:T(8,128)(2,1)S(1)}, u32[]{:S(2)}, u32[]{:S(2)}) collective-permute-start(bf16[2,160,640]{2,1,0:T(8,128)(2,1)} %pad_maximum_fusion.3), channel_id=1, source_target_pairs={{0,8},{1,9},{2,10},{3,11},{4,12},{5,13},{6,14},{7,15},{8,0},{9,1},... | collective-permute-start | bytes 1228808 | tf_op jit(solution)/shard_map/ppermute | solution.py:165
  111.6 27.4 %collective-permute-start.12 = (bf16[2,160,640]{2,1,0:T(8,128)(2,1)}, bf16[2,160,640]{2,1,0:T(8,128)(2,1)S(1)}, u32[]{:S(2)}, u32[]{:S(2)}) collective-permute-start(bf16[2,160,640]{2,1,0:T(8,128)(2,1)} %pad_maximum_fusion.4), channel_id=1, source_target_pairs={{0,9},{1,8},{2,11},{3,10},{4,13},{5,12},{6,15},{7,14},{8,1},{9,0},... | collective-permute-start | bytes 1228808 | tf_op jit(solution)/shard_map/ppermute | solution.py:165
  113.1 31.3 %collective-permute-start.13 = (bf16[2,160,640]{2,1,0:T(8,128)(2,1)}, bf16[2,160,640]{2,1,0:T(8,128)(2,1)S(1)}, u32[]{:S(2)}, u32[]{:S(2)}) collective-permute-start(bf16[2,160,640]{2,1,0:T(8,128)(2,1)} %pad_maximum_fusion.5), channel_id=1, source_target_pairs={{0,12},{1,13},{2,14},{3,15},{4,8},{5,9},{6,10},{7,11},{8,4},{9,5},... | collective-permute-start | bytes 1228808 | tf_op jit(solution)/shard_map/ppermute | solution.py:165
  117.6 34.2 %collective-permute-start.14 = (bf16[2,160,640]{2,1,0:T(8,128)(2,1)}, bf16[2,160,640]{2,1,0:T(8,128)(2,1)S(1)}, u32[]{:S(2)}, u32[]{:S(2)}) collective-permute-start(bf16[2,160,640]{2,1,0:T(8,128)(2,1)} %pad_maximum_fusion.6), channel_id=1, source_target_pairs={{0,13},{1,12},{2,15},{3,14},{4,9},{5,8},{6,11},{7,10},{8,5},{9,4},... | collective-permute-start | bytes 1228808 | tf_op jit(solution)/shard_map/ppermute | solution.py:165
  125.7 26.0 %collective-permute-start.8 = (bf16[2,160,640]{2,1,0:T(8,128)(2,1)}, bf16[2,160,640]{2,1,0:T(8,128)(2,1)S(1)}, u32[]{:S(2)}, u32[]{:S(2)}) collective-permute-start(bf16[2,160,640]{2,1,0:T(8,128)(2,1)} %pad_maximum_fusion), channel_id=1, source_target_pairs={{0,1},{1,0},{2,3},{3,2},{4,5},{5,4},{6,7},{7,6},{8,9},{9,8},{10,11... | collective-permute-start | bytes 1228808 | tf_op jit(solution)/shard_map/ppermute | solution.py:165
  152.2 22.0 %collective-permute-start.15 = (f32[160,640]{1,0:T(8,128)S(1)}, f32[160,640]{1,0:T(8,128)S(1)}, u32[]{:S(2)}, u32[]{:S(2)}) collective-permute-start(f32[160,640]{1,0:T(8,128)S(1)} %slice_bitcast_fusion), channel_id=1, source_target_pairs={{0,2},{1,3},{2,0},{3,1},{4,6},{5,7},{6,4},{7,5},{8,10},{9,11},{10,... | collective-permute-start | bytes 1228808 | tf_op jit(solution)/shard_map/ppermute | solution.py:167
  178.0 21.0 %copy-start.2 = (bf16[160,128]{1,0:T(8,128)(2,1)}, bf16[160,128]{1,0:T(8,128)(2,1)S(1)}, u32[]{:S(2)}) copy-start(bf16[160,128]{1,0:T(8,128)(2,1)S(1)} %fusion.68) | copy-start | bytes 122884
  178.0 9.5 %collective-permute-start.20 = (bf16[160,1,128]{2,0,1:T(8,128)(2,1)S(1)}, bf16[160,1,128]{2,0,1:T(8,128)(2,1)S(1)}, u32[]{:S(2)}, u32[]{:S(2)}) collective-permute-start(bf16[160,1,128]{2,0,1:T(8,128)(2,1)S(1)} %bitcast.133), channel_id=1, source_target_pairs={{0,16},{16,0},{32,48},{48,32},{64,80},{80,64},{96,112},{112,96},{1... | collective-permute-start | bytes 122888 | tf_op jit(solution)/shard_map/ppermute | solution.py:14
  183.7 12.9 %collective-permute-start.17 = (bf16[160,4,128]{2,0,1:T(8,128)(2,1)S(1)}, bf16[160,4,128]{2,0,1:T(8,128)(2,1)S(1)}, u32[]{:S(2)}, u32[]{:S(2)}) collective-permute-start(bf16[160,4,128]{2,0,1:T(8,128)(2,1)S(1)} %pad_maximum_fusion.10), channel_id=1, source_target_pairs={{16,18},{17,19},{18,16},{19,17},{20,22},{21,23},{22,20},{23,21},{2... | collective-permute-start | bytes 491528 | tf_op jit(solution)/shard_map/ppermute | solution.py:190
  187.4 11.4 %collective-permute-start.16 = (bf16[160,4,128]{2,0,1:T(8,128)(2,1)S(1)}, bf16[160,4,128]{2,0,1:T(8,128)(2,1)S(1)}, u32[]{:S(2)}, u32[]{:S(2)}) collective-permute-start(bf16[160,4,128]{2,0,1:T(8,128)(2,1)S(1)} %pad_maximum_fusion.10), channel_id=1, source_target_pairs={{0,18},{1,19},{2,16},{3,17},{4,22},{5,23},{6,20},{7,21},{8,26},{9,... | collective-permute-start | bytes 491528 | tf_op jit(solution)/shard_map/ppermute | solution.py:189
  225.6 15.6 %collective-permute-start.18 = (f32[650,128]{1,0:T(8,128)S(1)}, f32[650,128]{1,0:T(8,128)S(1)}, u32[]{:S(2)}, u32[]{:S(2)}) collective-permute-start(f32[650,128]{1,0:T(8,128)S(1)} %pad_maximum_fusion.7), channel_id=1, source_target_pairs={{16,18},{17,19},{18,16},{19,17},{20,22},{21,23},{22,20},{23,21},{2... | collective-permute-start | bytes 998408 | tf_op jit(solution)/shard_map/ppermute | solution.py:207
  229.8 11.6 %collective-permute-start.19 = (f32[650,128]{1,0:T(8,128)S(1)}, f32[650,128]{1,0:T(8,128)S(1)}, u32[]{:S(2)}, u32[]{:S(2)}) collective-permute-start(f32[650,128]{1,0:T(8,128)S(1)} %pad_maximum_fusion.8), channel_id=1, source_target_pairs={{0,16},{1,17},{2,18},{3,19},{4,20},{5,21},{6,22},{7,23},{8,24},{9,... | collective-permute-start | bytes 998408 | tf_op jit(solution)/shard_map/ppermute | solution.py:206
  (3 other events, 35.3 us)
Sparse Core Ops, SparseCore 0:
  9.1 89.0 all-gather.1

commit v4 on v3

--- a/solution.py
+++ b/solution.py
@@ -1,6 +1,10 @@
+import functools
+
 import jax
 import jax.numpy as jnp
 from jax import lax
+from jax.experimental import pallas as pl
+from jax.experimental.pallas import tpu as pltpu
 from jax.sharding import PartitionSpec as P
 
 HD = 128
@@ -77,6 +81,61 @@
 
     state, _ = lax.scan(advance, empty_state(req_query.shape[1]), (key_blocks, value_blocks))
     return state
+
+
+def flash_kernel(scale, q_ref, k_ref, v_ref, acc_ref, top_ref, total_ref):
+    step = pl.program_id(0)
+
+    @pl.when(step == 0)
+    def _():
+        acc_ref[...] = jnp.zeros_like(acc_ref)
+        top_ref[...] = jnp.full_like(top_ref, -1e30)
+        total_ref[...] = jnp.zeros_like(total_ref)
+
+    scores = lax.dot_general(
+        q_ref[...], k_ref[...], (((1,), (1,)), ((), ())), preferred_element_type=jnp.float32
+    ) * scale
+    old_top = top_ref[...]
+    new_top = jnp.maximum(old_top, jnp.max(scores, axis=1, keepdims=True))
+    factor = jnp.exp(old_top - new_top)
+    weights = jnp.exp(scores - new_top)
+    total_ref[...] = total_ref[...] * factor + jnp.sum(weights, axis=1, keepdims=True)
+    acc_ref[...] = acc_ref[...] * factor + jnp.dot(
+        weights.astype(jnp.bfloat16), v_ref[...], preferred_element_type=jnp.float32
+    )
+    top_ref[...] = new_top
+
+
+def prefix_attention(q_rows, joined, scale, block=512):
+    rows = q_rows.shape[0]
+    count = joined.shape[0]
+    cost = pl.CostEstimate(
+        flops=4 * rows * count * HD,
+        transcendentals=rows * count,
+        bytes_accessed=2 * (2 * count * HD + rows * HD) + 4 * rows * (HD + 2),
+    )
+    acc, top, total = pl.pallas_call(
+        functools.partial(flash_kernel, scale),
+        grid=(count // block,),
+        in_specs=[
+            pl.BlockSpec((rows, HD), lambda i: (0, 0)),
+            pl.BlockSpec((block, HD), lambda i: (i, 0)),
+            pl.BlockSpec((block, HD), lambda i: (i, 1)),
+        ],
+        out_specs=[
+            pl.BlockSpec((rows, HD), lambda i: (0, 0)),
+            pl.BlockSpec((rows, 1), lambda i: (0, 0)),
+            pl.BlockSpec((rows, 1), lambda i: (0, 0)),
+        ],
+        out_shape=[
+            jax.ShapeDtypeStruct((rows, HD), jnp.float32),
+            jax.ShapeDtypeStruct((rows, 1), jnp.float32),
+            jax.ShapeDtypeStruct((rows, 1), jnp.float32),
+        ],
+        compiler_params=pltpu.CompilerParams(dimension_semantics=("arbitrary",)),
+        cost_estimate=cost,
+    )(q_rows, joined, joined)
+    return top[:, 0], total[:, 0], acc
 
 
 def flat_perm(n_row, n_col, target):
@@ -179,8 +238,6 @@
     other_keyval = partner(keyval, "row", 0)
     suffix_keys = jnp.where(is_even, keyval[:, 0], other_keyval[:, 0])
     suffix_values = jnp.where(is_even, other_keyval[:, 0], keyval[:, 0])
-    half_keys = half_kv[:, :HD]
-    half_values = half_kv[:, HD:]
 
     axes = ("row", "col")
     cross = flat_perm(n_row, n_col, lambda r, c: (r ^ 1, c ^ half_bit) if r % 2 == 0 else (r ^ 1, c))
@@ -192,7 +249,14 @@
     q_second = jnp.where(is_even, q_cross, q_same)
     q_all = jnp.concatenate([q_first, q_second], axis=1)
 
-    half_state = attend_keys(q_all, half_keys, half_values, scale)
+    heads_all = q_all.shape[1]
+    q_rows = jnp.transpose(q_all, (1, 0, 2)).reshape(-1, HD)
+    top, total, accum = prefix_attention(q_rows, half_kv, scale)
+    half_state = (
+        top.reshape(heads_all, SUF),
+        total.reshape(heads_all, SUF),
+        accum.reshape(heads_all, SUF, HD),
+    )
     mine = jax.tree.map(
         lambda a, b: jnp.where(is_even, a, b),
         jax.tree.map(lambda x: x[:heads_here], half_state),

time: 251 us -> 279 us (1.11)
  Pallas kernels: 0 us -> 56 us
  matrix products: 25.2 us -> 4.9 us
  other arithmetic: 23.4 us -> 13.8 us
  waiting for transfers between devices: 116 us -> 124 us
  local copies, waits for them, and re-layouts: 23.1 us -> 17.3 us
    pallas_call x0 -> x1, Pallas kernels: none -> 56 us  [prefix_attention(): pl.pallas_call(functools.partial(flash_kernel, scale), grid=(count // blo...]
    dot_general x8 -> x0, matrix products: 18.7 us -> none  [the longest x4 10.7 us: block_stats(): jnp.einsum('thd,kd->htk', req_query, keys, preferred_element_type=jnp.flo...]
    reduce_sum x4 -> x0, other arithmetic: 7.53 us -> none  [block_stats(): total = jnp.sum(weights, axis=-1)]
    ppermute x1, waiting for transfers between devices: 14 us -> 18.5 us  [per_device(): lax.ppermute(half_sum[1], 'col', [(c, c ^ half_bit) for c in range(n_col)])]
    slice x1 -> x0, local copies, waits for them, and re-layouts: 3.85 us -> none  [per_device(): half_values = half_kv[:, HD:]]
    select_n x1 -> x3, other arithmetic: 0.05 us -> 2.84 us  [per_device(): jnp.where(is_even, a, b)]
    unnamed x16 -> x12, local copies, waits for them, and re-layouts: 10.7 us -> 10.7 us
  transfers between devices with their start and end apart: 22 -> 22, of which waited for: 15 -> 16; matrix products, arithmetic and copies ran while one was open for 13% -> 8% of each run, Pallas kernels for 0% -> 0%
where the time goes in v4:
time: 279 us; the launch traced here: 278 us
  waiting for transfers between devices  124 us (44%)
  Pallas kernels  56 us (20%)
  starting transfers between devices  32.7 us (12%)
  between operations  29.3 us (11%)
  local copies, waits for them, and re-layouts  17.3 us (6%)
  other arithmetic  13.8 us (5%)
  matrix products  4.9 us (2%)
    pallas_call x1, Pallas kernels, prefix_attention(): pl.pallas_call(functools.partial(flash_kernel, scale), grid=(count // blo...  56 us
    ppermute x7, waiting for transfers between devices, per_device(): blocks.append(lax.ppermute(piece, 'col', pairs))  38.6 us
    ppermute x7, waiting for transfers between devices, per_device(): got = lax.ppermute(piece, 'col', [(c, c ^ mask) for c in range(n_col)])  31.6 us
    ppermute x1, waiting for transfers between devices, per_device(): lax.ppermute(half_sum[1], 'col', [(c, c ^ half_bit) for c in range(n_col)])  18.5 us
    all_gather x1, waiting for transfers between devices, per_device(): gathered = lax.all_gather(hidden, 'row', axis=0, tiled=True)  13 us
    ppermute x1, waiting for transfers between devices, per_device(): lax.ppermute(pack_state(mine), axes, same)  10.7 us
    unnamed x12, local copies, waits for them, and re-layouts  10.7 us
    ppermute x1, waiting for transfers between devices, per_device(): q_same = lax.ppermute(query, axes, same)  8.38 us
  transfers between devices with their start and end apart: 22, of which 16 were waited for; matrix products, arithmetic and copies ran while one was open for 8% of the time, Pallas kernels for 0%

profile of v4, /device:TPU:32, one launch (start us, length us, event | category | flops | bytes accessed | tf_op | source)
XLA Modules:
  0.0 277.8 jit_solution(9618645091165448094)
XLA Ops:
  40.6 1.9 constant_dynamic-update-slice_fusion.5
  42.6 8.0 %collective-permute-done.3 = bf16[1024,256]{1,0:T(8,128)(2,1)} collective-permute-done((bf16[1024,256]{1,0:T(8,128)(2,1)S(1)}, bf16[1024,256]{1,0:T(8,128)(2,1)}, u32[]{:S(2)}, u32[]{:S(2)}) %collective-permute-start.3) | collective-permute-done | bytes 524320 | tf_op jit(solution)/shard_map/ppermute | solution.py:201
  52.5 11.2 %collective-permute-done.4 = bf16[1024,256]{1,0:T(8,128)(2,1)S(1)} collective-permute-done((bf16[1024,256]{1,0:T(8,128)(2,1)S(1)}, bf16[1024,256]{1,0:T(8,128)(2,1)S(1)}, u32[]{:S(2)}, u32[]{:S(2)}) %collective-permute-start.4) | collective-permute-done | bytes 524320 | tf_op jit(solution)/shard_map/ppermute | solution.py:201
  64.6 9.4 %collective-permute-done.5 = bf16[1024,256]{1,0:T(8,128)(2,1)S(1)} collective-permute-done((bf16[1024,256]{1,0:T(8,128)(2,1)S(1)}, bf16[1024,256]{1,0:T(8,128)(2,1)S(1)}, u32[]{:S(2)}, u32[]{:S(2)}) %collective-permute-start.5) | collective-permute-done | bytes 524320 | tf_op jit(solution)/shard_map/ppermute | solution.py:201
  75.7 8.6 %collective-permute-done.7 = bf16[1024,256]{1,0:T(8,128)(2,1)S(1)} collective-permute-done((bf16[1024,256]{1,0:T(8,128)(2,1)S(1)}, bf16[1024,256]{1,0:T(8,128)(2,1)S(1)}, u32[]{:S(2)}, u32[]{:S(2)}) %collective-permute-start.7) | collective-permute-done | bytes 524320 | tf_op jit(solution)/shard_map/ppermute | solution.py:201
  85.2 13.0 %all-gather.2.cloned.1.call-done = bf16[2560,512]{1,0:T(8,128)(2,1)} async-done(((bf16[160,512]{1,0:T(8,128)(2,1)}), bf16[2560,512]{1,0:T(8,128)(2,1)}) %all-gather.2.cloned.1.call-update) | async-done | bytes 2621456 | tf_op jit(solution)/shard_map/all_gather | solution.py:186
  98.2 4.0 %fusion.8 = f32[2560,640]{1,0:T(8,128)S(1)} fusion(bf16[2560,512]{1,0:T(8,128)(2,1)} %all-gather.2.cloned.1.call-done, bf16[512,128]{1,0:T(8,128)(2,1)S(1)} %copy-done.1, bf16[512,512]{1,0:T(8,128)(2,1)} %param.7), kind=kOutput, calls=%fused_computation.27 | convolution fusion | flops 1679032320 | bytes 9830400 | tf_op jit(solution)/shard_map/dot_general | solution.py:206
  102.6 2.4 copy-done
  107.1 2.7 collective-permute-start.11
  112.5 2.4 collective-permute-start.13
  116.8 8.7 %collective-permute-done.10 = bf16[2,160,640]{2,1,0:T(8,128)(2,1)S(1)} collective-permute-done((bf16[2,160,640]{2,1,0:T(8,128)(2,1)S(1)}, bf16[2,160,640]{2,1,0:T(8,128)(2,1)S(1)}, u32[]{:S(2)}, u32[]{:S(2)}) %collective-permute-start.10) | collective-permute-done | bytes 409632 | tf_op jit(solution)/shard_map/ppermute | solution.py:224
  128.1 8.4 %collective-permute-done.11 = bf16[2,160,640]{2,1,0:T(8,128)(2,1)S(1)} collective-permute-done((bf16[2,160,640]{2,1,0:T(8,128)(2,1)S(1)}, bf16[2,160,640]{2,1,0:T(8,128)(2,1)S(1)}, u32[]{:S(2)}, u32[]{:S(2)}) %collective-permute-start.11) | collective-permute-done | bytes 409632 | tf_op jit(solution)/shard_map/ppermute | solution.py:224
  136.5 2.4 collective-permute-done.12
  138.9 4.9 %collective-permute-done.13 = bf16[2,160,640]{2,1,0:T(8,128)(2,1)S(1)} collective-permute-done((bf16[2,160,640]{2,1,0:T(8,128)(2,1)}, bf16[2,160,640]{2,1,0:T(8,128)(2,1)S(1)}, u32[]{:S(2)}, u32[]{:S(2)}) %collective-permute-start.13) | collective-permute-done | bytes 409632 | tf_op jit(solution)/shard_map/ppermute | solution.py:224
  143.8 7.0 %collective-permute-done.14 = bf16[2,160,640]{2,1,0:T(8,128)(2,1)S(1)} collective-permute-done((bf16[2,160,640]{2,1,0:T(8,128)(2,1)}, bf16[2,160,640]{2,1,0:T(8,128)(2,1)S(1)}, u32[]{:S(2)}, u32[]{:S(2)}) %collective-permute-start.14) | collective-permute-done | bytes 409632 | tf_op jit(solution)/shard_map/ppermute | solution.py:224
  151.3 3.3 %collective-permute-start.15 = (f32[160,640]{1,0:T(8,128)S(1)}, f32[160,640]{1,0:T(8,128)S(1)}, u32[]{:S(2)}, u32[]{:S(2)}) collective-permute-start(f32[160,640]{1,0:T(8,128)S(1)} %slice_bitcast_fusion), channel_id=1, source_target_pairs={{0,2},{1,3},{2,0},{3,1},{4,6},{5,7},{6,4},{7,5},{8,10},{9,11},{10,... | collective-permute-start | bytes 1228808 | tf_op jit(solution)/shard_map/ppermute | solution.py:226
  155.1 18.5 %collective-permute-done.15 = f32[160,640]{1,0:T(8,128)S(1)} collective-permute-done((f32[160,640]{1,0:T(8,128)S(1)}, f32[160,640]{1,0:T(8,128)S(1)}, u32[]{:S(2)}, u32[]{:S(2)}) %collective-permute-start.15) | collective-permute-done | bytes 409632 | tf_op jit(solution)/shard_map/ppermute | solution.py:226
  174.3 3.8 %collective-permute-start.20 = (bf16[160,1,128]{2,0,1:T(8,128)(2,1)S(1)}, bf16[160,1,128]{2,0,1:T(8,128)(2,1)S(1)}, u32[]{:S(2)}, u32[]{:S(2)}) collective-permute-start(bf16[160,1,128]{2,0,1:T(8,128)(2,1)S(1)} %bitcast.84), channel_id=1, source_target_pairs={{0,16},{16,0},{32,48},{48,32},{64,80},{80,64},{96,112},{112,96},{1... | collective-permute-start | bytes 122888 | tf_op jit(solution)/shard_map/ppermute | solution.py:18
  178.5 4.1 %collective-permute-start.17 = (bf16[160,4,128]{2,0,1:T(8,128)(2,1)S(1)}, bf16[160,4,128]{2,0,1:T(8,128)(2,1)S(1)}, u32[]{:S(2)}, u32[]{:S(2)}) collective-permute-start(bf16[160,4,128]{2,0,1:T(8,128)(2,1)S(1)} %pad_maximum_fusion.10), channel_id=1, source_target_pairs={{16,18},{17,19},{18,16},{19,17},{20,22},{21,23},{22,20},{23,21},{2... | collective-permute-start | bytes 491528 | tf_op jit(solution)/shard_map/ppermute | solution.py:247
  183.0 8.4 %collective-permute-done.17 = bf16[160,4,128]{2,0,1:T(8,128)(2,1)S(1)} collective-permute-done((bf16[160,4,128]{2,0,1:T(8,128)(2,1)S(1)}, bf16[160,4,128]{2,0,1:T(8,128)(2,1)S(1)}, u32[]{:S(2)}, u32[]{:S(2)}) %collective-permute-start.17) | collective-permute-done | bytes 163872 | tf_op jit(solution)/shard_map/ppermute | solution.py:247
  191.4 2.3 collective-permute-done.16
  194.5 56.0 %shard_map.64 = (f32[1280,128]{1,0:T(8,128)}, f32[1280,1]{1,0:T(8,128)}, f32[1280,1]{1,0:T(8,128)}) custom-call(bf16[1280,128]{1,0:T(8,128)(2,1)} %bitcast.83, bf16[8192,256]{1,0:T(8,128)(2,1)} %constant_dynamic-update-slice_fusion.k_ref.v_ref, bf16[8192,256]{1,0:T(8,128)(2,1)} %constant_dynamic-update-slice_fusion.k_ref.v_ref), custom_call_target="tpu_custom_call" | custom-call | flops 5368709120 | bytes 5187584 | tf_op jit(solution)/shard_map/pallas_call | solution.py:117
  253.7 4.3 %collective-permute-start.18 = (f32[650,128]{1,0:T(8,128)S(1)}, f32[650,128]{1,0:T(8,128)S(1)}, u32[]{:S(2)}, u32[]{:S(2)}) collective-permute-start(f32[650,128]{1,0:T(8,128)S(1)} %pad_maximum_fusion.7), channel_id=1, source_target_pairs={{16,18},{17,19},{18,16},{19,17},{20,22},{21,23},{22,20},{23,21},{2... | collective-permute-start | bytes 998408 | tf_op jit(solution)/shard_map/ppermute | solution.py:271
  258.5 10.7 %collective-permute-done.18 = f32[650,128]{1,0:T(8,128)S(1)} collective-permute-done((f32[650,128]{1,0:T(8,128)S(1)}, f32[650,128]{1,0:T(8,128)S(1)}, u32[]{:S(2)}, u32[]{:S(2)}) %collective-permute-start.18) | collective-permute-done | bytes 332832 | tf_op jit(solution)/shard_map/ppermute | solution.py:271
  (98 shorter events, 42.0 us)
Async XLA Ops:
  6.5 23.0 %copy-start.2 = (s32[16]{0:T(128)S(1)}, s32[16]{0:T(128)}, u32[]{:S(2)}) copy-start(s32[16]{0:T(128)} %param.10) | copy-start | bytes 196
  6.5 91.6 %all-gather.2.cloned.1.call-start = ((), (), s32[]{:S(2)}) async-start(), calls=%async_computation | async-start | bytes 2785280 | tf_op jit(solution)/shard_map/all_gather | solution.py:186
  7.3 15.4 %collective-permute-start = (bf16[2,1024,128]{2,1,0:T(8,128)(2,1)}, bf16[2,1024,128]{2,1,0:T(8,128)(2,1)S(1)}, u32[]{:S(2)}, u32[]{:S(2)}) collective-permute-start(bf16[2,1024,128]{2,1,0:T(8,128)(2,1)} %param.9), channel_id=1, source_target_pairs={{0,16},{16,0},{32,48},{48,32},{64,80},{80,64},{96,112},{112,96},{1... | collective-permute-start | bytes 1572872 | tf_op jit(solution)/shard_map/ppermute | solution.py:18
  25.2 10.4 %collective-permute-start.1 = (bf16[1024,256]{1,0:T(8,128)(2,1)}, bf16[1024,256]{1,0:T(8,128)(2,1)}, u32[]{:S(2)}, u32[]{:S(2)}) collective-permute-start(bf16[1024,256]{1,0:T(8,128)(2,1)} %get-tuple-element.40), channel_id=1, source_target_pairs={{0,1},{1,0},{2,3},{3,2},{4,5},{5,4},{6,7},{7,6},{8,9},{9,8},{10,11... | collective-permute-start | bytes 1572872 | tf_op jit(solution)/shard_map/ppermute | solution.py:201
  25.2 15.1 %collective-permute-start.2 = (bf16[1024,256]{1,0:T(8,128)(2,1)}, bf16[1024,256]{1,0:T(8,128)(2,1)}, u32[]{:S(2)}, u32[]{:S(2)}) collective-permute-start(bf16[1024,256]{1,0:T(8,128)(2,1)} %get-tuple-element.41), channel_id=1, source_target_pairs={{0,4},{1,5},{2,6},{3,7},{4,0},{5,1},{6,2},{7,3},{8,12},{9,13},{10,... | collective-permute-start | bytes 1572872 | tf_op jit(solution)/shard_map/ppermute | solution.py:201
  25.3 25.3 %collective-permute-start.3 = (bf16[1024,256]{1,0:T(8,128)(2,1)S(1)}, bf16[1024,256]{1,0:T(8,128)(2,1)}, u32[]{:S(2)}, u32[]{:S(2)}) collective-permute-start(bf16[1024,256]{1,0:T(8,128)(2,1)S(1)} %get-tuple-element.42), channel_id=1, source_target_pairs={{0,5},{1,4},{2,7},{3,6},{4,1},{5,0},{6,3},{7,2},{8,13},{9,12},{10,... | collective-permute-start | bytes 1572872 | tf_op jit(solution)/shard_map/ppermute | solution.py:201
  31.3 32.4 %collective-permute-start.4 = (bf16[1024,256]{1,0:T(8,128)(2,1)S(1)}, bf16[1024,256]{1,0:T(8,128)(2,1)S(1)}, u32[]{:S(2)}, u32[]{:S(2)}) collective-permute-start(bf16[1024,256]{1,0:T(8,128)(2,1)S(1)} %get-tuple-element.43), channel_id=1, source_target_pairs={{0,8},{1,9},{2,10},{3,11},{4,12},{5,13},{6,14},{7,15},{8,0},{9,1},... | collective-permute-start | bytes 1572872 | tf_op jit(solution)/shard_map/ppermute | solution.py:201
  33.2 65.0 %copy-start.1 = (bf16[512,128]{1,0:T(8,128)(2,1)S(1)}, bf16[512,128]{1,0:T(8,128)(2,1)}, u32[]{:S(2)}) copy-start(bf16[512,128]{1,0:T(8,128)(2,1)} %param.8) | copy-start | bytes 393220
  33.2 40.9 %collective-permute-start.5 = (bf16[1024,256]{1,0:T(8,128)(2,1)S(1)}, bf16[1024,256]{1,0:T(8,128)(2,1)S(1)}, u32[]{:S(2)}, u32[]{:S(2)}) collective-permute-start(bf16[1024,256]{1,0:T(8,128)(2,1)S(1)} %get-tuple-element.44), channel_id=1, source_target_pairs={{0,9},{1,8},{2,11},{3,10},{4,13},{5,12},{6,15},{7,14},{8,1},{9,0},... | collective-permute-start | bytes 1572872 | tf_op jit(solution)/shard_map/ppermute | solution.py:201
  35.6 39.3 %collective-permute-start.6 = (bf16[1024,256]{1,0:T(8,128)(2,1)S(1)}, bf16[1024,256]{1,0:T(8,128)(2,1)S(1)}, u32[]{:S(2)}, u32[]{:S(2)}) collective-permute-start(bf16[1024,256]{1,0:T(8,128)(2,1)S(1)} %fusion.30), channel_id=1, source_target_pairs={{0,12},{1,13},{2,14},{3,15},{4,8},{5,9},{6,10},{7,11},{8,4},{9,5},... | collective-permute-start | bytes 1572872 | tf_op jit(solution)/shard_map/ppermute | solution.py:201
  40.3 44.0 %collective-permute-start.7 = (bf16[1024,256]{1,0:T(8,128)(2,1)S(1)}, bf16[1024,256]{1,0:T(8,128)(2,1)S(1)}, u32[]{:S(2)}, u32[]{:S(2)}) collective-permute-start(bf16[1024,256]{1,0:T(8,128)(2,1)S(1)} %get-tuple-element.39), channel_id=1, source_target_pairs={{0,13},{1,12},{2,15},{3,14},{4,9},{5,8},{6,11},{7,10},{8,5},{9,4},... | collective-permute-start | bytes 1572872 | tf_op jit(solution)/shard_map/ppermute | solution.py:201
  105.3 11.4 %collective-permute-start.9 = (bf16[2,160,640]{2,1,0:T(8,128)(2,1)S(1)}, bf16[2,160,640]{2,1,0:T(8,128)(2,1)S(1)}, u32[]{:S(2)}, u32[]{:S(2)}) collective-permute-start(bf16[2,160,640]{2,1,0:T(8,128)(2,1)S(1)} %pad_maximum_fusion.1), channel_id=1, source_target_pairs={{0,4},{1,5},{2,6},{3,7},{4,0},{5,1},{6,2},{7,3},{8,12},{9,13},{10,... | collective-permute-start | bytes 1228808 | tf_op jit(solution)/shard_map/ppermute | solution.py:224
  107.0 18.5 %collective-permute-start.10 = (bf16[2,160,640]{2,1,0:T(8,128)(2,1)S(1)}, bf16[2,160,640]{2,1,0:T(8,128)(2,1)S(1)}, u32[]{:S(2)}, u32[]{:S(2)}) collective-permute-start(bf16[2,160,640]{2,1,0:T(8,128)(2,1)S(1)} %pad_maximum_fusion.2), channel_id=1, source_target_pairs={{0,5},{1,4},{2,7},{3,6},{4,1},{5,0},{6,3},{7,2},{8,13},{9,12},{10,... | collective-permute-start | bytes 1228808 | tf_op jit(solution)/shard_map/ppermute | solution.py:224
  107.1 29.4 %collective-permute-start.11 = (bf16[2,160,640]{2,1,0:T(8,128)(2,1)S(1)}, bf16[2,160,640]{2,1,0:T(8,128)(2,1)S(1)}, u32[]{:S(2)}, u32[]{:S(2)}) collective-permute-start(bf16[2,160,640]{2,1,0:T(8,128)(2,1)S(1)} %pad_maximum_fusion.3), channel_id=1, source_target_pairs={{0,8},{1,9},{2,10},{3,11},{4,12},{5,13},{6,14},{7,15},{8,0},{9,1},... | collective-permute-start | bytes 1228808 | tf_op jit(solution)/shard_map/ppermute | solution.py:224
  110.6 28.3 %collective-permute-start.12 = (bf16[2,160,640]{2,1,0:T(8,128)(2,1)}, bf16[2,160,640]{2,1,0:T(8,128)(2,1)S(1)}, u32[]{:S(2)}, u32[]{:S(2)}) collective-permute-start(bf16[2,160,640]{2,1,0:T(8,128)(2,1)} %pad_maximum_fusion.4), channel_id=1, source_target_pairs={{0,9},{1,8},{2,11},{3,10},{4,13},{5,12},{6,15},{7,14},{8,1},{9,0},... | collective-permute-start | bytes 1228808 | tf_op jit(solution)/shard_map/ppermute | solution.py:224
  112.5 31.3 %collective-permute-start.13 = (bf16[2,160,640]{2,1,0:T(8,128)(2,1)}, bf16[2,160,640]{2,1,0:T(8,128)(2,1)S(1)}, u32[]{:S(2)}, u32[]{:S(2)}) collective-permute-start(bf16[2,160,640]{2,1,0:T(8,128)(2,1)} %pad_maximum_fusion.5), channel_id=1, source_target_pairs={{0,12},{1,13},{2,14},{3,15},{4,8},{5,9},{6,10},{7,11},{8,4},{9,5},... | collective-permute-start | bytes 1228808 | tf_op jit(solution)/shard_map/ppermute | solution.py:224
  116.7 34.1 %collective-permute-start.14 = (bf16[2,160,640]{2,1,0:T(8,128)(2,1)}, bf16[2,160,640]{2,1,0:T(8,128)(2,1)S(1)}, u32[]{:S(2)}, u32[]{:S(2)}) collective-permute-start(bf16[2,160,640]{2,1,0:T(8,128)(2,1)} %pad_maximum_fusion.6), channel_id=1, source_target_pairs={{0,13},{1,12},{2,15},{3,14},{4,9},{5,8},{6,11},{7,10},{8,5},{9,4},... | collective-permute-start | bytes 1228808 | tf_op jit(solution)/shard_map/ppermute | solution.py:224
  125.5 25.4 %collective-permute-start.8 = (bf16[2,160,640]{2,1,0:T(8,128)(2,1)}, bf16[2,160,640]{2,1,0:T(8,128)(2,1)S(1)}, u32[]{:S(2)}, u32[]{:S(2)}) collective-permute-start(bf16[2,160,640]{2,1,0:T(8,128)(2,1)} %pad_maximum_fusion), channel_id=1, source_target_pairs={{0,1},{1,0},{2,3},{3,2},{4,5},{5,4},{6,7},{7,6},{8,9},{9,8},{10,11... | collective-permute-start | bytes 1228808 | tf_op jit(solution)/shard_map/ppermute | solution.py:224
  151.3 22.3 %collective-permute-start.15 = (f32[160,640]{1,0:T(8,128)S(1)}, f32[160,640]{1,0:T(8,128)S(1)}, u32[]{:S(2)}, u32[]{:S(2)}) collective-permute-start(f32[160,640]{1,0:T(8,128)S(1)} %slice_bitcast_fusion), channel_id=1, source_target_pairs={{0,2},{1,3},{2,0},{3,1},{4,6},{5,7},{6,4},{7,5},{8,10},{9,11},{10,... | collective-permute-start | bytes 1228808 | tf_op jit(solution)/shard_map/ppermute | solution.py:226
  174.3 8.5 %collective-permute-start.20 = (bf16[160,1,128]{2,0,1:T(8,128)(2,1)S(1)}, bf16[160,1,128]{2,0,1:T(8,128)(2,1)S(1)}, u32[]{:S(2)}, u32[]{:S(2)}) collective-permute-start(bf16[160,1,128]{2,0,1:T(8,128)(2,1)S(1)} %bitcast.84), channel_id=1, source_target_pairs={{0,16},{16,0},{32,48},{48,32},{64,80},{80,64},{96,112},{112,96},{1... | collective-permute-start | bytes 122888 | tf_op jit(solution)/shard_map/ppermute | solution.py:18
  178.5 12.9 %collective-permute-start.17 = (bf16[160,4,128]{2,0,1:T(8,128)(2,1)S(1)}, bf16[160,4,128]{2,0,1:T(8,128)(2,1)S(1)}, u32[]{:S(2)}, u32[]{:S(2)}) collective-permute-start(bf16[160,4,128]{2,0,1:T(8,128)(2,1)S(1)} %pad_maximum_fusion.10), channel_id=1, source_target_pairs={{16,18},{17,19},{18,16},{19,17},{20,22},{21,23},{22,20},{23,21},{2... | collective-permute-start | bytes 491528 | tf_op jit(solution)/shard_map/ppermute | solution.py:247
  182.7 11.0 %collective-permute-start.16 = (bf16[160,4,128]{2,0,1:T(8,128)(2,1)S(1)}, bf16[160,4,128]{2,0,1:T(8,128)(2,1)S(1)}, u32[]{:S(2)}, u32[]{:S(2)}) collective-permute-start(bf16[160,4,128]{2,0,1:T(8,128)(2,1)S(1)} %pad_maximum_fusion.10), channel_id=1, source_target_pairs={{0,18},{1,19},{2,16},{3,17},{4,22},{5,23},{6,20},{7,21},{8,26},{9,... | collective-permute-start | bytes 491528 | tf_op jit(solution)/shard_map/ppermute | solution.py:246
  253.7 15.5 %collective-permute-start.18 = (f32[650,128]{1,0:T(8,128)S(1)}, f32[650,128]{1,0:T(8,128)S(1)}, u32[]{:S(2)}, u32[]{:S(2)}) collective-permute-start(f32[650,128]{1,0:T(8,128)S(1)} %pad_maximum_fusion.7), channel_id=1, source_target_pairs={{16,18},{17,19},{18,16},{19,17},{20,22},{21,23},{22,20},{23,21},{2... | collective-permute-start | bytes 998408 | tf_op jit(solution)/shard_map/ppermute | solution.py:271
  258.1 11.2 %collective-permute-start.19 = (f32[650,128]{1,0:T(8,128)S(1)}, f32[650,128]{1,0:T(8,128)S(1)}, u32[]{:S(2)}, u32[]{:S(2)}) collective-permute-start(f32[650,128]{1,0:T(8,128)S(1)} %pad_maximum_fusion.8), channel_id=1, source_target_pairs={{0,16},{1,17},{2,18},{3,19},{4,20},{5,21},{6,22},{7,23},{8,24},{9,... | collective-permute-start | bytes 998408 | tf_op jit(solution)/shard_map/ppermute | solution.py:270
  (1 other events, 2.7 us)
Sparse Core Ops, SparseCore 0:
  9.1 89.0 all-gather.1

commit v5 on v3

--- a/solution.py
+++ b/solution.py
@@ -1,16 +1,21 @@
+import functools
+
 import jax
 import jax.numpy as jnp
 from jax import lax
+from jax.sharding import Mesh
 from jax.sharding import PartitionSpec as P
 
 HD = 128
 PREFIX = 16384
 SUF = 160
-
-
-def partner(value, axis, stride):
+ROW = ("x", "zl")
+COL = ("y", "zh", "core")
+
+
+def partner(value, axis, stride, size):
     mask = 2**stride
-    pairs = [(source, source ^ mask) for source in range(lax.axis_size(axis))]
+    pairs = [(source, source ^ mask) for source in range(size)]
     return lax.ppermute(value, axis, pairs)
 
 
@@ -115,20 +120,26 @@
     return (stats[0], stats[1], accum)
 
 
-def per_device(hidden, w_query, w_keyval, prefix_cache, suffix_lengths, group_ids):
-    n_row = lax.axis_size("row")
-    n_col = lax.axis_size("col")
-    row_id = lax.axis_index("row")
-    col_id = lax.axis_index("col")
+def per_device(n_row, n_col, hidden, w_query, w_keyval, prefix_cache, suffix_lengths, group_ids):
+    row_id = lax.axis_index(ROW)
+    col_id = lax.axis_index(COL)
     heads_here = w_query.shape[1] // HD
     segments = w_keyval.shape[1] // HD
     scale = 1.0 / HD**0.5
     half_bit = 2
-    gathered = lax.all_gather(hidden, "row", axis=0, tiled=True)
+    n_low = n_row // 4
+    low_id = lax.axis_index("zl")
+    stacked = [hidden]
+    for mask in range(1, n_low):
+        stacked.append(lax.ppermute(hidden, "zl", [(i, i ^ mask) for i in range(n_low)]))
+    stacked = jnp.stack(stacked)
+    order = low_id ^ jnp.arange(n_low, dtype=jnp.int32)
+    gathered = jnp.take(stacked, order, axis=0).reshape(-1, hidden.shape[1])
+    gathered = lax.all_gather(gathered, "x", axis=0, tiled=True)
     odd = row_id % 2
     is_even = odd == 0
     handled = col_id ^ (half_bit * odd)
-    other_cache = partner(prefix_cache, "row", 0)
+    other_cache = partner(prefix_cache, ROW, 0, n_row)
     cache_keys = jnp.where(is_even, prefix_cache, other_cache)
     cache_values = jnp.where(is_even, other_cache, prefix_cache)
     kv_block = jnp.concatenate([cache_keys, cache_values], axis=-1)
@@ -139,7 +150,7 @@
         peer_group = group_ids[(col_id ^ mask) ^ (half_bit * odd)]
         piece = lax.dynamic_index_in_dim(kv_block, peer_group, 0, keepdims=False)
         pairs = [(c, c ^ mask) for c in range(n_col)]
-        blocks.append(lax.ppermute(piece, "col", pairs))
+        blocks.append(lax.ppermute(piece, COL, pairs))
     half_kv = jnp.concatenate(blocks, axis=0)
     gathered, half_kv = lax.optimization_barrier((gathered, half_kv))
     weights_all = jnp.concatenate([w_query, w_keyval], axis=1)
@@ -162,9 +173,9 @@
                 lax.dynamic_index_in_dim(low, peer ^ half_bit, 0, keepdims=False),
             ]
         )
-        got = lax.ppermute(piece, "col", [(c, c ^ mask) for c in range(n_col)])
+        got = lax.ppermute(piece, COL, [(c, c ^ mask) for c in range(n_col)])
         half_sum = half_sum + got.astype(jnp.float32)
-    across = lax.ppermute(half_sum[1], "col", [(c, c ^ half_bit) for c in range(n_col)])
+    across = lax.ppermute(half_sum[1], COL, [(c, c ^ half_bit) for c in range(n_col)])
     projected = half_sum[0] + across
     positions = PREFIX + jnp.arange(tok_block, dtype=jnp.int32) % SUF
     cosine, sine = rotary_tables(positions)
@@ -176,13 +187,13 @@
     keyval = jnp.where(is_key[None, :, None], rotate(keyval, cosine, sine), keyval).astype(
         jnp.bfloat16
     )
-    other_keyval = partner(keyval, "row", 0)
+    other_keyval = partner(keyval, ROW, 0, n_row)
     suffix_keys = jnp.where(is_even, keyval[:, 0], other_keyval[:, 0])
     suffix_values = jnp.where(is_even, other_keyval[:, 0], keyval[:, 0])
     half_keys = half_kv[:, :HD]
     half_values = half_kv[:, HD:]
 
-    axes = ("row", "col")
+    axes = ROW + COL
     cross = flat_perm(n_row, n_col, lambda r, c: (r ^ 1, c ^ half_bit) if r % 2 == 0 else (r ^ 1, c))
     back = flat_perm(n_row, n_col, lambda r, c: (r ^ 1, c) if r % 2 == 0 else (r ^ 1, c ^ half_bit))
     same = flat_perm(n_row, n_col, lambda r, c: (r, c ^ half_bit) if r % 2 == 1 else None)
@@ -228,17 +239,19 @@
 
 
 def solution(mesh):
+    n_row, n_col = mesh.devices.shape
+    fine = Mesh(mesh.devices.reshape(4, n_row // 4, 4, 2, n_col // 8), ROW + COL)
     return jax.shard_map(
-        per_device,
-        mesh=mesh,
+        functools.partial(per_device, n_row, n_col),
+        mesh=fine,
         in_specs=(
-            P("row", "col"),
-            P("col", "row"),
-            P("col", "row"),
-            P(None, "col", "row"),
+            P(ROW, COL),
+            P(COL, ROW),
+            P(COL, ROW),
+            P(None, COL, ROW),
             P(),
             P(),
         ),
-        out_specs=P("col", "row"),
+        out_specs=P(COL, ROW),
         check_vma=False,
     )

time: 251 us -> 268 us (1.068)
  starting transfers between devices: 33.6 us -> 47.3 us
  waiting for transfers between devices: 116 us -> 120 us
    ppermute x15 -> x18, starting transfers between devices: 19.4 us -> 30.5 us  [the longest x7 10.9 us: per_device(): got = lax.ppermute(piece, COL, [(c, c ^ mask) for c in range(n_col)])]
    all_gather x1, waiting for transfers between devices: 11.1 us -> 0.01 us  [per_device(): gathered = lax.all_gather(gathered, 'x', axis=0, tiled=True)]
    ppermute x15 -> x18, waiting for transfers between devices: 84.4 us -> 93.8 us  [the longest x7 35.9 us: per_device(): blocks.append(lax.ppermute(piece, COL, pairs))]
    ppermute x1, waiting for transfers between devices: 0.01 us -> 4 us  [per_device(): lax.ppermute(pack_state(theirs), axes, back)]
    ppermute x2, starting transfers between devices: 6.24 us -> 2.31 us  [partner(): return lax.ppermute(value, axis, pairs)]
    ppermute x1, starting transfers between devices: 3.71 us -> 7.09 us  [per_device(): q_same = lax.ppermute(query, axes, same)]
    ppermute x1, starting transfers between devices: 4.09 us -> 6.94 us  [per_device(): lax.ppermute(pack_state(mine), axes, same)]
    unnamed x16 -> x22, local copies, waits for them, and re-layouts: 10.7 us -> 10.7 us
  transfers between devices with their start and end apart: 22 -> 25, of which waited for: 15 -> 17; matrix products, arithmetic and copies ran while one was open for 13% -> 11% of each run, Pallas kernels for 0% -> 0%
where the time goes in v5:
time: 268 us; the launch traced here: 267 us
  waiting for transfers between devices  120 us (45%)
  starting transfers between devices  47.3 us (18%)
  between operations  28.6 us (11%)
  matrix products  25.2 us (9%)
  other arithmetic  24.4 us (9%)
  local copies, waits for them, and re-layouts  22.3 us (8%)
    ppermute x7, waiting for transfers between devices, per_device(): blocks.append(lax.ppermute(piece, COL, pairs))  35.9 us
    ppermute x7, waiting for transfers between devices, per_device(): got = lax.ppermute(piece, COL, [(c, c ^ mask) for c in range(n_col)])  29.2 us
    ppermute x1, waiting for transfers between devices, per_device(): lax.ppermute(half_sum[1], COL, [(c, c ^ half_bit) for c in range(n_col)])  15.5 us
    ppermute x3, waiting for transfers between devices, per_device(): lax.ppermute(hidden, 'zl', [(i, i ^ mask) for i in range(n_low)])  13.3 us
    ppermute x1, waiting for transfers between devices, per_device(): lax.ppermute(pack_state(mine), axes, same)  11 us
    ppermute x7, starting transfers between devices, per_device(): got = lax.ppermute(piece, COL, [(c, c ^ mask) for c in range(n_col)])  10.9 us
    unnamed x22, local copies, waits for them, and re-layouts  10.7 us
    dot_general x4, matrix products, block_stats(): jnp.einsum('thd,kd->htk', req_query, keys, preferred_element_type=jnp.flo...  10.7 us
  transfers between devices with their start and end apart: 25, of which 17 were waited for; matrix products, arithmetic and copies ran while one was open for 11% of the time, Pallas kernels for 0%

profile of v5, /device:TPU:32, one launch (start us, length us, event | category | flops | bytes accessed | tf_op | source)
XLA Modules:
  0.0 267.4 jit_solution(1166776864227792990)
XLA Ops:
  13.5 9.3 %collective-permute-done.2 = bf16[160,512]{1,0:T(8,128)(2,1)S(1)} collective-permute-done((bf16[160,512]{1,0:T(8,128)(2,1)}, bf16[160,512]{1,0:T(8,128)(2,1)S(1)}, u32[]{:S(2)}, u32[]{:S(2)}) %collective-permute-start.2) | collective-permute-done | bytes 163872 | tf_op jit(solution)/shard_map/ppermute | solution.py:134
  50.8 3.3 %collective-permute-start.7 = (bf16[1024,256]{1,0:T(8,128)(2,1)S(1)}, bf16[1024,256]{1,0:T(8,128)(2,1)S(1)}, u32[]{:S(2)}, u32[]{:S(2)}) collective-permute-start(bf16[1024,256]{1,0:T(8,128)(2,1)S(1)} %get-tuple-element.121), channel_id=1, source_target_pairs={{0,8},{1,9},{2,10},{3,11},{4,12},{5,13},{6,14},{7,15},{8,0},{9,1},... | collective-permute-start | bytes 1572872 | tf_op jit(solution)/shard_map/ppermute | solution.py:153
  55.1 2.9 %collective-permute-start.9 = (bf16[1024,256]{1,0:T(8,128)(2,1)S(1)}, bf16[1024,256]{1,0:T(8,128)(2,1)S(1)}, u32[]{:S(2)}, u32[]{:S(2)}) collective-permute-start(bf16[1024,256]{1,0:T(8,128)(2,1)S(1)} %fusion.50), channel_id=1, source_target_pairs={{0,12},{1,13},{2,14},{3,15},{4,8},{5,9},{6,10},{7,11},{8,4},{9,5},... | collective-permute-start | bytes 1572872 | tf_op jit(solution)/shard_map/ppermute | solution.py:153
  63.5 6.6 %collective-permute-done.6 = bf16[1024,256]{1,0:T(8,128)(2,1)} collective-permute-done((bf16[1024,256]{1,0:T(8,128)(2,1)S(1)}, bf16[1024,256]{1,0:T(8,128)(2,1)}, u32[]{:S(2)}, u32[]{:S(2)}) %collective-permute-start.6) | collective-permute-done | bytes 524320 | tf_op jit(solution)/shard_map/ppermute | solution.py:153
  72.0 12.7 %collective-permute-done.7 = bf16[1024,256]{1,0:T(8,128)(2,1)S(1)} collective-permute-done((bf16[1024,256]{1,0:T(8,128)(2,1)S(1)}, bf16[1024,256]{1,0:T(8,128)(2,1)S(1)}, u32[]{:S(2)}, u32[]{:S(2)}) %collective-permute-start.7) | collective-permute-done | bytes 524320 | tf_op jit(solution)/shard_map/ppermute | solution.py:153
  85.5 9.5 %collective-permute-done.8 = bf16[1024,256]{1,0:T(8,128)(2,1)S(1)} collective-permute-done((bf16[1024,256]{1,0:T(8,128)(2,1)S(1)}, bf16[1024,256]{1,0:T(8,128)(2,1)S(1)}, u32[]{:S(2)}, u32[]{:S(2)}) %collective-permute-start.8) | collective-permute-done | bytes 524320 | tf_op jit(solution)/shard_map/ppermute | solution.py:153
  96.7 7.2 %collective-permute-done.10 = bf16[1024,256]{1,0:T(8,128)(2,1)S(1)} collective-permute-done((bf16[1024,256]{1,0:T(8,128)(2,1)S(1)}, bf16[1024,256]{1,0:T(8,128)(2,1)S(1)}, u32[]{:S(2)}, u32[]{:S(2)}) %collective-permute-start.10) | collective-permute-done | bytes 524320 | tf_op jit(solution)/shard_map/ppermute | solution.py:153
  104.7 4.0 %fusion.28 = f32[2560,640]{1,0:T(8,128)S(1)} fusion(bf16[2560,512]{1,0:T(8,128)(2,1)} %all-gather.2.cloned.1.call-done, bf16[512,128]{1,0:T(8,128)(2,1)S(1)} %copy-done.5, bf16[512,512]{1,0:T(8,128)(2,1)} %param.9), kind=kOutput, calls=%fused_computation.51 | convolution fusion | flops 1679032320 | bytes 9830400 | tf_op jit(solution)/shard_map/dot_general | solution.py:158
  114.6 2.8 %collective-permute-start.14 = (bf16[2,160,640]{2,1,0:T(8,128)(2,1)}, bf16[2,160,640]{2,1,0:T(8,128)(2,1)S(1)}, u32[]{:S(2)}, u32[]{:S(2)}) collective-permute-start(bf16[2,160,640]{2,1,0:T(8,128)(2,1)} %pad_maximum_fusion.4), channel_id=1, source_target_pairs={{0,8},{1,9},{2,10},{3,11},{4,12},{5,13},{6,14},{7,15},{8,0},{9,1},... | collective-permute-start | bytes 1228808 | tf_op jit(solution)/shard_map/ppermute | solution.py:176
  119.6 3.0 %collective-permute-start.16 = (bf16[2,160,640]{2,1,0:T(8,128)(2,1)}, bf16[2,160,640]{2,1,0:T(8,128)(2,1)S(1)}, u32[]{:S(2)}, u32[]{:S(2)}) collective-permute-start(bf16[2,160,640]{2,1,0:T(8,128)(2,1)} %pad_maximum_fusion.6), channel_id=1, source_target_pairs={{0,12},{1,13},{2,14},{3,15},{4,8},{5,9},{6,10},{7,11},{8,4},{9,5},... | collective-permute-start | bytes 1228808 | tf_op jit(solution)/shard_map/ppermute | solution.py:176
  125.7 6.1 %collective-permute-done.13 = bf16[2,160,640]{2,1,0:T(8,128)(2,1)S(1)} collective-permute-done((bf16[2,160,640]{2,1,0:T(8,128)(2,1)S(1)}, bf16[2,160,640]{2,1,0:T(8,128)(2,1)S(1)}, u32[]{:S(2)}, u32[]{:S(2)}) %collective-permute-start.13) | collective-permute-done | bytes 409632 | tf_op jit(solution)/shard_map/ppermute | solution.py:176
  135.5 8.9 %collective-permute-done.14 = bf16[2,160,640]{2,1,0:T(8,128)(2,1)S(1)} collective-permute-done((bf16[2,160,640]{2,1,0:T(8,128)(2,1)}, bf16[2,160,640]{2,1,0:T(8,128)(2,1)S(1)}, u32[]{:S(2)}, u32[]{:S(2)}) %collective-permute-start.14) | collective-permute-done | bytes 409632 | tf_op jit(solution)/shard_map/ppermute | solution.py:176
  144.4 7.4 %collective-permute-done.15 = bf16[2,160,640]{2,1,0:T(8,128)(2,1)S(1)} collective-permute-done((bf16[2,160,640]{2,1,0:T(8,128)(2,1)}, bf16[2,160,640]{2,1,0:T(8,128)(2,1)S(1)}, u32[]{:S(2)}, u32[]{:S(2)}) %collective-permute-start.15) | collective-permute-done | bytes 409632 | tf_op jit(solution)/shard_map/ppermute | solution.py:176
  151.8 6.6 %collective-permute-done.17 = bf16[2,160,640]{2,1,0:T(8,128)(2,1)S(1)} collective-permute-done((bf16[2,160,640]{2,1,0:T(8,128)(2,1)}, bf16[2,160,640]{2,1,0:T(8,128)(2,1)S(1)}, u32[]{:S(2)}, u32[]{:S(2)}) %collective-permute-start.17) | collective-permute-done | bytes 409632 | tf_op jit(solution)/shard_map/ppermute | solution.py:176
  158.8 5.3 %collective-permute-start.18 = (f32[160,640]{1,0:T(8,128)S(1)}, f32[160,640]{1,0:T(8,128)S(1)}, u32[]{:S(2)}, u32[]{:S(2)}) collective-permute-start(f32[160,640]{1,0:T(8,128)S(1)} %slice_bitcast_fusion), channel_id=1, source_target_pairs={{0,2},{1,3},{2,0},{3,1},{4,6},{5,7},{6,4},{7,5},{8,10},{9,11},{10,... | collective-permute-start | bytes 1228808 | tf_op jit(solution)/shard_map/ppermute | solution.py:178
  164.1 3.9 %fusion.78 = (bf16[8192,128]{1,0:T(8,128)(2,1)S(1)}, bf16[8192,128]{1,0:T(8,128)(2,1)}) fusion(bf16[8192,256]{1,0:T(8,128)(2,1)} %constant_dynamic-update-slice_fusion), kind=kLoop, calls=%fused_computation.172 | loop fusion | bytes 8388608 | tf_op jit(solution)/shard_map/slice | solution.py:194
  167.9 15.5 %collective-permute-done.18 = f32[160,640]{1,0:T(8,128)S(1)} collective-permute-done((f32[160,640]{1,0:T(8,128)S(1)}, f32[160,640]{1,0:T(8,128)S(1)}, u32[]{:S(2)}, u32[]{:S(2)}) %collective-permute-start.18) | collective-permute-done | bytes 409632 | tf_op jit(solution)/shard_map/ppermute | solution.py:178
  188.7 7.1 %collective-permute-start.20 = (bf16[160,4,128]{2,0,1:T(8,128)(2,1)S(1)}, bf16[160,4,128]{2,0,1:T(8,128)(2,1)S(1)}, u32[]{:S(2)}, u32[]{:S(2)}) collective-permute-start(bf16[160,4,128]{2,0,1:T(8,128)(2,1)S(1)} %pad_maximum_fusion.11), channel_id=1, source_target_pairs={{16,18},{17,19},{18,16},{19,17},{20,22},{21,23},{22,20},{23,21},{2... | collective-permute-start | bytes 491528 | tf_op jit(solution)/shard_map/ppermute | solution.py:201
  198.0 8.6 %collective-permute-done.20 = bf16[160,4,128]{2,0,1:T(8,128)(2,1)S(1)} collective-permute-done((bf16[160,4,128]{2,0,1:T(8,128)(2,1)S(1)}, bf16[160,4,128]{2,0,1:T(8,128)(2,1)S(1)}, u32[]{:S(2)}, u32[]{:S(2)}) %collective-permute-start.20) | collective-permute-done | bytes 163872 | tf_op jit(solution)/shard_map/ppermute | solution.py:201
  208.8 26.4 %while.15 = (s32[]{:T(128)}, f32[8,160]{1,0:T(8,128)S(1)}, f32[8,160]{1,0:T(8,128)S(1)}, f32[8,160,128]{2,1,0:T(8,128)S(1)}, bf16[4,2048,128]{2,1,0:T(8,128)(2,1...) while((s32[]{:T(128)}, f32[8,160]{1,0:T(8,128)S(1)}, ...), condition=%wide.region_3.4_spmd.clone, body=%wide.region_0.3_spmd.clone.sunk | while | flops 1363811840 | bytes 34225268 | solution.py:83
  208.9 2.7 bitcast_reduce_fusion.2
  235.5 6.9 %collective-permute-start.21 = (f32[650,128]{1,0:T(8,128)S(1)}, f32[650,128]{1,0:T(8,128)S(1)}, u32[]{:S(2)}, u32[]{:S(2)}) collective-permute-start(f32[650,128]{1,0:T(8,128)S(1)} %pad_maximum_fusion.8), channel_id=1, source_target_pairs={{16,18},{17,19},{18,16},{19,17},{20,22},{21,23},{22,20},{23,21},{2... | collective-permute-start | bytes 998408 | tf_op jit(solution)/shard_map/ppermute | solution.py:218
  243.9 11.0 %collective-permute-done.21 = f32[650,128]{1,0:T(8,128)S(1)} collective-permute-done((f32[650,128]{1,0:T(8,128)S(1)}, f32[650,128]{1,0:T(8,128)S(1)}, u32[]{:S(2)}, u32[]{:S(2)}) %collective-permute-start.21) | collective-permute-done | bytes 332832 | tf_op jit(solution)/shard_map/ppermute | solution.py:218
  255.0 4.0 %collective-permute-done.22 = f32[650,128]{1,0:T(8,128)S(1)} collective-permute-done((f32[650,128]{1,0:T(8,128)S(1)}, f32[650,128]{1,0:T(8,128)S(1)}, u32[]{:S(2)}, u32[]{:S(2)}) %collective-permute-start.22) | collective-permute-done | bytes 332832 | tf_op jit(solution)/shard_map/ppermute | solution.py:217
  (136 shorter events, 83.7 us)
Async XLA Ops:
  6.5 98.2 %all-gather.2.cloned.1.call-start = ((), (), s32[]{:S(2)}) async-start(), calls=%async_computation | async-start | bytes 3276800 | tf_op jit(solution)/shard_map/all_gather | solution.py:138
  8.4 14.3 %collective-permute-start.2 = (bf16[160,512]{1,0:T(8,128)(2,1)}, bf16[160,512]{1,0:T(8,128)(2,1)S(1)}, u32[]{:S(2)}, u32[]{:S(2)}) collective-permute-start(bf16[160,512]{1,0:T(8,128)(2,1)} %param.8), channel_id=1, source_target_pairs={{0,48},{16,32},{32,16},{48,0},{1,49},{17,33},{33,17},{49,1},{2,50}... | collective-permute-start | bytes 491528 | tf_op jit(solution)/shard_map/ppermute | solution.py:134
  10.5 14.0 %collective-permute-start.1 = (bf16[160,512]{1,0:T(8,128)(2,1)}, bf16[160,512]{1,0:T(8,128)(2,1)S(1)}, u32[]{:S(2)}, u32[]{:S(2)}) collective-permute-start(bf16[160,512]{1,0:T(8,128)(2,1)} %param.8), channel_id=1, source_target_pairs={{0,32},{16,48},{32,0},{48,16},{1,33},{17,49},{33,1},{49,17},{2,34}... | collective-permute-start | bytes 491528 | tf_op jit(solution)/shard_map/ppermute | solution.py:134
  27.1 15.4 %collective-permute-start.3 = (bf16[2,1024,128]{2,1,0:T(8,128)(2,1)S(1)}, bf16[2,1024,128]{2,1,0:T(8,128)(2,1)S(1)}, u32[]{:S(2)}, u32[]{:S(2)}) collective-permute-start(bf16[2,1024,128]{2,1,0:T(8,128)(2,1)S(1)} %copy-done.2), channel_id=1, source_target_pairs={{0,16},{16,0},{32,48},{48,32},{64,80},{80,64},{96,112},{112,96},{1... | collective-permute-start | bytes 1572872 | tf_op jit(solution)/shard_map/ppermute | solution.py:19
  44.0 11.2 %collective-permute-start.4 = (bf16[1024,256]{1,0:T(8,128)(2,1)}, bf16[1024,256]{1,0:T(8,128)(2,1)}, u32[]{:S(2)}, u32[]{:S(2)}) collective-permute-start(bf16[1024,256]{1,0:T(8,128)(2,1)} %get-tuple-element.118), channel_id=1, source_target_pairs={{0,1},{1,0},{2,3},{3,2},{4,5},{5,4},{6,7},{7,6},{8,9},{9,8},{10,11... | collective-permute-start | bytes 1572872 | tf_op jit(solution)/shard_map/ppermute | solution.py:153
  44.7 15.3 %collective-permute-start.5 = (bf16[1024,256]{1,0:T(8,128)(2,1)}, bf16[1024,256]{1,0:T(8,128)(2,1)}, u32[]{:S(2)}, u32[]{:S(2)}) collective-permute-start(bf16[1024,256]{1,0:T(8,128)(2,1)} %get-tuple-element.119), channel_id=1, source_target_pairs={{0,4},{1,5},{2,6},{3,7},{4,0},{5,1},{6,2},{7,3},{8,12},{9,13},{10,... | collective-permute-start | bytes 1572872 | tf_op jit(solution)/shard_map/ppermute | solution.py:153
  46.9 23.2 %collective-permute-start.6 = (bf16[1024,256]{1,0:T(8,128)(2,1)S(1)}, bf16[1024,256]{1,0:T(8,128)(2,1)}, u32[]{:S(2)}, u32[]{:S(2)}) collective-permute-start(bf16[1024,256]{1,0:T(8,128)(2,1)S(1)} %get-tuple-element.120), channel_id=1, source_target_pairs={{0,5},{1,4},{2,7},{3,6},{4,1},{5,0},{6,3},{7,2},{8,13},{9,12},{10,... | collective-permute-start | bytes 1572872 | tf_op jit(solution)/shard_map/ppermute | solution.py:153
  50.8 33.9 %collective-permute-start.7 = (bf16[1024,256]{1,0:T(8,128)(2,1)S(1)}, bf16[1024,256]{1,0:T(8,128)(2,1)S(1)}, u32[]{:S(2)}, u32[]{:S(2)}) collective-permute-start(bf16[1024,256]{1,0:T(8,128)(2,1)S(1)} %get-tuple-element.121), channel_id=1, source_target_pairs={{0,8},{1,9},{2,10},{3,11},{4,12},{5,13},{6,14},{7,15},{8,0},{9,1},... | collective-permute-start | bytes 1572872 | tf_op jit(solution)/shard_map/ppermute | solution.py:153
  54.2 40.8 %collective-permute-start.8 = (bf16[1024,256]{1,0:T(8,128)(2,1)S(1)}, bf16[1024,256]{1,0:T(8,128)(2,1)S(1)}, u32[]{:S(2)}, u32[]{:S(2)}) collective-permute-start(bf16[1024,256]{1,0:T(8,128)(2,1)S(1)} %get-tuple-element.122), channel_id=1, source_target_pairs={{0,9},{1,8},{2,11},{3,10},{4,13},{5,12},{6,15},{7,14},{8,1},{9,0},... | collective-permute-start | bytes 1572872 | tf_op jit(solution)/shard_map/ppermute | solution.py:153
  55.1 40.7 %collective-permute-start.9 = (bf16[1024,256]{1,0:T(8,128)(2,1)S(1)}, bf16[1024,256]{1,0:T(8,128)(2,1)S(1)}, u32[]{:S(2)}, u32[]{:S(2)}) collective-permute-start(bf16[1024,256]{1,0:T(8,128)(2,1)S(1)} %fusion.50), channel_id=1, source_target_pairs={{0,12},{1,13},{2,14},{3,15},{4,8},{5,9},{6,10},{7,11},{8,4},{9,5},... | collective-permute-start | bytes 1572872 | tf_op jit(solution)/shard_map/ppermute | solution.py:153
  59.9 43.9 %collective-permute-start.10 = (bf16[1024,256]{1,0:T(8,128)(2,1)S(1)}, bf16[1024,256]{1,0:T(8,128)(2,1)S(1)}, u32[]{:S(2)}, u32[]{:S(2)}) collective-permute-start(bf16[1024,256]{1,0:T(8,128)(2,1)S(1)} %get-tuple-element.117), channel_id=1, source_target_pairs={{0,13},{1,12},{2,15},{3,14},{4,9},{5,8},{6,11},{7,10},{8,5},{9,4},... | collective-permute-start | bytes 1572872 | tf_op jit(solution)/shard_map/ppermute | solution.py:153
  111.9 12.4 %collective-permute-start.12 = (bf16[2,160,640]{2,1,0:T(8,128)(2,1)S(1)}, bf16[2,160,640]{2,1,0:T(8,128)(2,1)S(1)}, u32[]{:S(2)}, u32[]{:S(2)}) collective-permute-start(bf16[2,160,640]{2,1,0:T(8,128)(2,1)S(1)} %pad_maximum_fusion.2), channel_id=1, source_target_pairs={{0,4},{1,5},{2,6},{3,7},{4,0},{5,1},{6,2},{7,3},{8,12},{9,13},{10,... | collective-permute-start | bytes 1228808 | tf_op jit(solution)/shard_map/ppermute | solution.py:176
  112.4 19.4 %collective-permute-start.13 = (bf16[2,160,640]{2,1,0:T(8,128)(2,1)S(1)}, bf16[2,160,640]{2,1,0:T(8,128)(2,1)S(1)}, u32[]{:S(2)}, u32[]{:S(2)}) collective-permute-start(bf16[2,160,640]{2,1,0:T(8,128)(2,1)S(1)} %pad_maximum_fusion.3), channel_id=1, source_target_pairs={{0,5},{1,4},{2,7},{3,6},{4,1},{5,0},{6,3},{7,2},{8,13},{9,12},{10,... | collective-permute-start | bytes 1228808 | tf_op jit(solution)/shard_map/ppermute | solution.py:176
  114.6 29.8 %collective-permute-start.14 = (bf16[2,160,640]{2,1,0:T(8,128)(2,1)}, bf16[2,160,640]{2,1,0:T(8,128)(2,1)S(1)}, u32[]{:S(2)}, u32[]{:S(2)}) collective-permute-start(bf16[2,160,640]{2,1,0:T(8,128)(2,1)} %pad_maximum_fusion.4), channel_id=1, source_target_pairs={{0,8},{1,9},{2,10},{3,11},{4,12},{5,13},{6,14},{7,15},{8,0},{9,1},... | collective-permute-start | bytes 1228808 | tf_op jit(solution)/shard_map/ppermute | solution.py:176
  118.2 33.6 %collective-permute-start.15 = (bf16[2,160,640]{2,1,0:T(8,128)(2,1)}, bf16[2,160,640]{2,1,0:T(8,128)(2,1)S(1)}, u32[]{:S(2)}, u32[]{:S(2)}) collective-permute-start(bf16[2,160,640]{2,1,0:T(8,128)(2,1)} %pad_maximum_fusion.5), channel_id=1, source_target_pairs={{0,9},{1,8},{2,11},{3,10},{4,13},{5,12},{6,15},{7,14},{8,1},{9,0},... | collective-permute-start | bytes 1228808 | tf_op jit(solution)/shard_map/ppermute | solution.py:176
  119.6 32.2 %collective-permute-start.16 = (bf16[2,160,640]{2,1,0:T(8,128)(2,1)}, bf16[2,160,640]{2,1,0:T(8,128)(2,1)S(1)}, u32[]{:S(2)}, u32[]{:S(2)}) collective-permute-start(bf16[2,160,640]{2,1,0:T(8,128)(2,1)} %pad_maximum_fusion.6), channel_id=1, source_target_pairs={{0,12},{1,13},{2,14},{3,15},{4,8},{5,9},{6,10},{7,11},{8,4},{9,5},... | collective-permute-start | bytes 1228808 | tf_op jit(solution)/shard_map/ppermute | solution.py:176
  124.3 34.0 %collective-permute-start.17 = (bf16[2,160,640]{2,1,0:T(8,128)(2,1)}, bf16[2,160,640]{2,1,0:T(8,128)(2,1)S(1)}, u32[]{:S(2)}, u32[]{:S(2)}) collective-permute-start(bf16[2,160,640]{2,1,0:T(8,128)(2,1)} %pad_maximum_fusion.7), channel_id=1, source_target_pairs={{0,13},{1,12},{2,15},{3,14},{4,9},{5,8},{6,11},{7,10},{8,5},{9,4},... | collective-permute-start | bytes 1228808 | tf_op jit(solution)/shard_map/ppermute | solution.py:176
  131.8 26.6 %collective-permute-start.11 = (bf16[2,160,640]{2,1,0:T(8,128)(2,1)}, bf16[2,160,640]{2,1,0:T(8,128)(2,1)S(1)}, u32[]{:S(2)}, u32[]{:S(2)}) collective-permute-start(bf16[2,160,640]{2,1,0:T(8,128)(2,1)} %pad_maximum_fusion.1), channel_id=1, source_target_pairs={{0,1},{1,0},{2,3},{3,2},{4,5},{5,4},{6,7},{7,6},{8,9},{9,8},{10,11... | collective-permute-start | bytes 1228808 | tf_op jit(solution)/shard_map/ppermute | solution.py:176
  158.8 24.6 %collective-permute-start.18 = (f32[160,640]{1,0:T(8,128)S(1)}, f32[160,640]{1,0:T(8,128)S(1)}, u32[]{:S(2)}, u32[]{:S(2)}) collective-permute-start(f32[160,640]{1,0:T(8,128)S(1)} %slice_bitcast_fusion), channel_id=1, source_target_pairs={{0,2},{1,3},{2,0},{3,1},{4,6},{5,7},{6,4},{7,5},{8,10},{9,11},{10,... | collective-permute-start | bytes 1228808 | tf_op jit(solution)/shard_map/ppermute | solution.py:178
  187.2 8.9 %collective-permute-start.23 = (bf16[160,1,128]{2,0,1:T(8,128)(2,1)S(1)}, bf16[160,1,128]{2,0,1:T(8,128)(2,1)S(1)}, u32[]{:S(2)}, u32[]{:S(2)}) collective-permute-start(bf16[160,1,128]{2,0,1:T(8,128)(2,1)S(1)} %bitcast.141), channel_id=1, source_target_pairs={{0,16},{16,0},{32,48},{48,32},{64,80},{80,64},{96,112},{112,96},{1... | collective-permute-start | bytes 122888 | tf_op jit(solution)/shard_map/ppermute | solution.py:19
  188.7 17.9 %collective-permute-start.20 = (bf16[160,4,128]{2,0,1:T(8,128)(2,1)S(1)}, bf16[160,4,128]{2,0,1:T(8,128)(2,1)S(1)}, u32[]{:S(2)}, u32[]{:S(2)}) collective-permute-start(bf16[160,4,128]{2,0,1:T(8,128)(2,1)S(1)} %pad_maximum_fusion.11), channel_id=1, source_target_pairs={{16,18},{17,19},{18,16},{19,17},{20,22},{21,23},{22,20},{23,21},{2... | collective-permute-start | bytes 491528 | tf_op jit(solution)/shard_map/ppermute | solution.py:201
  195.8 12.9 %collective-permute-start.19 = (bf16[160,4,128]{2,0,1:T(8,128)(2,1)S(1)}, bf16[160,4,128]{2,0,1:T(8,128)(2,1)S(1)}, u32[]{:S(2)}, u32[]{:S(2)}) collective-permute-start(bf16[160,4,128]{2,0,1:T(8,128)(2,1)S(1)} %pad_maximum_fusion.11), channel_id=1, source_target_pairs={{0,18},{1,19},{2,16},{3,17},{4,22},{5,23},{6,20},{7,21},{8,26},{9,... | collective-permute-start | bytes 491528 | tf_op jit(solution)/shard_map/ppermute | solution.py:200
  235.5 19.3 %collective-permute-start.21 = (f32[650,128]{1,0:T(8,128)S(1)}, f32[650,128]{1,0:T(8,128)S(1)}, u32[]{:S(2)}, u32[]{:S(2)}) collective-permute-start(f32[650,128]{1,0:T(8,128)S(1)} %pad_maximum_fusion.8), channel_id=1, source_target_pairs={{16,18},{17,19},{18,16},{19,17},{20,22},{21,23},{22,20},{23,21},{2... | collective-permute-start | bytes 998408 | tf_op jit(solution)/shard_map/ppermute | solution.py:218
  242.6 16.4 %collective-permute-start.22 = (f32[650,128]{1,0:T(8,128)S(1)}, f32[650,128]{1,0:T(8,128)S(1)}, u32[]{:S(2)}, u32[]{:S(2)}) collective-permute-start(f32[650,128]{1,0:T(8,128)S(1)} %pad_maximum_fusion.9), channel_id=1, source_target_pairs={{0,16},{1,17},{2,18},{3,19},{4,20},{5,21},{6,22},{7,23},{8,24},{9,... | collective-permute-start | bytes 998408 | tf_op jit(solution)/shard_map/ppermute | solution.py:217
  (9 other events, 204.1 us)
Sparse Core Ops, SparseCore 0:
  27.2 40.2 all-gather.1

commit v6 on v5

--- a/solution.py
+++ b/solution.py
@@ -127,6 +127,8 @@
     segments = w_keyval.shape[1] // HD
     scale = 1.0 / HD**0.5
     half_bit = 2
+    other_cache = partner(prefix_cache, ROW, 0, n_row)
+    hidden, other_cache = lax.optimization_barrier((hidden, other_cache))
     n_low = n_row // 4
     low_id = lax.axis_index("zl")
     stacked = [hidden]
@@ -139,7 +141,6 @@
     odd = row_id % 2
     is_even = odd == 0
     handled = col_id ^ (half_bit * odd)
-    other_cache = partner(prefix_cache, ROW, 0, n_row)
     cache_keys = jnp.where(is_even, prefix_cache, other_cache)
     cache_values = jnp.where(is_even, other_cache, prefix_cache)
     kv_block = jnp.concatenate([cache_keys, cache_values], axis=-1)

time: 268 us -> 280 us (1.045)
  waiting for transfers between devices: 120 us -> 126 us
  starting transfers between devices: 47.3 us -> 50.1 us
    ppermute x2, waiting for transfers between devices: 0.01 us -> 12.1 us  [partner(): return lax.ppermute(value, axis, pairs)]
    ppermute x2, starting transfers between devices: 2.31 us -> 9.01 us  [partner(): return lax.ppermute(value, axis, pairs)]
    ppermute x1, waiting for transfers between devices: 15.5 us -> 10.9 us  [per_device(): lax.ppermute(half_sum[1], COL, [(c, c ^ half_bit) for c in range(n_col)])]
    ppermute x1, waiting for transfers between devices: 4 us -> 0.01 us  [per_device(): lax.ppermute(pack_state(theirs), axes, back)]
    ppermute x1, waiting for transfers between devices: 8.56 us -> 11.8 us  [per_device(): q_same = lax.ppermute(query, axes, same)]
  transfers between devices with their start and end apart: 25 -> 25, of which waited for: 17 -> 16; matrix products, arithmetic and copies ran while one was open for 11% -> 11% of each run, Pallas kernels for 0% -> 0%
where the time goes in v6:
time: 280 us; the launch traced here: 277 us
  waiting for transfers between devices  126 us (45%)
  starting transfers between devices  50.1 us (18%)
  between operations  28.7 us (10%)
  matrix products  25.2 us (9%)
  other arithmetic  24.4 us (9%)
  local copies, waits for them, and re-layouts  22.3 us (8%)
    ppermute x7, waiting for transfers between devices, per_device(): blocks.append(lax.ppermute(piece, COL, pairs))  35.9 us
    ppermute x7, waiting for transfers between devices, per_device(): got = lax.ppermute(piece, COL, [(c, c ^ mask) for c in range(n_col)])  29.2 us
    ppermute x1, waiting for transfers between devices, per_device(): lax.ppermute(pack_state(mine), axes, same)  12.5 us
    ppermute x2, waiting for transfers between devices, partner(): return lax.ppermute(value, axis, pairs)  12.1 us
    ppermute x1, waiting for transfers between devices, per_device(): q_same = lax.ppermute(query, axes, same)  11.8 us
    ppermute x1, waiting for transfers between devices, per_device(): lax.ppermute(half_sum[1], COL, [(c, c ^ half_bit) for c in range(n_col)])  10.9 us
    ppermute x7, starting transfers between devices, per_device(): got = lax.ppermute(piece, COL, [(c, c ^ mask) for c in range(n_col)])  10.9 us
    ppermute x3, waiting for transfers between devices, per_device(): lax.ppermute(hidden, 'zl', [(i, i ^ mask) for i in range(n_low)])  10.8 us
  transfers between devices with their start and end apart: 25, of which 16 were waited for; matrix products, arithmetic and copies ran while one was open for 11% of the time, Pallas kernels for 0%

profile of v6, /device:TPU:32, one launch (start us, length us, event | category | flops | bytes accessed | tf_op | source)
XLA Modules:
  0.0 276.7 jit_solution(15055549753184023105)
XLA Ops:
  8.4 12.1 %collective-permute-done = bf16[2,1024,128]{2,1,0:T(8,128)(2,1)S(1)} collective-permute-done((bf16[2,1024,128]{2,1,0:T(8,128)(2,1)}, bf16[2,1024,128]{2,1,0:T(8,128)(2,1)S(1)}, u32[]{:S(2)}, u32[]{:S(2)}) %collective-permute-start) | collective-permute-done | bytes 524320 | tf_op jit(solution)/shard_map/ppermute | solution.py:19
  25.4 9.0 %collective-permute-done.3 = bf16[160,512]{1,0:T(8,128)(2,1)S(1)} collective-permute-done((bf16[160,512]{1,0:T(8,128)(2,1)}, bf16[160,512]{1,0:T(8,128)(2,1)S(1)}, u32[]{:S(2)}, u32[]{:S(2)}) %collective-permute-start.3) | collective-permute-done | bytes 163872 | tf_op jit(solution)/shard_map/ppermute | solution.py:136
  60.4 3.3 %collective-permute-start.7 = (bf16[1024,256]{1,0:T(8,128)(2,1)S(1)}, bf16[1024,256]{1,0:T(8,128)(2,1)S(1)}, u32[]{:S(2)}, u32[]{:S(2)}) collective-permute-start(bf16[1024,256]{1,0:T(8,128)(2,1)S(1)} %get-tuple-element.125), channel_id=1, source_target_pairs={{0,8},{1,9},{2,10},{3,11},{4,12},{5,13},{6,14},{7,15},{8,0},{9,1},... | collective-permute-start | bytes 1572872 | tf_op jit(solution)/shard_map/ppermute | solution.py:154
  64.7 2.9 %collective-permute-start.9 = (bf16[1024,256]{1,0:T(8,128)(2,1)S(1)}, bf16[1024,256]{1,0:T(8,128)(2,1)S(1)}, u32[]{:S(2)}, u32[]{:S(2)}) collective-permute-start(bf16[1024,256]{1,0:T(8,128)(2,1)S(1)} %fusion.50), channel_id=1, source_target_pairs={{0,12},{1,13},{2,14},{3,15},{4,8},{5,9},{6,10},{7,11},{8,4},{9,5},... | collective-permute-start | bytes 1572872 | tf_op jit(solution)/shard_map/ppermute | solution.py:154
  73.1 6.6 %collective-permute-done.6 = bf16[1024,256]{1,0:T(8,128)(2,1)} collective-permute-done((bf16[1024,256]{1,0:T(8,128)(2,1)S(1)}, bf16[1024,256]{1,0:T(8,128)(2,1)}, u32[]{:S(2)}, u32[]{:S(2)}) %collective-permute-start.6) | collective-permute-done | bytes 524320 | tf_op jit(solution)/shard_map/ppermute | solution.py:154
  81.6 12.7 %collective-permute-done.7 = bf16[1024,256]{1,0:T(8,128)(2,1)S(1)} collective-permute-done((bf16[1024,256]{1,0:T(8,128)(2,1)S(1)}, bf16[1024,256]{1,0:T(8,128)(2,1)S(1)}, u32[]{:S(2)}, u32[]{:S(2)}) %collective-permute-start.7) | collective-permute-done | bytes 524320 | tf_op jit(solution)/shard_map/ppermute | solution.py:154
  95.2 9.5 %collective-permute-done.8 = bf16[1024,256]{1,0:T(8,128)(2,1)S(1)} collective-permute-done((bf16[1024,256]{1,0:T(8,128)(2,1)S(1)}, bf16[1024,256]{1,0:T(8,128)(2,1)S(1)}, u32[]{:S(2)}, u32[]{:S(2)}) %collective-permute-start.8) | collective-permute-done | bytes 524320 | tf_op jit(solution)/shard_map/ppermute | solution.py:154
  106.3 7.2 %collective-permute-done.10 = bf16[1024,256]{1,0:T(8,128)(2,1)S(1)} collective-permute-done((bf16[1024,256]{1,0:T(8,128)(2,1)S(1)}, bf16[1024,256]{1,0:T(8,128)(2,1)S(1)}, u32[]{:S(2)}, u32[]{:S(2)}) %collective-permute-start.10) | collective-permute-done | bytes 524320 | tf_op jit(solution)/shard_map/ppermute | solution.py:154
  114.3 4.0 %fusion.28 = f32[2560,640]{1,0:T(8,128)S(1)} fusion(bf16[2560,512]{1,0:T(8,128)(2,1)} %all-gather.2.cloned.1.call-done, bf16[512,128]{1,0:T(8,128)(2,1)S(1)} %copy-done.5, bf16[512,512]{1,0:T(8,128)(2,1)} %param.9), kind=kOutput, calls=%fused_computation.51 | convolution fusion | flops 1679032320 | bytes 9830400 | tf_op jit(solution)/shard_map/dot_general | solution.py:159
  124.2 2.8 %collective-permute-start.14 = (bf16[2,160,640]{2,1,0:T(8,128)(2,1)}, bf16[2,160,640]{2,1,0:T(8,128)(2,1)S(1)}, u32[]{:S(2)}, u32[]{:S(2)}) collective-permute-start(bf16[2,160,640]{2,1,0:T(8,128)(2,1)} %pad_maximum_fusion.4), channel_id=1, source_target_pairs={{0,8},{1,9},{2,10},{3,11},{4,12},{5,13},{6,14},{7,15},{8,0},{9,1},... | collective-permute-start | bytes 1228808 | tf_op jit(solution)/shard_map/ppermute | solution.py:177
  129.2 3.0 %collective-permute-start.16 = (bf16[2,160,640]{2,1,0:T(8,128)(2,1)}, bf16[2,160,640]{2,1,0:T(8,128)(2,1)S(1)}, u32[]{:S(2)}, u32[]{:S(2)}) collective-permute-start(bf16[2,160,640]{2,1,0:T(8,128)(2,1)} %pad_maximum_fusion.6), channel_id=1, source_target_pairs={{0,12},{1,13},{2,14},{3,15},{4,8},{5,9},{6,10},{7,11},{8,4},{9,5},... | collective-permute-start | bytes 1228808 | tf_op jit(solution)/shard_map/ppermute | solution.py:177
  135.3 6.1 %collective-permute-done.13 = bf16[2,160,640]{2,1,0:T(8,128)(2,1)S(1)} collective-permute-done((bf16[2,160,640]{2,1,0:T(8,128)(2,1)S(1)}, bf16[2,160,640]{2,1,0:T(8,128)(2,1)S(1)}, u32[]{:S(2)}, u32[]{:S(2)}) %collective-permute-start.13) | collective-permute-done | bytes 409632 | tf_op jit(solution)/shard_map/ppermute | solution.py:177
  145.1 8.9 %collective-permute-done.14 = bf16[2,160,640]{2,1,0:T(8,128)(2,1)S(1)} collective-permute-done((bf16[2,160,640]{2,1,0:T(8,128)(2,1)}, bf16[2,160,640]{2,1,0:T(8,128)(2,1)S(1)}, u32[]{:S(2)}, u32[]{:S(2)}) %collective-permute-start.14) | collective-permute-done | bytes 409632 | tf_op jit(solution)/shard_map/ppermute | solution.py:177
  154.0 7.4 %collective-permute-done.15 = bf16[2,160,640]{2,1,0:T(8,128)(2,1)S(1)} collective-permute-done((bf16[2,160,640]{2,1,0:T(8,128)(2,1)}, bf16[2,160,640]{2,1,0:T(8,128)(2,1)S(1)}, u32[]{:S(2)}, u32[]{:S(2)}) %collective-permute-start.15) | collective-permute-done | bytes 409632 | tf_op jit(solution)/shard_map/ppermute | solution.py:177
  161.4 6.6 %collective-permute-done.17 = bf16[2,160,640]{2,1,0:T(8,128)(2,1)S(1)} collective-permute-done((bf16[2,160,640]{2,1,0:T(8,128)(2,1)}, bf16[2,160,640]{2,1,0:T(8,128)(2,1)S(1)}, u32[]{:S(2)}, u32[]{:S(2)}) %collective-permute-start.17) | collective-permute-done | bytes 409632 | tf_op jit(solution)/shard_map/ppermute | solution.py:177
  168.4 5.1 %collective-permute-start.18 = (f32[160,640]{1,0:T(8,128)S(1)}, f32[160,640]{1,0:T(8,128)S(1)}, u32[]{:S(2)}, u32[]{:S(2)}) collective-permute-start(f32[160,640]{1,0:T(8,128)S(1)} %slice_bitcast_fusion), channel_id=1, source_target_pairs={{0,2},{1,3},{2,0},{3,1},{4,6},{5,7},{6,4},{7,5},{8,10},{9,11},{10,... | collective-permute-start | bytes 1228808 | tf_op jit(solution)/shard_map/ppermute | solution.py:179
  173.6 3.9 %fusion.78 = (bf16[8192,128]{1,0:T(8,128)(2,1)S(1)}, bf16[8192,128]{1,0:T(8,128)(2,1)}) fusion(bf16[8192,256]{1,0:T(8,128)(2,1)} %constant_dynamic-update-slice_fusion), kind=kLoop, calls=%fused_computation.172 | loop fusion | bytes 8388608 | tf_op jit(solution)/shard_map/slice | solution.py:195
  177.4 10.9 %collective-permute-done.18 = f32[160,640]{1,0:T(8,128)S(1)} collective-permute-done((f32[160,640]{1,0:T(8,128)S(1)}, f32[160,640]{1,0:T(8,128)S(1)}, u32[]{:S(2)}, u32[]{:S(2)}) %collective-permute-start.18) | collective-permute-done | bytes 409632 | tf_op jit(solution)/shard_map/ppermute | solution.py:179
  192.2 7.1 %collective-permute-start.23 = (bf16[160,1,128]{2,0,1:T(8,128)(2,1)S(1)}, bf16[160,1,128]{2,0,1:T(8,128)(2,1)S(1)}, u32[]{:S(2)}, u32[]{:S(2)}) collective-permute-start(bf16[160,1,128]{2,0,1:T(8,128)(2,1)S(1)} %bitcast.141), channel_id=1, source_target_pairs={{0,16},{16,0},{32,48},{48,32},{64,80},{80,64},{96,112},{112,96},{1... | collective-permute-start | bytes 122888 | tf_op jit(solution)/shard_map/ppermute | solution.py:19
  200.7 5.1 %collective-permute-start.20 = (bf16[160,4,128]{2,0,1:T(8,128)(2,1)S(1)}, bf16[160,4,128]{2,0,1:T(8,128)(2,1)S(1)}, u32[]{:S(2)}, u32[]{:S(2)}) collective-permute-start(bf16[160,4,128]{2,0,1:T(8,128)(2,1)S(1)} %pad_maximum_fusion.11), channel_id=1, source_target_pairs={{16,18},{17,19},{18,16},{19,17},{20,22},{21,23},{22,20},{23,21},{2... | collective-permute-start | bytes 491528 | tf_op jit(solution)/shard_map/ppermute | solution.py:202
  207.9 11.8 %collective-permute-done.20 = bf16[160,4,128]{2,0,1:T(8,128)(2,1)S(1)} collective-permute-done((bf16[160,4,128]{2,0,1:T(8,128)(2,1)S(1)}, bf16[160,4,128]{2,0,1:T(8,128)(2,1)S(1)}, u32[]{:S(2)}, u32[]{:S(2)}) %collective-permute-start.20) | collective-permute-done | bytes 163872 | tf_op jit(solution)/shard_map/ppermute | solution.py:202
  222.6 26.4 %while.15 = (s32[]{:T(128)}, f32[8,160]{1,0:T(8,128)S(1)}, f32[8,160]{1,0:T(8,128)S(1)}, f32[8,160,128]{2,1,0:T(8,128)S(1)}, bf16[4,2048,128]{2,1,0:T(8,128)(2,1...) while((s32[]{:T(128)}, f32[8,160]{1,0:T(8,128)S(1)}, ...), condition=%wide.region_3.4_spmd.clone, body=%wide.region_0.3_spmd.clone.sunk | while | flops 1363811840 | bytes 34225268 | solution.py:83
  249.2 4.9 %collective-permute-start.21 = (f32[650,128]{1,0:T(8,128)S(1)}, f32[650,128]{1,0:T(8,128)S(1)}, u32[]{:S(2)}, u32[]{:S(2)}) collective-permute-start(f32[650,128]{1,0:T(8,128)S(1)} %pad_maximum_fusion.8), channel_id=1, source_target_pairs={{16,18},{17,19},{18,16},{19,17},{20,22},{21,23},{22,20},{23,21},{2... | collective-permute-start | bytes 998408 | tf_op jit(solution)/shard_map/ppermute | solution.py:219
  255.6 12.5 %collective-permute-done.21 = f32[650,128]{1,0:T(8,128)S(1)} collective-permute-done((f32[650,128]{1,0:T(8,128)S(1)}, f32[650,128]{1,0:T(8,128)S(1)}, u32[]{:S(2)}, u32[]{:S(2)}) %collective-permute-start.21) | collective-permute-done | bytes 332832 | tf_op jit(solution)/shard_map/ppermute | solution.py:219
  (136 shorter events, 84.6 us)
Async XLA Ops:
  6.5 107.8 %all-gather.2.cloned.1.call-start = ((), (), s32[]{:S(2)}) async-start(), calls=%async_computation | async-start | bytes 3276800 | tf_op jit(solution)/shard_map/all_gather | solution.py:140
  6.5 14.0 %collective-permute-start = (bf16[2,1024,128]{2,1,0:T(8,128)(2,1)}, bf16[2,1024,128]{2,1,0:T(8,128)(2,1)S(1)}, u32[]{:S(2)}, u32[]{:S(2)}) collective-permute-start(bf16[2,1024,128]{2,1,0:T(8,128)(2,1)} %param.11), channel_id=1, source_target_pairs={{0,16},{16,0},{32,48},{48,32},{64,80},{80,64},{96,112},{112,96},{1... | collective-permute-start | bytes 1572872 | tf_op jit(solution)/shard_map/ppermute | solution.py:19
  20.5 14.0 %collective-permute-start.3 = (bf16[160,512]{1,0:T(8,128)(2,1)}, bf16[160,512]{1,0:T(8,128)(2,1)S(1)}, u32[]{:S(2)}, u32[]{:S(2)}) collective-permute-start(bf16[160,512]{1,0:T(8,128)(2,1)} %param.8), channel_id=1, source_target_pairs={{0,48},{16,32},{32,16},{48,0},{1,49},{17,33},{33,17},{49,1},{2,50}... | collective-permute-start | bytes 491528 | tf_op jit(solution)/shard_map/ppermute | solution.py:136
  22.6 13.6 %collective-permute-start.2 = (bf16[160,512]{1,0:T(8,128)(2,1)}, bf16[160,512]{1,0:T(8,128)(2,1)S(1)}, u32[]{:S(2)}, u32[]{:S(2)}) collective-permute-start(bf16[160,512]{1,0:T(8,128)(2,1)} %param.8), channel_id=1, source_target_pairs={{0,32},{16,48},{32,0},{48,16},{1,33},{17,49},{33,1},{49,17},{2,34}... | collective-permute-start | bytes 491528 | tf_op jit(solution)/shard_map/ppermute | solution.py:136
  23.8 12.4 %collective-permute-start.1 = (bf16[160,512]{1,0:T(8,128)(2,1)}, bf16[160,512]{1,0:T(8,128)(2,1)S(1)}, u32[]{:S(2)}, u32[]{:S(2)}) collective-permute-start(bf16[160,512]{1,0:T(8,128)(2,1)} %param.8), channel_id=1, source_target_pairs={{0,16},{16,0},{32,48},{48,32},{1,17},{17,1},{33,49},{49,33},{2,18}... | collective-permute-start | bytes 491528 | tf_op jit(solution)/shard_map/ppermute | solution.py:136
  54.3 15.3 %collective-permute-start.5 = (bf16[1024,256]{1,0:T(8,128)(2,1)}, bf16[1024,256]{1,0:T(8,128)(2,1)}, u32[]{:S(2)}, u32[]{:S(2)}) collective-permute-start(bf16[1024,256]{1,0:T(8,128)(2,1)} %get-tuple-element.123), channel_id=1, source_target_pairs={{0,4},{1,5},{2,6},{3,7},{4,0},{5,1},{6,2},{7,3},{8,12},{9,13},{10,... | collective-permute-start | bytes 1572872 | tf_op jit(solution)/shard_map/ppermute | solution.py:154
  56.5 23.2 %collective-permute-start.6 = (bf16[1024,256]{1,0:T(8,128)(2,1)S(1)}, bf16[1024,256]{1,0:T(8,128)(2,1)}, u32[]{:S(2)}, u32[]{:S(2)}) collective-permute-start(bf16[1024,256]{1,0:T(8,128)(2,1)S(1)} %get-tuple-element.124), channel_id=1, source_target_pairs={{0,5},{1,4},{2,7},{3,6},{4,1},{5,0},{6,3},{7,2},{8,13},{9,12},{10,... | collective-permute-start | bytes 1572872 | tf_op jit(solution)/shard_map/ppermute | solution.py:154
  60.4 33.9 %collective-permute-start.7 = (bf16[1024,256]{1,0:T(8,128)(2,1)S(1)}, bf16[1024,256]{1,0:T(8,128)(2,1)S(1)}, u32[]{:S(2)}, u32[]{:S(2)}) collective-permute-start(bf16[1024,256]{1,0:T(8,128)(2,1)S(1)} %get-tuple-element.125), channel_id=1, source_target_pairs={{0,8},{1,9},{2,10},{3,11},{4,12},{5,13},{6,14},{7,15},{8,0},{9,1},... | collective-permute-start | bytes 1572872 | tf_op jit(solution)/shard_map/ppermute | solution.py:154
  63.8 40.8 %collective-permute-start.8 = (bf16[1024,256]{1,0:T(8,128)(2,1)S(1)}, bf16[1024,256]{1,0:T(8,128)(2,1)S(1)}, u32[]{:S(2)}, u32[]{:S(2)}) collective-permute-start(bf16[1024,256]{1,0:T(8,128)(2,1)S(1)} %get-tuple-element.126), channel_id=1, source_target_pairs={{0,9},{1,8},{2,11},{3,10},{4,13},{5,12},{6,15},{7,14},{8,1},{9,0},... | collective-permute-start | bytes 1572872 | tf_op jit(solution)/shard_map/ppermute | solution.py:154
  64.7 40.7 %collective-permute-start.9 = (bf16[1024,256]{1,0:T(8,128)(2,1)S(1)}, bf16[1024,256]{1,0:T(8,128)(2,1)S(1)}, u32[]{:S(2)}, u32[]{:S(2)}) collective-permute-start(bf16[1024,256]{1,0:T(8,128)(2,1)S(1)} %fusion.50), channel_id=1, source_target_pairs={{0,12},{1,13},{2,14},{3,15},{4,8},{5,9},{6,10},{7,11},{8,4},{9,5},... | collective-permute-start | bytes 1572872 | tf_op jit(solution)/shard_map/ppermute | solution.py:154
  69.6 43.9 %collective-permute-start.10 = (bf16[1024,256]{1,0:T(8,128)(2,1)S(1)}, bf16[1024,256]{1,0:T(8,128)(2,1)S(1)}, u32[]{:S(2)}, u32[]{:S(2)}) collective-permute-start(bf16[1024,256]{1,0:T(8,128)(2,1)S(1)} %get-tuple-element.121), channel_id=1, source_target_pairs={{0,13},{1,12},{2,15},{3,14},{4,9},{5,8},{6,11},{7,10},{8,5},{9,4},... | collective-permute-start | bytes 1572872 | tf_op jit(solution)/shard_map/ppermute | solution.py:154
  121.5 12.4 %collective-permute-start.12 = (bf16[2,160,640]{2,1,0:T(8,128)(2,1)S(1)}, bf16[2,160,640]{2,1,0:T(8,128)(2,1)S(1)}, u32[]{:S(2)}, u32[]{:S(2)}) collective-permute-start(bf16[2,160,640]{2,1,0:T(8,128)(2,1)S(1)} %pad_maximum_fusion.2), channel_id=1, source_target_pairs={{0,4},{1,5},{2,6},{3,7},{4,0},{5,1},{6,2},{7,3},{8,12},{9,13},{10,... | collective-permute-start | bytes 1228808 | tf_op jit(solution)/shard_map/ppermute | solution.py:177
  122.0 19.4 %collective-permute-start.13 = (bf16[2,160,640]{2,1,0:T(8,128)(2,1)S(1)}, bf16[2,160,640]{2,1,0:T(8,128)(2,1)S(1)}, u32[]{:S(2)}, u32[]{:S(2)}) collective-permute-start(bf16[2,160,640]{2,1,0:T(8,128)(2,1)S(1)} %pad_maximum_fusion.3), channel_id=1, source_target_pairs={{0,5},{1,4},{2,7},{3,6},{4,1},{5,0},{6,3},{7,2},{8,13},{9,12},{10,... | collective-permute-start | bytes 1228808 | tf_op jit(solution)/shard_map/ppermute | solution.py:177
  124.2 29.8 %collective-permute-start.14 = (bf16[2,160,640]{2,1,0:T(8,128)(2,1)}, bf16[2,160,640]{2,1,0:T(8,128)(2,1)S(1)}, u32[]{:S(2)}, u32[]{:S(2)}) collective-permute-start(bf16[2,160,640]{2,1,0:T(8,128)(2,1)} %pad_maximum_fusion.4), channel_id=1, source_target_pairs={{0,8},{1,9},{2,10},{3,11},{4,12},{5,13},{6,14},{7,15},{8,0},{9,1},... | collective-permute-start | bytes 1228808 | tf_op jit(solution)/shard_map/ppermute | solution.py:177
  127.8 33.6 %collective-permute-start.15 = (bf16[2,160,640]{2,1,0:T(8,128)(2,1)}, bf16[2,160,640]{2,1,0:T(8,128)(2,1)S(1)}, u32[]{:S(2)}, u32[]{:S(2)}) collective-permute-start(bf16[2,160,640]{2,1,0:T(8,128)(2,1)} %pad_maximum_fusion.5), channel_id=1, source_target_pairs={{0,9},{1,8},{2,11},{3,10},{4,13},{5,12},{6,15},{7,14},{8,1},{9,0},... | collective-permute-start | bytes 1228808 | tf_op jit(solution)/shard_map/ppermute | solution.py:177
  129.2 32.2 %collective-permute-start.16 = (bf16[2,160,640]{2,1,0:T(8,128)(2,1)}, bf16[2,160,640]{2,1,0:T(8,128)(2,1)S(1)}, u32[]{:S(2)}, u32[]{:S(2)}) collective-permute-start(bf16[2,160,640]{2,1,0:T(8,128)(2,1)} %pad_maximum_fusion.6), channel_id=1, source_target_pairs={{0,12},{1,13},{2,14},{3,15},{4,8},{5,9},{6,10},{7,11},{8,4},{9,5},... | collective-permute-start | bytes 1228808 | tf_op jit(solution)/shard_map/ppermute | solution.py:177
  133.9 34.0 %collective-permute-start.17 = (bf16[2,160,640]{2,1,0:T(8,128)(2,1)}, bf16[2,160,640]{2,1,0:T(8,128)(2,1)S(1)}, u32[]{:S(2)}, u32[]{:S(2)}) collective-permute-start(bf16[2,160,640]{2,1,0:T(8,128)(2,1)} %pad_maximum_fusion.7), channel_id=1, source_target_pairs={{0,13},{1,12},{2,15},{3,14},{4,9},{5,8},{6,11},{7,10},{8,5},{9,4},... | collective-permute-start | bytes 1228808 | tf_op jit(solution)/shard_map/ppermute | solution.py:177
  141.4 26.6 %collective-permute-start.11 = (bf16[2,160,640]{2,1,0:T(8,128)(2,1)}, bf16[2,160,640]{2,1,0:T(8,128)(2,1)S(1)}, u32[]{:S(2)}, u32[]{:S(2)}) collective-permute-start(bf16[2,160,640]{2,1,0:T(8,128)(2,1)} %pad_maximum_fusion.1), channel_id=1, source_target_pairs={{0,1},{1,0},{2,3},{3,2},{4,5},{5,4},{6,7},{7,6},{8,9},{9,8},{10,11... | collective-permute-start | bytes 1228808 | tf_op jit(solution)/shard_map/ppermute | solution.py:177
  168.4 19.9 %collective-permute-start.18 = (f32[160,640]{1,0:T(8,128)S(1)}, f32[160,640]{1,0:T(8,128)S(1)}, u32[]{:S(2)}, u32[]{:S(2)}) collective-permute-start(f32[160,640]{1,0:T(8,128)S(1)} %slice_bitcast_fusion), channel_id=1, source_target_pairs={{0,2},{1,3},{2,0},{3,1},{4,6},{5,7},{6,4},{7,5},{8,10},{9,11},{10,... | collective-permute-start | bytes 1228808 | tf_op jit(solution)/shard_map/ppermute | solution.py:179
  192.2 13.9 %collective-permute-start.23 = (bf16[160,1,128]{2,0,1:T(8,128)(2,1)S(1)}, bf16[160,1,128]{2,0,1:T(8,128)(2,1)S(1)}, u32[]{:S(2)}, u32[]{:S(2)}) collective-permute-start(bf16[160,1,128]{2,0,1:T(8,128)(2,1)S(1)} %bitcast.141), channel_id=1, source_target_pairs={{0,16},{16,0},{32,48},{48,32},{64,80},{80,64},{96,112},{112,96},{1... | collective-permute-start | bytes 122888 | tf_op jit(solution)/shard_map/ppermute | solution.py:19
  200.7 19.0 %collective-permute-start.20 = (bf16[160,4,128]{2,0,1:T(8,128)(2,1)S(1)}, bf16[160,4,128]{2,0,1:T(8,128)(2,1)S(1)}, u32[]{:S(2)}, u32[]{:S(2)}) collective-permute-start(bf16[160,4,128]{2,0,1:T(8,128)(2,1)S(1)} %pad_maximum_fusion.11), channel_id=1, source_target_pairs={{16,18},{17,19},{18,16},{19,17},{20,22},{21,23},{22,20},{23,21},{2... | collective-permute-start | bytes 491528 | tf_op jit(solution)/shard_map/ppermute | solution.py:202
  205.7 16.8 %collective-permute-start.19 = (bf16[160,4,128]{2,0,1:T(8,128)(2,1)S(1)}, bf16[160,4,128]{2,0,1:T(8,128)(2,1)S(1)}, u32[]{:S(2)}, u32[]{:S(2)}) collective-permute-start(bf16[160,4,128]{2,0,1:T(8,128)(2,1)S(1)} %pad_maximum_fusion.11), channel_id=1, source_target_pairs={{0,18},{1,19},{2,16},{3,17},{4,22},{5,23},{6,20},{7,21},{8,26},{9,... | collective-permute-start | bytes 491528 | tf_op jit(solution)/shard_map/ppermute | solution.py:201
  249.2 18.9 %collective-permute-start.21 = (f32[650,128]{1,0:T(8,128)S(1)}, f32[650,128]{1,0:T(8,128)S(1)}, u32[]{:S(2)}, u32[]{:S(2)}) collective-permute-start(f32[650,128]{1,0:T(8,128)S(1)} %pad_maximum_fusion.8), channel_id=1, source_target_pairs={{16,18},{17,19},{18,16},{19,17},{20,22},{21,23},{22,20},{23,21},{2... | collective-permute-start | bytes 998408 | tf_op jit(solution)/shard_map/ppermute | solution.py:219
  254.3 14.0 %collective-permute-start.22 = (f32[650,128]{1,0:T(8,128)S(1)}, f32[650,128]{1,0:T(8,128)S(1)}, u32[]{:S(2)}, u32[]{:S(2)}) collective-permute-start(f32[650,128]{1,0:T(8,128)S(1)} %pad_maximum_fusion.9), channel_id=1, source_target_pairs={{0,16},{1,17},{2,18},{3,19},{4,20},{5,21},{6,22},{7,23},{8,24},{9,... | collective-permute-start | bytes 998408 | tf_op jit(solution)/shard_map/ppermute | solution.py:218
  (9 other events, 252.5 us)
Sparse Core Ops, SparseCore 0:
  39.0 40.8 all-gather.1

commit v7 on v3

--- a/solution.py
+++ b/solution.py
@@ -164,8 +164,10 @@
         )
         got = lax.ppermute(piece, "col", [(c, c ^ mask) for c in range(n_col)])
         half_sum = half_sum + got.astype(jnp.float32)
-    across = lax.ppermute(half_sum[1], "col", [(c, c ^ half_bit) for c in range(n_col)])
-    projected = half_sum[0] + across
+    kept = jnp.where(is_even, half_sum[0], half_sum[1])
+    sent = jnp.where(is_even, half_sum[1], half_sum[0])
+    across = lax.ppermute(sent, "col", [(c, c ^ half_bit) for c in range(n_col)])
+    projected = kept + across
     positions = PREFIX + jnp.arange(tok_block, dtype=jnp.int32) % SUF
     cosine, sine = rotary_tables(positions)
     query = projected[:, : heads_here * HD].reshape(tok_block, heads_here, HD)
@@ -176,23 +178,40 @@
     keyval = jnp.where(is_key[None, :, None], rotate(keyval, cosine, sine), keyval).astype(
         jnp.bfloat16
     )
-    other_keyval = partner(keyval, "row", 0)
+    axes = ("row", "col")
+    pair = flat_perm(n_row, n_col, lambda r, c: (r ^ 1, c ^ half_bit))
+    back = flat_perm(n_row, n_col, lambda r, c: (r ^ 1, c) if r % 2 == 0 else (r ^ 1, c ^ half_bit))
+    same = flat_perm(n_row, n_col, lambda r, c: (r, c ^ half_bit) if r % 2 == 1 else None)
+    mixed = jnp.concatenate([query, keyval], axis=1)
+    other = lax.ppermute(mixed, axes, pair)
+    other_query = other[:, :heads_here]
+    other_keyval = other[:, heads_here:]
+    q_all = jnp.where(
+        is_even,
+        jnp.concatenate([query, other_query], axis=1),
+        jnp.concatenate([other_query, query], axis=1),
+    )
     suffix_keys = jnp.where(is_even, keyval[:, 0], other_keyval[:, 0])
     suffix_values = jnp.where(is_even, other_keyval[:, 0], keyval[:, 0])
+
     half_keys = half_kv[:, :HD]
     half_values = half_kv[:, HD:]
-
-    axes = ("row", "col")
-    cross = flat_perm(n_row, n_col, lambda r, c: (r ^ 1, c ^ half_bit) if r % 2 == 0 else (r ^ 1, c))
-    back = flat_perm(n_row, n_col, lambda r, c: (r ^ 1, c) if r % 2 == 0 else (r ^ 1, c ^ half_bit))
-    same = flat_perm(n_row, n_col, lambda r, c: (r, c ^ half_bit) if r % 2 == 1 else None)
-    q_cross = lax.ppermute(query, axes, cross)
-    q_same = lax.ppermute(query, axes, same)
-    q_first = jnp.where(is_even, query, q_cross)
-    q_second = jnp.where(is_even, q_cross, q_same)
-    q_all = jnp.concatenate([q_first, q_second], axis=1)
-
     half_state = attend_keys(q_all, half_keys, half_values, scale)
+    places = jnp.arange(SUF, dtype=jnp.int32)
+    handled_length = suffix_lengths[handled]
+    own_mask = (places[None, :] <= places[:, None]) & (places[None, :] < handled_length) & is_even
+    scores = (
+        jnp.einsum("thd,kd->htk", q_all, suffix_keys, preferred_element_type=jnp.float32) * scale
+    )
+    scores = jnp.where(own_mask[None], scores, -1e30)
+    own_top = jnp.maximum(jnp.max(scores, axis=-1), half_state[0])
+    weights = jnp.exp(scores - own_top[..., None])
+    weights = jnp.where(own_mask[None], weights, 0.0)
+    own_total = jnp.sum(weights, axis=-1)
+    own_accum = jnp.einsum(
+        "htk,kd->htd", weights.astype(jnp.bfloat16), suffix_values, preferred_element_type=jnp.float32
+    )
+    half_state = combine_all([half_state, (own_top, own_total, own_accum)])
     mine = jax.tree.map(
         lambda a, b: jnp.where(is_even, a, b),
         jax.tree.map(lambda x: x[:heads_here], half_state),
@@ -208,19 +227,7 @@
     first_state = jax.tree.map(lambda a, b: jnp.where(is_even, a, b), mine, from_same)
 
     length = suffix_lengths[col_id]
-    places = jnp.arange(SUF, dtype=jnp.int32)
-    mask = (places[None, :] <= places[:, None]) & (places[None, :] < length)
-    scores = (
-        jnp.einsum("thd,kd->htk", query, suffix_keys, preferred_element_type=jnp.float32) * scale
-    )
-    scores = jnp.where(mask[None], scores, -1e30)
-    own_top = jnp.max(scores, axis=-1)
-    weights = jnp.exp(scores - own_top[..., None])
-    own_total = jnp.sum(weights, axis=-1)
-    own_accum = jnp.einsum(
-        "htk,kd->htd", weights.astype(jnp.bfloat16), suffix_values, preferred_element_type=jnp.float32
-    )
-    merged = combine_all([first_state, from_cross, (own_top, own_total, own_accum)])
+    merged = combine_all([first_state, from_cross])
     result = merged[2] / merged[1][..., None]
     live = (places < length).astype(jnp.float32)
     result = result * live[None, :, None]

time: 251 us -> 243 us (0.968)
  local copies, waits for them, and re-layouts: 23.1 us -> 19.4 us
  other arithmetic: 23.4 us -> 20 us
    ppermute x2 -> x1, starting transfers between devices: 6.24 us -> 1.9 us  [partner(): return lax.ppermute(value, axis, pairs)]
    all_gather x1, waiting for transfers between devices: 11.1 us -> 14.9 us  [per_device(): gathered = lax.all_gather(hidden, 'row', axis=0, tiled=True)]
    ppermute x3 -> x2, waiting for transfers between devices: 23.4 us -> 21 us  [the longest x1 18.9 us: per_device(): lax.ppermute(sent, 'col', [(c, c ^ half_bit) for c in range(n_col)])]
    ppermute x3 -> x2, starting transfers between devices: 7.94 us -> 8.27 us  [the longest x1 4.32 us: per_device(): other = lax.ppermute(mixed, axes, pair)]
    unnamed x16 -> x10, local copies, waits for them, and re-layouts: 10.7 us -> 10.7 us
  transfers between devices with their start and end apart: 22 -> 20, of which waited for: 15 -> 14; matrix products, arithmetic and copies ran while one was open for 13% -> 10% of each run, Pallas kernels for 0% -> 0%
where the time goes in v7:
time: 243 us; the launch traced here: 241 us
  waiting for transfers between devices  115 us (47%)
  starting transfers between devices  34.8 us (14%)
  between operations  28.2 us (12%)
  matrix products  23.8 us (10%)
  other arithmetic  20 us (8%)
  local copies, waits for them, and re-layouts  19.4 us (8%)
    ppermute x7, waiting for transfers between devices, per_device(): blocks.append(lax.ppermute(piece, 'col', pairs))  36.4 us
    ppermute x7, waiting for transfers between devices, per_device(): got = lax.ppermute(piece, 'col', [(c, c ^ mask) for c in range(n_col)])  30.3 us
    ppermute x1, waiting for transfers between devices, per_device(): lax.ppermute(sent, 'col', [(c, c ^ half_bit) for c in range(n_col)])  18.9 us
    all_gather x1, waiting for transfers between devices, per_device(): gathered = lax.all_gather(hidden, 'row', axis=0, tiled=True)  14.9 us
    ppermute x1, waiting for transfers between devices, per_device(): lax.ppermute(pack_state(mine), axes, same)  11.4 us
    dot_general x4, matrix products, block_stats(): jnp.einsum('thd,kd->htk', req_query, keys, preferred_element_type=jnp.flo...  10.7 us
    unnamed x10, local copies, waits for them, and re-layouts  10.7 us
    ppermute x7, starting transfers between devices, per_device(): blocks.append(lax.ppermute(piece, 'col', pairs))  9.32 us
  transfers between devices with their start and end apart: 20, of which 14 were waited for; matrix products, arithmetic and copies ran while one was open for 10% of the time, Pallas kernels for 0%

profile of v7, /device:TPU:32, one launch (start us, length us, event | category | flops | bytes accessed | tf_op | source)
XLA Modules:
  0.0 241.0 jit_solution(4561192440374373256)
XLA Ops:
  29.5 2.9 %collective-permute-start.4 = (bf16[1024,256]{1,0:T(8,128)(2,1)S(1)}, bf16[1024,256]{1,0:T(8,128)(2,1)S(1)}, u32[]{:S(2)}, u32[]{:S(2)}) collective-permute-start(bf16[1024,256]{1,0:T(8,128)(2,1)S(1)} %get-tuple-element.124), channel_id=1, source_target_pairs={{0,8},{1,9},{2,10},{3,11},{4,12},{5,13},{6,14},{7,15},{8,0},{9,1},... | collective-permute-start | bytes 1572872 | tf_op jit(solution)/shard_map/ppermute | solution.py:142
  33.8 2.7 %collective-permute-start.6 = (bf16[1024,256]{1,0:T(8,128)(2,1)S(1)}, bf16[1024,256]{1,0:T(8,128)(2,1)S(1)}, u32[]{:S(2)}, u32[]{:S(2)}) collective-permute-start(bf16[1024,256]{1,0:T(8,128)(2,1)S(1)} %fusion.55), channel_id=1, source_target_pairs={{0,12},{1,13},{2,14},{3,15},{4,8},{5,9},{6,10},{7,11},{8,4},{9,5},... | collective-permute-start | bytes 1572872 | tf_op jit(solution)/shard_map/ppermute | solution.py:142
  42.5 6.9 %collective-permute-done.3 = bf16[1024,256]{1,0:T(8,128)(2,1)} collective-permute-done((bf16[1024,256]{1,0:T(8,128)(2,1)S(1)}, bf16[1024,256]{1,0:T(8,128)(2,1)}, u32[]{:S(2)}, u32[]{:S(2)}) %collective-permute-start.3) | collective-permute-done | bytes 524320 | tf_op jit(solution)/shard_map/ppermute | solution.py:142
  51.4 12.3 %collective-permute-done.4 = bf16[1024,256]{1,0:T(8,128)(2,1)S(1)} collective-permute-done((bf16[1024,256]{1,0:T(8,128)(2,1)S(1)}, bf16[1024,256]{1,0:T(8,128)(2,1)S(1)}, u32[]{:S(2)}, u32[]{:S(2)}) %collective-permute-start.4) | collective-permute-done | bytes 524320 | tf_op jit(solution)/shard_map/ppermute | solution.py:142
  64.6 9.5 %collective-permute-done.5 = bf16[1024,256]{1,0:T(8,128)(2,1)S(1)} collective-permute-done((bf16[1024,256]{1,0:T(8,128)(2,1)S(1)}, bf16[1024,256]{1,0:T(8,128)(2,1)S(1)}, u32[]{:S(2)}, u32[]{:S(2)}) %collective-permute-start.5) | collective-permute-done | bytes 524320 | tf_op jit(solution)/shard_map/ppermute | solution.py:142
  75.7 6.8 %collective-permute-done.7 = bf16[1024,256]{1,0:T(8,128)(2,1)S(1)} collective-permute-done((bf16[1024,256]{1,0:T(8,128)(2,1)S(1)}, bf16[1024,256]{1,0:T(8,128)(2,1)S(1)}, u32[]{:S(2)}, u32[]{:S(2)}) %collective-permute-start.7) | collective-permute-done | bytes 524320 | tf_op jit(solution)/shard_map/ppermute | solution.py:142
  83.4 14.9 %all-gather.2.cloned.1.call-done = bf16[2560,512]{1,0:T(8,128)(2,1)} async-done(((bf16[160,512]{1,0:T(8,128)(2,1)}), bf16[2560,512]{1,0:T(8,128)(2,1)}) %all-gather.2.cloned.1.call-update) | async-done | bytes 2621456 | tf_op jit(solution)/shard_map/all_gather | solution.py:127
  98.3 4.0 %fusion.32 = f32[2560,640]{1,0:T(8,128)S(1)} fusion(bf16[2560,512]{1,0:T(8,128)(2,1)} %all-gather.2.cloned.1.call-done, bf16[512,128]{1,0:T(8,128)(2,1)S(1)} %copy-done.1, bf16[512,512]{1,0:T(8,128)(2,1)} %param.9), kind=kOutput, calls=%fused_computation.53 | convolution fusion | flops 1679032320 | bytes 9830400 | tf_op jit(solution)/shard_map/dot_general | solution.py:147
  107.7 2.9 %collective-permute-start.11 = (bf16[2,160,640]{2,1,0:T(8,128)(2,1)}, bf16[2,160,640]{2,1,0:T(8,128)(2,1)S(1)}, u32[]{:S(2)}, u32[]{:S(2)}) collective-permute-start(bf16[2,160,640]{2,1,0:T(8,128)(2,1)} %pad_maximum_fusion.3), channel_id=1, source_target_pairs={{0,8},{1,9},{2,10},{3,11},{4,12},{5,13},{6,14},{7,15},{8,0},{9,1},... | collective-permute-start | bytes 1228808 | tf_op jit(solution)/shard_map/ppermute | solution.py:165
  117.3 7.5 %collective-permute-done.10 = bf16[2,160,640]{2,1,0:T(8,128)(2,1)S(1)} collective-permute-done((bf16[2,160,640]{2,1,0:T(8,128)(2,1)S(1)}, bf16[2,160,640]{2,1,0:T(8,128)(2,1)S(1)}, u32[]{:S(2)}, u32[]{:S(2)}) %collective-permute-start.10) | collective-permute-done | bytes 409632 | tf_op jit(solution)/shard_map/ppermute | solution.py:165
  128.0 9.3 %collective-permute-done.11 = bf16[2,160,640]{2,1,0:T(8,128)(2,1)S(1)} collective-permute-done((bf16[2,160,640]{2,1,0:T(8,128)(2,1)}, bf16[2,160,640]{2,1,0:T(8,128)(2,1)S(1)}, u32[]{:S(2)}, u32[]{:S(2)}) %collective-permute-start.11) | collective-permute-done | bytes 409632 | tf_op jit(solution)/shard_map/ppermute | solution.py:165
  138.6 5.8 %collective-permute-done.13 = bf16[2,160,640]{2,1,0:T(8,128)(2,1)S(1)} collective-permute-done((bf16[2,160,640]{2,1,0:T(8,128)(2,1)}, bf16[2,160,640]{2,1,0:T(8,128)(2,1)S(1)}, u32[]{:S(2)}, u32[]{:S(2)}) %collective-permute-start.13) | collective-permute-done | bytes 409632 | tf_op jit(solution)/shard_map/ppermute | solution.py:165
  144.5 6.3 %collective-permute-done.14 = bf16[2,160,640]{2,1,0:T(8,128)(2,1)S(1)} collective-permute-done((bf16[2,160,640]{2,1,0:T(8,128)(2,1)}, bf16[2,160,640]{2,1,0:T(8,128)(2,1)S(1)}, u32[]{:S(2)}, u32[]{:S(2)}) %collective-permute-start.14) | collective-permute-done | bytes 409632 | tf_op jit(solution)/shard_map/ppermute | solution.py:165
  151.3 3.9 %collective-permute-start.15 = (f32[160,640]{1,0:T(8,128)S(1)}, f32[160,640]{1,0:T(8,128)S(1)}, u32[]{:S(2)}, u32[]{:S(2)}) collective-permute-start(f32[160,640]{1,0:T(8,128)S(1)} %select_bitcast_fusion), channel_id=1, source_target_pairs={{0,2},{1,3},{2,0},{3,1},{4,6},{5,7},{6,4},{7,5},{8,10},{9,11},{10,... | collective-permute-start | bytes 1228808 | tf_op jit(solution)/shard_map/ppermute | solution.py:169
  155.7 18.9 %collective-permute-done.15 = f32[160,640]{1,0:T(8,128)S(1)} collective-permute-done((f32[160,640]{1,0:T(8,128)S(1)}, f32[160,640]{1,0:T(8,128)S(1)}, u32[]{:S(2)}, u32[]{:S(2)}) %collective-permute-start.15) | collective-permute-done | bytes 409632 | tf_op jit(solution)/shard_map/ppermute | solution.py:169
  175.8 4.3 %collective-permute-start.16 = (bf16[160,5,128]{2,0,1:T(8,128)(2,1)S(1)}, bf16[160,5,128]{2,0,1:T(8,128)(2,1)S(1)}, u32[]{:S(2)}, u32[]{:S(2)}) collective-permute-start(bf16[160,5,128]{2,0,1:T(8,128)(2,1)S(1)} %pad_maximum_fusion.9), channel_id=1, source_target_pairs={{0,18},{1,19},{2,16},{3,17},{4,22},{5,23},{6,20},{7,21},{8,26},{9,... | collective-permute-start | bytes 614408 | tf_op jit(solution)/shard_map/ppermute | solution.py:186
  180.1 3.8 %fusion.82 = (bf16[8192,128]{1,0:T(8,128)(2,1)S(1)}, bf16[8192,128]{1,0:T(8,128)(2,1)}) fusion(bf16[8192,256]{1,0:T(8,128)(2,1)} %constant_dynamic-update-slice_fusion), kind=kLoop, calls=%fused_computation.170 | loop fusion | bytes 8388608 | tf_op jit(solution)/shard_map/slice | solution.py:198
  186.2 26.4 %while.15 = (s32[]{:T(128)}, f32[8,160]{1,0:T(8,128)S(1)}, f32[8,160]{1,0:T(8,128)S(1)}, f32[8,160,128]{2,1,0:T(8,128)S(1)}, bf16[4,2048,128]{2,1,0:T(8,128)(2,1...) while((s32[]{:T(128)}, f32[8,160]{1,0:T(8,128)S(1)}, ...), condition=%wide.region_3.4_spmd.clone, body=%wide.region_0.3_spmd.clone.sunk | while | flops 1363811840 | bytes 34225268 | solution.py:78
  186.2 2.7 %bitcast_reduce_fusion.2 = (f32[8,160]{1,0:T(8,128)S(1)}, f32[2048,160,8]{0,1,2:T(8,128)S(1)}) fusion(bf16[160,8,128]{2,0,1:T(8,128)(2,1)S(1)} %get-tuple-element.244, bf16[4,2048,128]{2,1,0:T(8,128)(2,1)} %get-tuple-element.243, s32[]{:T(128)S(6)} %copy.34), kind=kOutput, calls=%fused_computation.1.clone.1 | convolution fusion | flops 676330240 | bytes 11342852 | tf_op jit(solution)/shard_map/while/body/eval_jaxpr/thd,kd->htk/dot_general | solution.py:42
  192.8 2.7 %bitcast_reduce_fusion.2 = (f32[8,160]{1,0:T(8,128)S(1)}, f32[2048,160,8]{0,1,2:T(8,128)S(1)}) fusion(bf16[160,8,128]{2,0,1:T(8,128)(2,1)S(1)} %get-tuple-element.244, bf16[4,2048,128]{2,1,0:T(8,128)(2,1)} %get-tuple-element.243, s32[]{:T(128)S(6)} %copy.34), kind=kOutput, calls=%fused_computation.1.clone.1 | convolution fusion | flops 676330240 | bytes 11342852 | tf_op jit(solution)/shard_map/while/body/eval_jaxpr/thd,kd->htk/dot_general | solution.py:42
  199.5 2.7 %bitcast_reduce_fusion.2 = (f32[8,160]{1,0:T(8,128)S(1)}, f32[2048,160,8]{0,1,2:T(8,128)S(1)}) fusion(bf16[160,8,128]{2,0,1:T(8,128)(2,1)S(1)} %get-tuple-element.244, bf16[4,2048,128]{2,1,0:T(8,128)(2,1)} %get-tuple-element.243, s32[]{:T(128)S(6)} %copy.34), kind=kOutput, calls=%fused_computation.1.clone.1 | convolution fusion | flops 676330240 | bytes 11342852 | tf_op jit(solution)/shard_map/while/body/eval_jaxpr/thd,kd->htk/dot_general | solution.py:42
  206.1 2.7 %bitcast_reduce_fusion.2 = (f32[8,160]{1,0:T(8,128)S(1)}, f32[2048,160,8]{0,1,2:T(8,128)S(1)}) fusion(bf16[160,8,128]{2,0,1:T(8,128)(2,1)S(1)} %get-tuple-element.244, bf16[4,2048,128]{2,1,0:T(8,128)(2,1)} %get-tuple-element.243, s32[]{:T(128)S(6)} %copy.34), kind=kOutput, calls=%fused_computation.1.clone.1 | convolution fusion | flops 676330240 | bytes 11342852 | tf_op jit(solution)/shard_map/while/body/eval_jaxpr/thd,kd->htk/dot_general | solution.py:42
  214.2 5.9 %collective-permute-start.17 = (f32[650,128]{1,0:T(8,128)S(1)}, f32[650,128]{1,0:T(8,128)S(1)}, u32[]{:S(2)}, u32[]{:S(2)}) collective-permute-start(f32[650,128]{1,0:T(8,128)S(1)} %pad_maximum_fusion.7), channel_id=1, source_target_pairs={{16,18},{17,19},{18,16},{19,17},{20,22},{21,23},{22,20},{23,21},{2... | collective-permute-start | bytes 998408 | tf_op jit(solution)/shard_map/ppermute | solution.py:226
  221.3 11.4 %collective-permute-done.17 = f32[650,128]{1,0:T(8,128)S(1)} collective-permute-done((f32[650,128]{1,0:T(8,128)S(1)}, f32[650,128]{1,0:T(8,128)S(1)}, u32[]{:S(2)}, u32[]{:S(2)}) %collective-permute-start.17) | collective-permute-done | bytes 332832 | tf_op jit(solution)/shard_map/ppermute | solution.py:226
  (108 shorter events, 61.7 us)
Async XLA Ops:
  6.5 91.8 %all-gather.2.cloned.1.call-start = ((), (), s32[]{:S(2)}) async-start(), calls=%async_computation | async-start | bytes 2785280 | tf_op jit(solution)/shard_map/all_gather | solution.py:127
  7.3 14.3 %collective-permute-start = (bf16[2,1024,128]{2,1,0:T(8,128)(2,1)}, bf16[2,1024,128]{2,1,0:T(8,128)(2,1)S(1)}, u32[]{:S(2)}, u32[]{:S(2)}) collective-permute-start(bf16[2,1024,128]{2,1,0:T(8,128)(2,1)} %param.11), channel_id=1, source_target_pairs={{0,16},{16,0},{32,48},{48,32},{64,80},{80,64},{96,112},{112,96},{1... | collective-permute-start | bytes 1572872 | tf_op jit(solution)/shard_map/ppermute | solution.py:14
  24.0 9.8 %collective-permute-start.1 = (bf16[1024,256]{1,0:T(8,128)(2,1)}, bf16[1024,256]{1,0:T(8,128)(2,1)}, u32[]{:S(2)}, u32[]{:S(2)}) collective-permute-start(bf16[1024,256]{1,0:T(8,128)(2,1)} %get-tuple-element.121), channel_id=1, source_target_pairs={{0,1},{1,0},{2,3},{3,2},{4,5},{5,4},{6,7},{7,6},{8,9},{9,8},{10,11... | collective-permute-start | bytes 1572872 | tf_op jit(solution)/shard_map/ppermute | solution.py:142
  24.0 15.1 %collective-permute-start.2 = (bf16[1024,256]{1,0:T(8,128)(2,1)}, bf16[1024,256]{1,0:T(8,128)(2,1)}, u32[]{:S(2)}, u32[]{:S(2)}) collective-permute-start(bf16[1024,256]{1,0:T(8,128)(2,1)} %get-tuple-element.122), channel_id=1, source_target_pairs={{0,4},{1,5},{2,6},{3,7},{4,0},{5,1},{6,2},{7,3},{8,12},{9,13},{10,... | collective-permute-start | bytes 1572872 | tf_op jit(solution)/shard_map/ppermute | solution.py:142
  25.3 24.2 %collective-permute-start.3 = (bf16[1024,256]{1,0:T(8,128)(2,1)S(1)}, bf16[1024,256]{1,0:T(8,128)(2,1)}, u32[]{:S(2)}, u32[]{:S(2)}) collective-permute-start(bf16[1024,256]{1,0:T(8,128)(2,1)S(1)} %get-tuple-element.123), channel_id=1, source_target_pairs={{0,5},{1,4},{2,7},{3,6},{4,1},{5,0},{6,3},{7,2},{8,13},{9,12},{10,... | collective-permute-start | bytes 1572872 | tf_op jit(solution)/shard_map/ppermute | solution.py:142
  29.5 34.2 %collective-permute-start.4 = (bf16[1024,256]{1,0:T(8,128)(2,1)S(1)}, bf16[1024,256]{1,0:T(8,128)(2,1)S(1)}, u32[]{:S(2)}, u32[]{:S(2)}) collective-permute-start(bf16[1024,256]{1,0:T(8,128)(2,1)S(1)} %get-tuple-element.124), channel_id=1, source_target_pairs={{0,8},{1,9},{2,10},{3,11},{4,12},{5,13},{6,14},{7,15},{8,0},{9,1},... | collective-permute-start | bytes 1572872 | tf_op jit(solution)/shard_map/ppermute | solution.py:142
  32.5 65.8 %copy-start.1 = (bf16[512,128]{1,0:T(8,128)(2,1)S(1)}, bf16[512,128]{1,0:T(8,128)(2,1)}, u32[]{:S(2)}) copy-start(bf16[512,128]{1,0:T(8,128)(2,1)} %param.10) | copy-start | bytes 393220
  32.5 41.5 %collective-permute-start.5 = (bf16[1024,256]{1,0:T(8,128)(2,1)S(1)}, bf16[1024,256]{1,0:T(8,128)(2,1)S(1)}, u32[]{:S(2)}, u32[]{:S(2)}) collective-permute-start(bf16[1024,256]{1,0:T(8,128)(2,1)S(1)} %get-tuple-element.125), channel_id=1, source_target_pairs={{0,9},{1,8},{2,11},{3,10},{4,13},{5,12},{6,15},{7,14},{8,1},{9,0},... | collective-permute-start | bytes 1572872 | tf_op jit(solution)/shard_map/ppermute | solution.py:142
  33.8 41.1 %collective-permute-start.6 = (bf16[1024,256]{1,0:T(8,128)(2,1)S(1)}, bf16[1024,256]{1,0:T(8,128)(2,1)S(1)}, u32[]{:S(2)}, u32[]{:S(2)}) collective-permute-start(bf16[1024,256]{1,0:T(8,128)(2,1)S(1)} %fusion.55), channel_id=1, source_target_pairs={{0,12},{1,13},{2,14},{3,15},{4,8},{5,9},{6,10},{7,11},{8,4},{9,5},... | collective-permute-start | bytes 1572872 | tf_op jit(solution)/shard_map/ppermute | solution.py:142
  39.1 43.4 %collective-permute-start.7 = (bf16[1024,256]{1,0:T(8,128)(2,1)S(1)}, bf16[1024,256]{1,0:T(8,128)(2,1)S(1)}, u32[]{:S(2)}, u32[]{:S(2)}) collective-permute-start(bf16[1024,256]{1,0:T(8,128)(2,1)S(1)} %get-tuple-element.120), channel_id=1, source_target_pairs={{0,13},{1,12},{2,15},{3,14},{4,9},{5,8},{6,11},{7,10},{8,5},{9,4},... | collective-permute-start | bytes 1572872 | tf_op jit(solution)/shard_map/ppermute | solution.py:142
  102.4 2.8 %copy-start = (f32[2560,640]{1,0:T(8,128)}, f32[2560,640]{1,0:T(8,128)S(1)}, u32[]{:S(2)}) copy-start(f32[2560,640]{1,0:T(8,128)S(1)} %fusion.32) | copy-start | bytes 19660804
  105.5 11.8 %collective-permute-start.9 = (bf16[2,160,640]{2,1,0:T(8,128)(2,1)S(1)}, bf16[2,160,640]{2,1,0:T(8,128)(2,1)S(1)}, u32[]{:S(2)}, u32[]{:S(2)}) collective-permute-start(bf16[2,160,640]{2,1,0:T(8,128)(2,1)S(1)} %pad_maximum_fusion.1), channel_id=1, source_target_pairs={{0,4},{1,5},{2,6},{3,7},{4,0},{5,1},{6,2},{7,3},{8,12},{9,13},{10,... | collective-permute-start | bytes 1228808 | tf_op jit(solution)/shard_map/ppermute | solution.py:165
  106.7 18.1 %collective-permute-start.10 = (bf16[2,160,640]{2,1,0:T(8,128)(2,1)S(1)}, bf16[2,160,640]{2,1,0:T(8,128)(2,1)S(1)}, u32[]{:S(2)}, u32[]{:S(2)}) collective-permute-start(bf16[2,160,640]{2,1,0:T(8,128)(2,1)S(1)} %pad_maximum_fusion.2), channel_id=1, source_target_pairs={{0,5},{1,4},{2,7},{3,6},{4,1},{5,0},{6,3},{7,2},{8,13},{9,12},{10,... | collective-permute-start | bytes 1228808 | tf_op jit(solution)/shard_map/ppermute | solution.py:165
  107.7 29.6 %collective-permute-start.11 = (bf16[2,160,640]{2,1,0:T(8,128)(2,1)}, bf16[2,160,640]{2,1,0:T(8,128)(2,1)S(1)}, u32[]{:S(2)}, u32[]{:S(2)}) collective-permute-start(bf16[2,160,640]{2,1,0:T(8,128)(2,1)} %pad_maximum_fusion.3), channel_id=1, source_target_pairs={{0,8},{1,9},{2,10},{3,11},{4,12},{5,13},{6,14},{7,15},{8,0},{9,1},... | collective-permute-start | bytes 1228808 | tf_op jit(solution)/shard_map/ppermute | solution.py:165
  111.4 27.3 %collective-permute-start.12 = (bf16[2,160,640]{2,1,0:T(8,128)(2,1)}, bf16[2,160,640]{2,1,0:T(8,128)(2,1)S(1)}, u32[]{:S(2)}, u32[]{:S(2)}) collective-permute-start(bf16[2,160,640]{2,1,0:T(8,128)(2,1)} %pad_maximum_fusion.4), channel_id=1, source_target_pairs={{0,9},{1,8},{2,11},{3,10},{4,13},{5,12},{6,15},{7,14},{8,1},{9,0},... | collective-permute-start | bytes 1228808 | tf_op jit(solution)/shard_map/ppermute | solution.py:165
  113.2 31.3 %collective-permute-start.13 = (bf16[2,160,640]{2,1,0:T(8,128)(2,1)}, bf16[2,160,640]{2,1,0:T(8,128)(2,1)S(1)}, u32[]{:S(2)}, u32[]{:S(2)}) collective-permute-start(bf16[2,160,640]{2,1,0:T(8,128)(2,1)} %pad_maximum_fusion.5), channel_id=1, source_target_pairs={{0,12},{1,13},{2,14},{3,15},{4,8},{5,9},{6,10},{7,11},{8,4},{9,5},... | collective-permute-start | bytes 1228808 | tf_op jit(solution)/shard_map/ppermute | solution.py:165
  117.3 33.5 %collective-permute-start.14 = (bf16[2,160,640]{2,1,0:T(8,128)(2,1)}, bf16[2,160,640]{2,1,0:T(8,128)(2,1)S(1)}, u32[]{:S(2)}, u32[]{:S(2)}) collective-permute-start(bf16[2,160,640]{2,1,0:T(8,128)(2,1)} %pad_maximum_fusion.6), channel_id=1, source_target_pairs={{0,13},{1,12},{2,15},{3,14},{4,9},{5,8},{6,11},{7,10},{8,5},{9,4},... | collective-permute-start | bytes 1228808 | tf_op jit(solution)/shard_map/ppermute | solution.py:165
  124.8 26.0 %collective-permute-start.8 = (bf16[2,160,640]{2,1,0:T(8,128)(2,1)}, bf16[2,160,640]{2,1,0:T(8,128)(2,1)S(1)}, u32[]{:S(2)}, u32[]{:S(2)}) collective-permute-start(bf16[2,160,640]{2,1,0:T(8,128)(2,1)} %pad_maximum_fusion), channel_id=1, source_target_pairs={{0,1},{1,0},{2,3},{3,2},{4,5},{5,4},{6,7},{7,6},{8,9},{9,8},{10,11... | collective-permute-start | bytes 1228808 | tf_op jit(solution)/shard_map/ppermute | solution.py:165
  151.3 23.3 %collective-permute-start.15 = (f32[160,640]{1,0:T(8,128)S(1)}, f32[160,640]{1,0:T(8,128)S(1)}, u32[]{:S(2)}, u32[]{:S(2)}) collective-permute-start(f32[160,640]{1,0:T(8,128)S(1)} %select_bitcast_fusion), channel_id=1, source_target_pairs={{0,2},{1,3},{2,0},{3,1},{4,6},{5,7},{6,4},{7,5},{8,10},{9,11},{10,... | collective-permute-start | bytes 1228808 | tf_op jit(solution)/shard_map/ppermute | solution.py:169
  175.8 10.2 %collective-permute-start.16 = (bf16[160,5,128]{2,0,1:T(8,128)(2,1)S(1)}, bf16[160,5,128]{2,0,1:T(8,128)(2,1)S(1)}, u32[]{:S(2)}, u32[]{:S(2)}) collective-permute-start(bf16[160,5,128]{2,0,1:T(8,128)(2,1)S(1)} %pad_maximum_fusion.9), channel_id=1, source_target_pairs={{0,18},{1,19},{2,16},{3,17},{4,22},{5,23},{6,20},{7,21},{8,26},{9,... | collective-permute-start | bytes 614408 | tf_op jit(solution)/shard_map/ppermute | solution.py:186
  214.2 18.4 %collective-permute-start.17 = (f32[650,128]{1,0:T(8,128)S(1)}, f32[650,128]{1,0:T(8,128)S(1)}, u32[]{:S(2)}, u32[]{:S(2)}) collective-permute-start(f32[650,128]{1,0:T(8,128)S(1)} %pad_maximum_fusion.7), channel_id=1, source_target_pairs={{16,18},{17,19},{18,16},{19,17},{20,22},{21,23},{22,20},{23,21},{2... | collective-permute-start | bytes 998408 | tf_op jit(solution)/shard_map/ppermute | solution.py:226
  220.3 12.6 %collective-permute-start.18 = (f32[650,128]{1,0:T(8,128)S(1)}, f32[650,128]{1,0:T(8,128)S(1)}, u32[]{:S(2)}, u32[]{:S(2)}) collective-permute-start(f32[650,128]{1,0:T(8,128)S(1)} %pad_maximum_fusion.8), channel_id=1, source_target_pairs={{0,16},{1,17},{2,18},{3,19},{4,20},{5,21},{6,22},{7,23},{8,24},{9,... | collective-permute-start | bytes 998408 | tf_op jit(solution)/shard_map/ppermute | solution.py:225
Sparse Core Ops, SparseCore 0:
  9.1 89.1 all-gather.1
